TPU v7x, 32 devices: a whole 2x2x4 slice. The times are simulated.
32 devices in a mesh: groups: 2 (over x), wide: 8 (over z, y), narrow: 2 (over core).
Axes of the slice: x: 2, y: 2, z: 4, core: 2. Of those that a mesh axis runs over, the one named last changes fastest.
Arguments:
- queries: bfloat16 [8192, 1024], P(('groups', 'narrow', 'wide')), parts along dimension 0, may hold values from -8 to 8
- keys: bfloat16 [8192, 1024], P(('groups', 'narrow', 'wide')), parts along dimension 0, may hold values from -8 to 8
- values: bfloat16 [8192, 1024], P(('groups', 'narrow', 'wide')), parts along dimension 0, may hold values from -6 to 6
- block_lists: int32 [16, 32, 16], P(('groups', 'wide'), 'narrow'), parts along dimension 0, may hold values from 0 to 31, as said below
- block_counts: int32 [16, 32], P(('groups', 'wide'), 'narrow'), parts along dimension 0, may hold values from 1 to 16
Outputs:
- attention: bfloat16 [8192, 1024], P(('groups', 'narrow', 'wide')), parts along dimension 0
There are 2 independent parts, one for each index of `groups`. A program takes and returns all parts, laid end to end along the dimension named above; each array names one. Nothing has to cross between parts.
Inputs may be any that keep to these rules, and one draw needn't show every extreme that they name: `block_lists`: entries are block indices; the first entry of each list is the query block's own index and the first block_counts entries of a list are distinct; later entries are ignored.
All inputs are finite; a program needn't handle non-finite values.
Results may differ from a plain program's by a relative error of at most 0.0044.
Values may be sent and summed in bfloat16 or wider, within the bound.
No kernel may reach another device: no remote copies, remote signals or barrier semaphores. Data moves between devices by JAX's collectives and lax.ppermute only.
A program may use at most 128 MiB of HBM per device.

v0:
```python
import math

import jax
import jax.numpy as jnp
from jax import lax
from jax.sharding import PartitionSpec as P

BLOCK = 128


def attend_batch(query_groups_tiled, key_table, value_table, lists, counts):
    blocks, block_rows, head_size = query_groups_tiled.shape
    inverse_root = 1.0 / math.sqrt(head_size)
    rounds = jnp.max(counts)

    def one_round(position, carry):
        running_max, row_total, accum = carry
        column = lax.dynamic_index_in_dim(lists, position, 1, keepdims=False)
        key_blocks = jnp.take(key_table, column, axis=0)
        value_blocks = jnp.take(value_table, column, axis=0)
        logit_scores = (
            jnp.einsum(
                "nqd,nkd->nqk", query_groups_tiled, key_blocks, preferred_element_type=jnp.float32
            )
            * inverse_root
        )
        valid = (position < counts)[:, None, None]
        new_max = jnp.where(
            valid,
            jnp.maximum(running_max, jnp.max(logit_scores, axis=-1, keepdims=True)),
            running_max,
        )
        weights = jnp.where(valid, jnp.exp(logit_scores - new_max), 0.0)
        factor = jnp.exp(running_max - new_max)
        row_total = row_total * factor + jnp.sum(weights, axis=-1, keepdims=True)
        accum = accum * factor + jnp.einsum(
            "nqk,nkd->nqd",
            weights.astype(jnp.bfloat16),
            value_blocks,
            preferred_element_type=jnp.float32,
        )
        return (new_max, row_total, accum)

    start = (
        jnp.full((blocks, block_rows, 1), -1e30, jnp.float32),
        jnp.zeros((blocks, block_rows, 1), jnp.float32),
        jnp.zeros((blocks, block_rows, head_size), jnp.float32),
    )
    running_max, row_total, accum = lax.fori_loop(0, rounds, one_round, start)
    return (accum / jnp.where(row_total > 0.0, row_total, 1.0)).astype(jnp.bfloat16)


def per_device(queries, keys, values, block_lists, block_counts):
    head_queries, head_keys, head_values = (
        lax.all_to_all(queries, "wide", split_axis=1, concat_axis=0, tiled=True),
        lax.all_to_all(keys, "wide", split_axis=1, concat_axis=0, tiled=True),
        lax.all_to_all(values, "wide", split_axis=1, concat_axis=0, tiled=True),
    )
    key_rows, value_rows = (
        lax.all_gather(head_keys, "narrow", axis=0, tiled=True),
        lax.all_gather(head_values, "narrow", axis=0, tiled=True),
    )
    head_size = head_queries.shape[1]
    query_groups_tiled = head_queries.reshape(-1, BLOCK, head_size)
    key_table = key_rows.reshape(-1, BLOCK, head_size)
    value_table = value_rows.reshape(-1, BLOCK, head_size)
    attended = attend_batch(
        query_groups_tiled, key_table, value_table, block_lists[0], block_counts[0]
    )
    return lax.all_to_all(
        attended.reshape(-1, head_size), "wide", split_axis=0, concat_axis=1, tiled=True
    )


def solution(mesh):
    in_specs = (
        P(("groups", "narrow", "wide"), None),
        P(("groups", "narrow", "wide"), None),
        P(("groups", "narrow", "wide"), None),
        P(("groups", "wide"), "narrow", None),
        P(("groups", "wide"), "narrow"),
    )
    out_specs = P(("groups", "narrow", "wide"), None)
    return jax.shard_map(
        per_device, mesh=mesh, in_specs=in_specs, out_specs=out_specs, check_vma=False
    )
```

profile of v0, /device:TPU:0, one launch (start us, length us, event | category | flops | bytes accessed | tf_op | source)
XLA Modules:
  0.0 209.1 jit_solution(16607844047298249746)
XLA Ops:
  6.5 1.3 copy.17
  7.8 0.3 copy.18
  8.1 21.7 %all_to_all.73 = bf16[256,8,128]{2,0,1:T(8,128)(2,1)} all-to-all(bf16[256,8,128]{2,0,1:T(8,128)(2,1)S(1)} %copy.18), channel_id=1, replica_groups=mesh['groups'=2,'wide'=8,'narrow'=2] {'wide'}, dimensions={1} | all-to-all | bytes 1048576 | tf_op jit(solution)/shard_map/all_to_all | solution.py:56
  29.9 1.0 copy-done.1
  31.1 0.3 copy.21
  31.4 17.7 %all_to_all.74 = bf16[256,8,128]{2,0,1:T(8,128)(2,1)} all-to-all(bf16[256,8,128]{2,0,1:T(8,128)(2,1)S(1)} %copy.21), channel_id=1, replica_groups=mesh['groups'=2,'wide'=8,'narrow'=2] {'wide'}, dimensions={1} | all-to-all | bytes 1048576 | tf_op jit(solution)/shard_map/all_to_all | solution.py:57
  49.1 0.9 copy_bitcast_fusion
  50.0 4.3 %all-to-all-start.1 = ((bf16[256,8,128]{2,0,1:T(8,128)(2,1)}), bf16[256,8,128]{2,0,1:T(8,128)(2,1)}, u32[]{:S(2)}, u32[]{:S(2)}) async-start(bf16[256,8,128]{2,0,1:T(8,128)(2,1)} %copy_bitcast_fusion), calls=%async_computation.1 | async-start | bytes 1048576 | tf_op jit(solution)/shard_map/all_to_all | solution.py:55
  54.3 0.7 copy-done.2
  55.0 0.7 reduce_max.18
  55.7 12.2 %all-to-all-done.1 = bf16[256,8,128]{2,0,1:T(8,128)(2,1)} async-done(((bf16[256,8,128]{2,0,1:T(8,128)(2,1)}), bf16[256,8,128]{2,0,1:T(8,128)(2,1)}, u32[]{:S(2)}, u32[]{:S(2)}) %all-to-all-start.1) | async-done | bytes 524320 | tf_op jit(solution)/shard_map/all_to_all | solution.py:55
  68.0 29.7 %while.14 = (s32[]{:T(128)}, f32[16,128,1]{1,0,2:T(8,128)S(1)}, f32[16,128,1]{1,0,2:T(8,128)S(1)}, f32[16,128,128]{2,1,0:T(8,128)S(1)}, s32[]{:T(128)}, /*index=...) while((s32[]{:T(128)}, f32[16,128,1]{1,0,2:T(8,128)S(1)}, ...), condition=%wide.region_4.6_spmd, body=%wide.region_1.5_spmd.sunk | while | flops 137372784 | bytes 9048727 | solution.py:49
  68.7 1.9 gather_fusion
  70.6 1.6 fusion.30
  72.2 1.9 gather_fusion.1
  74.1 0.9 convolution_add_fusion.2
  75.9 1.9 gather_fusion
  77.8 1.6 fusion.30
  79.5 1.9 gather_fusion.1
  81.4 0.9 convolution_add_fusion.2
  83.2 1.9 gather_fusion
  85.1 1.6 fusion.30
  86.7 1.9 gather_fusion.1
  88.6 0.9 convolution_add_fusion.2
  90.5 1.9 gather_fusion
  92.3 1.6 fusion.30
  94.0 1.9 gather_fusion.1
  95.9 0.9 convolution_add_fusion.2
  97.7 0.3 divide_convert_fusion
  98.0 102.9 %all_to_all.75 = bf16[8,256,128]{2,1,0:T(8,128)(2,1)S(1)} all-to-all(bf16[8,256,128]{2,1,0:T(8,128)(2,1)S(1)} %bitcast.51), channel_id=1, replica_groups=mesh['groups'=2,'wide'=8,'narrow'=2] {'wide'}, dimensions={0} | all-to-all | bytes 1048576 | tf_op jit(solution)/shard_map/all_to_all | solution.py:70
  201.0 0.2 copy.22
  201.2 1.0 copy.23
  (42 shorter events, 1.8 us)
Async XLA Ops:
  6.5 42.5 %copy-start = (bf16[256,1024]{1,0:T(8,128)(2,1)S(1)}, bf16[256,1024]{1,0:T(8,128)(2,1)}, u32[]{:S(2)}) copy-start(bf16[256,1024]{1,0:T(8,128)(2,1)} %param.9) | copy-start | bytes 1572868
  6.5 61.3 %all-gather.3.cloned.1.call-start = ((), (), s32[]{:S(2)}) async-start(), calls=%async_computation.4 | async-start | bytes 1572864 | tf_op jit(solution)/shard_map/all_gather | solution.py:60
  29.8 1.0 copy-start.1
  29.9 38.0 %all-gather.5.cloned.1.call-start = ((), (), s32[]{:S(2)}) async-start(), calls=%async_computation.5 | async-start | bytes 1572864 | tf_op jit(solution)/shard_map/all_gather | solution.py:61
  50.0 4.3 %copy-start.3 = (s32[1,16,16]{2,1,0:T(8,128)S(1)}, s32[1,16,16]{2,1,0:T(8,128)}, u32[]{:S(2)}) copy-start(s32[1,16,16]{2,1,0:T(8,128)} %param.12) | copy-start | bytes 3076
  50.0 17.9 %all-to-all-start.1 = ((bf16[256,8,128]{2,0,1:T(8,128)(2,1)}), bf16[256,8,128]{2,0,1:T(8,128)(2,1)}, u32[]{:S(2)}, u32[]{:S(2)}) async-start(bf16[256,8,128]{2,0,1:T(8,128)(2,1)} %copy_bitcast_fusion), calls=%async_computation.1 | async-start | bytes 1048576 | tf_op jit(solution)/shard_map/all_to_all | solution.py:55
  54.3 0.7 copy-start.2
Sparse Core Ops, SparseCore 0:
  30.0 8.0 all-gather.2
  49.2 8.0 all-gather.4
where the time goes:
time: 212 us; the launch traced here: 209 us
  blocking collectives  142 us (67%)
  local copies, waits for them, and re-layouts  21 us (10%)
  between operations  13.5 us (6%)
  waiting for transfers between devices  12.2 us (6%)
  matrix products  9.98 us (5%)
  starting transfers between devices  4.32 us (2%)
  loops' own time  3.39 us (2%)
  other arithmetic  2.32 us (1%)
    all_to_all x1, blocking collectives, per_device(): lax.all_to_all(attended.reshape(-1, head_size), 'wide', split_axis=0, con...  103 us
    all_to_all x1, blocking collectives, per_device(): lax.all_to_all(keys, 'wide', split_axis=1, concat_axis=0, tiled=True)  21.7 us
    all_to_all x1, blocking collectives, per_device(): lax.all_to_all(values, 'wide', split_axis=1, concat_axis=0, tiled=True)  17.7 us
    all_to_all x1, waiting for transfers between devices, per_device(): lax.all_to_all(queries, 'wide', split_axis=1, concat_axis=0, tiled=True)  12.2 us
    gather x4, local copies, waits for them, and re-layouts, one_round(): value_blocks = jnp.take(value_table, column, axis=0)  7.52 us
    gather x4, local copies, waits for them, and re-layouts, one_round(): key_blocks = jnp.take(key_table, column, axis=0)  7.49 us
    dot_general x4, matrix products, one_round(): jnp.einsum('nqd,nkd->nqk', query_groups_tiled, key_blocks, preferred_elem...  6.31 us
    all_to_all x1, starting transfers between devices, per_device(): lax.all_to_all(queries, 'wide', split_axis=1, concat_axis=0, tiled=True)  4.27 us
  transfers between devices with their start and end apart: 3, of which 1 were waited for; matrix products, arithmetic and copies ran while one was open for 1% of the time, Pallas kernels for 0%

commit v1 on v0

v1 whole, which is shorter than its diff:
```python
import functools
import math

import jax
import jax.numpy as jnp
from jax import lax
from jax.experimental import pallas as pl
from jax.experimental.pallas import tpu as pltpu
from jax.sharding import PartitionSpec as P

BLOCK = 128


def attend_kernel(lists_ref, counts_ref, q_ref, k_ref, v_ref, o_ref, kbuf, vbuf, *, inverse_root):
    b = pl.program_id(0)
    count = counts_ref[b]
    slots = lists_ref.shape[1]
    key_blocks = k_ref.shape[0] // BLOCK
    first = lists_ref[b, 0]
    for j in range(slots):
        index = jnp.where(j < count, lists_ref[b, j], first)
        index = jnp.minimum(jnp.maximum(index, 0), key_blocks - 1)
        start = pl.multiple_of(index * BLOCK, BLOCK)
        kbuf[pl.ds(j * BLOCK, BLOCK), :] = k_ref[pl.ds(start, BLOCK), :]
        vbuf[pl.ds(j * BLOCK, BLOCK), :] = v_ref[pl.ds(start, BLOCK), :]
    logit_scores = (
        lax.dot_general(
            q_ref[...],
            kbuf[...],
            (((1,), (1,)), ((), ())),
            preferred_element_type=jnp.float32,
        )
        * inverse_root
    )
    slot_of = lax.broadcasted_iota(jnp.int32, logit_scores.shape, 1) // BLOCK
    logit_scores = jnp.where(slot_of < count, logit_scores, -jnp.inf)
    row_max = jnp.max(logit_scores, axis=1, keepdims=True)
    weights = jnp.exp(logit_scores - row_max)
    row_total = jnp.sum(weights, axis=1, keepdims=True)
    weighted_sum = jnp.dot(
        weights.astype(jnp.bfloat16), vbuf[...], preferred_element_type=jnp.float32
    )
    o_ref[...] = (weighted_sum / row_total).astype(o_ref.dtype)


def attend(head_queries, key_rows, value_rows, lists, counts):
    rows, head_size = head_queries.shape
    query_blocks = rows // BLOCK
    slots = lists.shape[1]
    key_rows_total = key_rows.shape[0]
    kernel = functools.partial(attend_kernel, inverse_root=1.0 / math.sqrt(head_size))
    grid_spec = pltpu.PrefetchScalarGridSpec(
        num_scalar_prefetch=2,
        grid=(query_blocks,),
        in_specs=[
            pl.BlockSpec((BLOCK, head_size), lambda b, lists, counts: (b, 0)),
            pl.BlockSpec((key_rows_total, head_size), lambda b, lists, counts: (0, 0)),
            pl.BlockSpec((key_rows_total, head_size), lambda b, lists, counts: (0, 0)),
        ],
        out_specs=pl.BlockSpec((BLOCK, head_size), lambda b, lists, counts: (b, 0)),
        scratch_shapes=[
            pltpu.VMEM((slots * BLOCK, head_size), head_queries.dtype),
            pltpu.VMEM((slots * BLOCK, head_size), head_queries.dtype),
        ],
    )
    return pl.pallas_call(
        kernel,
        grid_spec=grid_spec,
        out_shape=jax.ShapeDtypeStruct((rows, head_size), jnp.bfloat16),
        compiler_params=pltpu.CompilerParams(dimension_semantics=("arbitrary",)),
    )(lists, counts, head_queries, key_rows, value_rows)


def per_device(queries, keys, values, block_lists, block_counts):
    head_queries, head_keys, head_values = (
        lax.all_to_all(queries, "wide", split_axis=1, concat_axis=0, tiled=True),
        lax.all_to_all(keys, "wide", split_axis=1, concat_axis=0, tiled=True),
        lax.all_to_all(values, "wide", split_axis=1, concat_axis=0, tiled=True),
    )
    key_rows, value_rows = (
        lax.all_gather(head_keys, "narrow", axis=0, tiled=True),
        lax.all_gather(head_values, "narrow", axis=0, tiled=True),
    )
    attended = attend(head_queries, key_rows, value_rows, block_lists[0], block_counts[0])
    return lax.all_to_all(attended, "wide", split_axis=0, concat_axis=1, tiled=True)


def solution(mesh):
    in_specs = (
        P(("groups", "narrow", "wide"), None),
        P(("groups", "narrow", "wide"), None),
        P(("groups", "narrow", "wide"), None),
        P(("groups", "wide"), "narrow", None),
        P(("groups", "wide"), "narrow"),
    )
    out_specs = P(("groups", "narrow", "wide"), None)
    return jax.shard_map(
        per_device, mesh=mesh, in_specs=in_specs, out_specs=out_specs, check_vma=False
    )
```

time: 212 us -> 109 us (0.51); the launches traced: 209 us -> 108 us
  blocking collectives: 142 us -> 74.5 us
  local copies, waits for them, and re-layouts: 21 us -> 4.17 us
  Pallas kernels: 0 us -> 16.1 us
  waiting for transfers between devices: 12.2 us -> 0.04 us
  matrix products: 9.98 us -> 0 us
  starting transfers between devices: 4.32 us -> 0.04 us
  loops' own time: 3.39 us -> 0 us
  other arithmetic: 2.32 us -> 0 us
    all_to_all x1 -> x2, blocking collectives: 103 us -> 35.2 us  [the longest x1 17.6 us: per_device(): lax.all_to_all(attended, 'wide', split_axis=0, concat_axis=1, tiled=True)]
    pallas_call x0 -> x1, Pallas kernels: none -> 16.1 us  [attend(): pl.pallas_call(kernel, grid_spec=grid_spec, out_shape=jax.ShapeDtypeStruc...]
    gather x8 -> x0, local copies, waits for them, and re-layouts: 15 us -> none  [the longest x4 7.52 us: one_round(): value_blocks = jnp.take(value_table, column, axis=0)]
    all_to_all x1 -> x0, waiting for transfers between devices: 12.2 us -> none  [per_device(): lax.all_to_all(queries, 'wide', split_axis=1, concat_axis=0, tiled=True)]
    dot_general x8 -> x0, matrix products: 9.98 us -> none  [the longest x4 6.31 us: one_round(): jnp.einsum('nqd,nkd->nqk', query_groups_tiled, key_blocks, preferred_elem...]
    all_to_all x1 -> x0, starting transfers between devices: 4.27 us -> none  [per_device(): lax.all_to_all(queries, 'wide', split_axis=1, concat_axis=0, tiled=True)]
    another operation x1 -> x0, loops' own time: 3.39 us -> none  [attend_batch(): running_max, row_total, accum = lax.fori_loop(0, rounds, one_round, start)]
  transfers between devices with their start and end apart: 3 -> 2, of which waited for: 1 -> 0; matrix products, arithmetic and copies ran while one was open for 1% -> 0% of each run, Pallas kernels for 0% -> 0%
where the time goes in v1:
time: 109 us; the launch traced here: 108 us
  blocking collectives  74.5 us (68%)
  Pallas kernels  16.1 us (15%)
  between operations  13.4 us (12%)
  local copies, waits for them, and re-layouts  4.17 us (4%)
    all_to_all x1, blocking collectives, per_device(): lax.all_to_all(keys, 'wide', split_axis=1, concat_axis=0, tiled=True)  21.7 us
    all_to_all x1, blocking collectives, per_device(): lax.all_to_all(attended, 'wide', split_axis=0, concat_axis=1, tiled=True)  17.6 us
    all_to_all x1, blocking collectives, per_device(): lax.all_to_all(values, 'wide', split_axis=1, concat_axis=0, tiled=True)  17.6 us
    all_to_all x1, blocking collectives, per_device(): lax.all_to_all(queries, 'wide', split_axis=1, concat_axis=0, tiled=True)  17.5 us
    pallas_call x1, Pallas kernels, attend(): pl.pallas_call(kernel, grid_spec=grid_spec, out_shape=jax.ShapeDtypeStruc...  16.1 us
    unnamed x6, local copies, waits for them, and re-layouts  3.02 us
  transfers between devices with their start and end apart: 2, of which 0 were waited for; matrix products, arithmetic and copies ran while one was open for 0% of the time, Pallas kernels for 0%

profile of v1, /device:TPU:0, one launch (start us, length us, event | category | flops | bytes accessed | tf_op | source)
XLA Modules:
  0.0 108.3 jit_solution(15008278100029893649)
XLA Ops:
  6.5 0.0 copy-start
  6.5 0.0 all-gather.3.cloned.1.call-start
  6.5 1.0 copy-done
  7.6 0.1 copy_bitcast_fusion.2
  7.7 21.7 %all_to_all.76 = bf16[256,8,128]{2,0,1:T(8,128)(2,1)} all-to-all(bf16[256,8,128]{2,0,1:T(8,128)(2,1)S(1)} %copy_bitcast_fusion.2), channel_id=1, replica_groups=mesh['groups'=2,'wide'=8,'narrow'=2] {'wide'}, dimensions={1} | all-to-all | bytes 1048576 | tf_op jit(solution)/shard_map/all_to_all | solution.py:77
  29.4 0.0 copy-start.1
  29.4 0.0 all-gather.3.cloned.1.call-update
  29.4 0.0 all-gather.5.cloned.1.call-start
  29.5 1.0 copy-done.1
  30.4 0.1 copy_bitcast_fusion.1
  30.5 17.6 %all_to_all.77 = bf16[256,8,128]{2,0,1:T(8,128)(2,1)} all-to-all(bf16[256,8,128]{2,0,1:T(8,128)(2,1)S(1)} %copy_bitcast_fusion.1), channel_id=1, replica_groups=mesh['groups'=2,'wide'=8,'narrow'=2] {'wide'}, dimensions={1} | all-to-all | bytes 1048576 | tf_op jit(solution)/shard_map/all_to_all | solution.py:78
  48.2 0.0 copy-start.2
  48.2 0.0 all-gather.5.cloned.1.call-update
  48.2 1.0 copy-done.2
  49.2 0.1 copy_bitcast_fusion.3
  49.3 17.5 %all_to_all.78 = bf16[256,8,128]{2,0,1:T(8,128)(2,1)} all-to-all(bf16[256,8,128]{2,0,1:T(8,128)(2,1)S(1)} %copy_bitcast_fusion.3), channel_id=1, replica_groups=mesh['groups'=2,'wide'=8,'narrow'=2] {'wide'}, dimensions={1} | all-to-all | bytes 1048576 | tf_op jit(solution)/shard_map/all_to_all | solution.py:76
  66.8 0.0 all-gather.3.cloned.1.call-done.k_ref
  66.8 0.0 all-gather.5.cloned.1.call-done.v_ref
  66.8 16.1 %shard_map.55 = bf16[2048,128]{1,0:T(8,128)(2,1)} custom-call(s32[16,16]{1,0:T(8,128)} %bitcast.37, s32[16]{0:T(128)} %bitcast.38, bf16[2048,128]{1,0:T(8,128)(2,1)} %bitcast.35, bf16[4096,128]{1,0:T(8,128)(2,1)} %all-gather.3.cloned.1.call-done.k_ref, bf16[4096,128]{1,0:T(8,128)(2,1)} %all-gather.5.cloned.1.call-done.v_ref), custom_call_target="tpu_custom_call" | custom-call | tf_op jit(solution)/shard_map/pallas_call | solution.py:66
  82.9 17.6 %all_to_all.79 = bf16[8,256,128]{2,1,0:T(8,128)(2,1)S(1)} all-to-all(bf16[8,256,128]{2,1,0:T(8,128)(2,1)} %bitcast.36), channel_id=1, replica_groups=mesh['groups'=2,'wide'=8,'narrow'=2] {'wide'}, dimensions={0} | all-to-all | bytes 1048576 | tf_op jit(solution)/shard_map/all_to_all | solution.py:85
  100.6 0.9 copy_bitcast_fusion
Async XLA Ops:
  6.5 1.0 copy-start
  6.5 60.3 %all-gather.3.cloned.1.call-start = ((), (), s32[]{:S(2)}) async-start(), calls=%async_computation.4 | async-start | bytes 1572864 | tf_op jit(solution)/shard_map/all_gather | solution.py:81
  29.4 1.0 copy-start.1
  29.4 37.4 %all-gather.5.cloned.1.call-start = ((), (), s32[]{:S(2)}) async-start(), calls=%async_computation.5 | async-start | bytes 1572864 | tf_op jit(solution)/shard_map/all_gather | solution.py:82
  48.2 1.0 copy-start.2
Sparse Core Ops, SparseCore 0:
  29.5 8.0 all-gather.2
  48.3 8.0 all-gather.4

commit v2 on v1

v2 whole, which is shorter than its diff:
```python
import functools
import math

import jax
import jax.numpy as jnp
from jax import lax
from jax.experimental import pallas as pl
from jax.experimental.pallas import tpu as pltpu
from jax.sharding import PartitionSpec as P

BLOCK = 128


def attend_kernel(
    lists_ref, counts_ref, q_ref, own_ref, other_ref, o_ref, kbuf, vbuf, *, inverse_root, head_size
):
    b = pl.program_id(0)
    count = counts_ref[b]
    slots = lists_ref.shape[1]
    half_blocks = other_ref.shape[0] // BLOCK
    first = lists_ref[b, 0]
    own_k = own_ref.shape[1] - 2 * head_size
    for j in range(slots):
        index = jnp.where(j < count, lists_ref[b, j], first)
        index = jnp.minimum(jnp.maximum(index, 0), 2 * half_blocks - 1)
        rows = pl.ds(j * BLOCK, BLOCK)

        @pl.when(index < half_blocks)
        def _():
            start = pl.multiple_of(index * BLOCK, BLOCK)
            kbuf[rows, :] = own_ref[pl.ds(start, BLOCK), pl.ds(own_k, head_size)]
            vbuf[rows, :] = own_ref[pl.ds(start, BLOCK), pl.ds(own_k + head_size, head_size)]

        @pl.when(index >= half_blocks)
        def _():
            start = pl.multiple_of((index - half_blocks) * BLOCK, BLOCK)
            kbuf[rows, :] = other_ref[pl.ds(start, BLOCK), pl.ds(0, head_size)]
            vbuf[rows, :] = other_ref[pl.ds(start, BLOCK), pl.ds(head_size, head_size)]

    logit_scores = (
        lax.dot_general(
            q_ref[...],
            kbuf[...],
            (((1,), (1,)), ((), ())),
            preferred_element_type=jnp.float32,
        )
        * inverse_root
    )
    slot_of = lax.broadcasted_iota(jnp.int32, logit_scores.shape, 1) // BLOCK
    logit_scores = jnp.where(slot_of < count, logit_scores, -jnp.inf)
    row_max = jnp.max(logit_scores, axis=1, keepdims=True)
    weights = jnp.exp(logit_scores - row_max)
    row_total = jnp.sum(weights, axis=1, keepdims=True)
    weighted_sum = jnp.dot(
        weights.astype(jnp.bfloat16), vbuf[...], preferred_element_type=jnp.float32
    )
    o_ref[...] = (weighted_sum / row_total).astype(o_ref.dtype)


def attend(own, other, lists, counts, head_size):
    rows = own.shape[0]
    query_blocks = rows // BLOCK
    slots = lists.shape[1]
    kernel = functools.partial(
        attend_kernel, inverse_root=1.0 / math.sqrt(head_size), head_size=head_size
    )
    grid_spec = pltpu.PrefetchScalarGridSpec(
        num_scalar_prefetch=2,
        grid=(query_blocks,),
        in_specs=[
            pl.BlockSpec((BLOCK, head_size), lambda b, lists, counts: (b, 0)),
            pl.BlockSpec(own.shape, lambda b, lists, counts: (0, 0)),
            pl.BlockSpec(other.shape, lambda b, lists, counts: (0, 0)),
        ],
        out_specs=pl.BlockSpec((BLOCK, head_size), lambda b, lists, counts: (b, 0)),
        scratch_shapes=[
            pltpu.VMEM((slots * BLOCK, head_size), own.dtype),
            pltpu.VMEM((slots * BLOCK, head_size), own.dtype),
        ],
    )
    return pl.pallas_call(
        kernel,
        grid_spec=grid_spec,
        out_shape=jax.ShapeDtypeStruct((rows, head_size), jnp.bfloat16),
        compiler_params=pltpu.CompilerParams(dimension_semantics=("arbitrary",)),
    )(lists, counts, own, own, other)


def per_device(queries, keys, values, block_lists, block_counts):
    rows = queries.shape[0]
    width = lax.axis_size("wide")
    head_size = queries.shape[1] // width
    stacked = jnp.concatenate(
        [a.reshape(rows, width, head_size) for a in (queries, keys, values)], axis=2
    )
    own = lax.all_to_all(stacked, "wide", split_axis=1, concat_axis=0, tiled=True)
    own = own.reshape(rows * width, 3 * head_size)
    other = lax.ppermute(own[:, head_size:], "narrow", [(0, 1), (1, 0)])
    half_blocks = own.shape[0] // BLOCK
    n = lax.axis_index("narrow")
    lists = (block_lists[0] + (2 * half_blocks - n * half_blocks)) % (2 * half_blocks)
    attended = attend(own, other, lists, block_counts[0], head_size)
    return lax.all_to_all(attended, "wide", split_axis=0, concat_axis=1, tiled=True)


def solution(mesh):
    in_specs = (
        P(("groups", "narrow", "wide"), None),
        P(("groups", "narrow", "wide"), None),
        P(("groups", "narrow", "wide"), None),
        P(("groups", "wide"), "narrow", None),
        P(("groups", "wide"), "narrow"),
    )
    out_specs = P(("groups", "narrow", "wide"), None)
    return jax.shard_map(
        per_device, mesh=mesh, in_specs=in_specs, out_specs=out_specs, check_vma=False
    )
```

time: 109 us -> 93.4 us (0.86)
  between operations: 13.4 us -> 0.04 us
  blocking collectives: 74.5 us -> 62.6 us
  Pallas kernels: 16.1 us -> 21.9 us
  waiting for transfers between devices: 0.04 us -> 2.25 us
  local copies, waits for them, and re-layouts: 4.17 us -> 5.44 us
    all_to_all x3 -> x1, blocking collectives: 56.9 us -> 44.1 us  [per_device(): lax.all_to_all(stacked, 'wide', split_axis=1, concat_axis=0, tiled=True)]
    pallas_call x1, Pallas kernels: 16.1 us -> 21.9 us  [attend(): pl.pallas_call(kernel, grid_spec=grid_spec, out_shape=jax.ShapeDtypeStruc...]
    reshape x0 -> x2, local copies, waits for them, and re-layouts: none -> 2.48 us  [per_device(): a.reshape(rows, width, head_size)]
    ppermute x0 -> x1, waiting for transfers between devices: none -> 2.25 us  [per_device(): other = lax.ppermute(own[:, head_size:], 'narrow', [(0, 1), (1, 0)])]
    unnamed x6 -> x8, local copies, waits for them, and re-layouts: 3.02 us -> 0.98 us
    slice x0 -> x1, local copies, waits for them, and re-layouts: none -> 1.1 us  [per_device(): other = lax.ppermute(own[:, head_size:], 'narrow', [(0, 1), (1, 0)])]
  transfers between devices with their start and end apart: 2 -> 1, of which waited for: 0 -> 1; matrix products, arithmetic and copies ran while one was open for 0% -> 1% of each run, Pallas kernels for 0% -> 0%
where the time goes in v2:
time: 93.4 us; the launch traced here: 93 us
  blocking collectives  62.6 us (67%)
  Pallas kernels  21.9 us (23%)
  local copies, waits for them, and re-layouts  5.44 us (6%)
  waiting for transfers between devices  2.25 us (2%)
    all_to_all x1, blocking collectives, per_device(): lax.all_to_all(stacked, 'wide', split_axis=1, concat_axis=0, tiled=True)  44.1 us
    pallas_call x1, Pallas kernels, attend(): pl.pallas_call(kernel, grid_spec=grid_spec, out_shape=jax.ShapeDtypeStruc...  21.9 us
    all_to_all x1, blocking collectives, per_device(): lax.all_to_all(attended, 'wide', split_axis=0, concat_axis=1, tiled=True)  18.5 us
    reshape x2, local copies, waits for them, and re-layouts, per_device(): a.reshape(rows, width, head_size)  2.48 us
    ppermute x1, waiting for transfers between devices, per_device(): other = lax.ppermute(own[:, head_size:], 'narrow', [(0, 1), (1, 0)])  2.25 us
  transfers between devices with their start and end apart: 1, of which 1 were waited for; matrix products, arithmetic and copies ran while one was open for 1% of the time, Pallas kernels for 0%

profile of v2, /device:TPU:0, one launch (start us, length us, event | category | flops | bytes accessed | tf_op | source)
XLA Modules:
  0.0 93.0 jit_solution(12560124186792518781)
XLA Ops:
  0.0 0.0 copy-start
  0.0 1.2 %copy_bitcast_fusion.3 = bf16[256,8,128]{2,0,1:T(8,128)(2,1)S(1)} fusion(bf16[256,1024]{1,0:T(8,128)(2,1)} %param.5), kind=kLoop, calls=%fused_computation.4 | loop fusion | bytes 1048576 | tf_op jit(solution)/shard_map/reshape | solution.py:94
  1.2 0.0 copy-done
  1.2 1.3 %copy_bitcast_fusion.1 = (bf16[256,8,128]{2,0,1:T(8,128)(2,1)S(1)}, bf16[256,8,128]{2,0,1:T(8,128)(2,1)S(1)}) fusion(bf16[256,1024]{1,0:T(8,128)(2,1)S(1)} %copy-done, bf16[256,1024]{1,0:T(8,128)(2,1)} %param.7), kind=kLoop, calls=%fused_computation.2 | loop fusion | bytes 2097152 | tf_op jit(solution)/shard_map/reshape | solution.py:94
  2.5 0.2 pad_maximum_fusion
  2.7 44.1 %all_to_all.34 = bf16[256,8,384]{2,0,1:T(8,128)(2,1)S(1)} all-to-all(bf16[256,8,384]{2,0,1:T(8,128)(2,1)S(1)} %pad_maximum_fusion), channel_id=1, replica_groups=mesh['groups'=2,'wide'=8,'narrow'=2] {'wide'}, dimensions={1} | all-to-all | bytes 3145728 | tf_op jit(solution)/shard_map/all_to_all | solution.py:96
  46.8 0.0 copy-start.1
  46.8 0.0 copy-start.3
  46.8 1.1 %slice.4 = bf16[2048,256]{1,0:T(8,128)(2,1)} slice(bf16[2048,384]{1,0:T(8,128)(2,1)S(1)} %bitcast.32), slice={[0:2048], [128:384]} | slice | bytes 2097152 | tf_op jit(solution)/shard_map/slice | solution.py:98
  47.9 0.0 collective-permute-start
  47.9 0.0 copy-done.3
  47.9 0.6 add_select_fusion.lists_ref
  48.5 2.3 %collective-permute-done.other_ref = bf16[2048,256]{1,0:T(8,128)(2,1)S(1)} collective-permute-done((bf16[2048,256]{1,0:T(8,128)(2,1)}, bf16[2048,256]{1,0:T(8,128)(2,1)S(1)}, u32[]{:S(2)}, u32[]{:S(2)}) %collective-permute-start) | collective-permute-done | bytes 1048608 | tf_op jit(solution)/shard_map/ppermute | solution.py:98
  50.8 0.0 copy-start.2
  50.8 0.0 copy-done.1
  50.8 1.0 %copy-done.2 = bf16[2048,256]{1,0:T(8,128)(2,1)} copy-done((bf16[2048,256]{1,0:T(8,128)(2,1)}, bf16[2048,256]{1,0:T(8,128)(2,1)S(1)}, u32[]{:S(2)}) %copy-start.2) | copy-done | bytes 1048600
  51.8 21.9 %shard_map.55 = bf16[2048,128]{1,0:T(8,128)(2,1)} custom-call(s32[16,16]{1,0:T(8,128)} %add_select_fusion.lists_ref, s32[16]{0:T(128)} %bitcast.36, bf16[2048,384]{1,0:T(8,128)(2,1)} %bitcast.33, bf16[2048,384]{1,0:T(8,128)(2,1)} %bitcast.34, bf16[2048,256]{1,0:T(8,128)(2,1)} %copy-done.2), custom_call_target="tpu_custom_call" | custom-call | tf_op jit(solution)/shard_map/pallas_call | solution.py:81
  73.6 18.5 %all_to_all.35 = bf16[8,256,128]{2,1,0:T(8,128)(2,1)S(1)} all-to-all(bf16[8,256,128]{2,1,0:T(8,128)(2,1)} %bitcast.35), channel_id=1, replica_groups=mesh['groups'=2,'wide'=8,'narrow'=2] {'wide'}, dimensions={0} | all-to-all | bytes 1048576 | tf_op jit(solution)/shard_map/all_to_all | solution.py:103
  92.1 0.9 copy_bitcast_fusion
Async XLA Ops:
  0.0 1.2 %copy-start = (bf16[256,1024]{1,0:T(8,128)(2,1)S(1)}, bf16[256,1024]{1,0:T(8,128)(2,1)}, u32[]{:S(2)}) copy-start(bf16[256,1024]{1,0:T(8,128)(2,1)} %param.6) | copy-start | bytes 1572868
  46.8 4.0 %copy-start.1 = (bf16[256,8,384]{2,0,1:T(8,128)(2,1)}, bf16[256,8,384]{2,0,1:T(8,128)(2,1)S(1)}, u32[]{:S(2)}) copy-start(bf16[256,8,384]{2,0,1:T(8,128)(2,1)S(1)} %all_to_all.34) | copy-start | bytes 4718596
  46.8 1.1 %copy-start.3 = (s32[1,16,16]{2,1,0:T(8,128)S(1)}, s32[1,16,16]{2,1,0:T(8,128)}, u32[]{:S(2)}) copy-start(s32[1,16,16]{2,1,0:T(8,128)} %param.8) | copy-start | bytes 3076
  47.9 2.9 %collective-permute-start = (bf16[2048,256]{1,0:T(8,128)(2,1)}, bf16[2048,256]{1,0:T(8,128)(2,1)S(1)}, u32[]{:S(2)}, u32[]{:S(2)}) collective-permute-start(bf16[2048,256]{1,0:T(8,128)(2,1)} %slice.4), channel_id=1, source_target_pairs={{0,1},{1,0},{2,3},{3,2},{4,5},{5,4},{6,7},{7,6},{8,9},{9,8},{10,11... | collective-permute-start | bytes 3145736 | tf_op jit(solution)/shard_map/ppermute | solution.py:98
  50.8 1.0 %copy-start.2 = (bf16[2048,256]{1,0:T(8,128)(2,1)}, bf16[2048,256]{1,0:T(8,128)(2,1)S(1)}, u32[]{:S(2)}) copy-start(bf16[2048,256]{1,0:T(8,128)(2,1)S(1)} %collective-permute-done.other_ref) | copy-start | bytes 3145732

commit v3 on v2

v3 whole, which is shorter than its diff:
```python
import functools
import math

import jax
import jax.numpy as jnp
from jax import lax
from jax.experimental import pallas as pl
from jax.experimental.pallas import tpu as pltpu
from jax.sharding import PartitionSpec as P

BLOCK = 128
CHUNK = 4


def attend_kernel(
    lists_ref, counts_ref, own_ref, other_ref, o_ref, kbuf, vbuf, sbuf, *, inverse_root, head_size
):
    query_blocks = own_ref.shape[0] // BLOCK
    slots = lists_ref.shape[1]
    half_blocks = other_ref.shape[0] // BLOCK
    own_k = own_ref.shape[1] - 2 * head_size
    chunk_keys = CHUNK * BLOCK

    def one_block(b, carry):
        count = counts_ref[b]
        chunks = (count + (CHUNK - 1)) // CHUNK
        first = lists_ref[b, 0]
        for j in range(slots):
            index = jnp.where(j < count, lists_ref[b, j], first)
            index = jnp.minimum(jnp.maximum(index, 0), 2 * half_blocks - 1)
            rows = pl.ds((j % CHUNK) * BLOCK, BLOCK)
            live = j < chunks * CHUNK

            @pl.when(live & (index < half_blocks))
            def _():
                start = pl.multiple_of(index * BLOCK, BLOCK)
                kbuf[j // CHUNK, rows, :] = own_ref[pl.ds(start, BLOCK), pl.ds(own_k, head_size)]
                vbuf[j // CHUNK, rows, :] = own_ref[
                    pl.ds(start, BLOCK), pl.ds(own_k + head_size, head_size)
                ]

            @pl.when(live & (index >= half_blocks))
            def _():
                start = pl.multiple_of((index - half_blocks) * BLOCK, BLOCK)
                kbuf[j // CHUNK, rows, :] = other_ref[pl.ds(start, BLOCK), pl.ds(0, head_size)]
                vbuf[j // CHUNK, rows, :] = other_ref[
                    pl.ds(start, BLOCK), pl.ds(head_size, head_size)
                ]

        q_rows = pl.ds(pl.multiple_of(b * BLOCK, BLOCK), BLOCK)
        queries = own_ref[q_rows, pl.ds(0, head_size)]

        def scores_pass(c, row_max):
            logit_scores = (
                lax.dot_general(
                    queries,
                    kbuf[c],
                    (((1,), (1,)), ((), ())),
                    preferred_element_type=jnp.float32,
                )
                * inverse_root
            )
            sbuf[c] = logit_scores
            return jnp.maximum(row_max, jnp.max(logit_scores, axis=1, keepdims=True))

        row_max = lax.fori_loop(
            0, chunks, scores_pass, jnp.full((BLOCK, 1), -jnp.inf, jnp.float32)
        )

        def weights_pass(c, carry):
            row_total, weighted_sum = carry
            weights = jnp.exp(sbuf[c] - row_max)
            slot_of = c * CHUNK + lax.broadcasted_iota(jnp.int32, weights.shape, 1) // BLOCK
            weights = jnp.where(slot_of < count, weights, 0.0)
            row_total = row_total + jnp.sum(weights, axis=1, keepdims=True)
            weighted_sum = weighted_sum + jnp.dot(
                weights.astype(jnp.bfloat16), vbuf[c], preferred_element_type=jnp.float32
            )
            return row_total, weighted_sum

        row_total, weighted_sum = lax.fori_loop(
            0,
            chunks,
            weights_pass,
            (
                jnp.zeros((BLOCK, 1), jnp.float32),
                jnp.zeros((BLOCK, head_size), jnp.float32),
            ),
        )
        o_ref[q_rows, :] = (weighted_sum / row_total).astype(o_ref.dtype)
        return carry

    lax.fori_loop(0, query_blocks, one_block, 0)


def attend(own, other, lists, counts, head_size):
    rows = own.shape[0]
    slots = lists.shape[1]
    chunks = -(-slots // CHUNK)
    kernel = functools.partial(
        attend_kernel, inverse_root=1.0 / math.sqrt(head_size), head_size=head_size
    )
    grid_spec = pltpu.PrefetchScalarGridSpec(
        num_scalar_prefetch=2,
        grid=(1,),
        in_specs=[
            pl.BlockSpec(own.shape, lambda i, lists, counts: (0, 0)),
            pl.BlockSpec(other.shape, lambda i, lists, counts: (0, 0)),
        ],
        out_specs=pl.BlockSpec((rows, head_size), lambda i, lists, counts: (0, 0)),
        scratch_shapes=[
            pltpu.VMEM((chunks, CHUNK * BLOCK, head_size), own.dtype),
            pltpu.VMEM((chunks, CHUNK * BLOCK, head_size), own.dtype),
            pltpu.VMEM((chunks, BLOCK, CHUNK * BLOCK), jnp.float32),
        ],
    )
    return pl.pallas_call(
        kernel,
        grid_spec=grid_spec,
        out_shape=jax.ShapeDtypeStruct((rows, head_size), jnp.bfloat16),
        compiler_params=pltpu.CompilerParams(dimension_semantics=("arbitrary",)),
    )(lists, counts, own, other)


def per_device(queries, keys, values, block_lists, block_counts):
    rows = queries.shape[0]
    width = lax.axis_size("wide")
    head_size = queries.shape[1] // width
    stacked = jnp.concatenate(
        [a.reshape(rows, width, head_size) for a in (queries, keys, values)], axis=2
    )
    own = lax.all_to_all(stacked, "wide", split_axis=1, concat_axis=0, tiled=True)
    own = own.reshape(rows * width, 3 * head_size)
    other = lax.ppermute(own[:, head_size:], "narrow", [(0, 1), (1, 0)])
    half_blocks = own.shape[0] // BLOCK
    n = lax.axis_index("narrow")
    lists = (block_lists[0] + (2 * half_blocks - n * half_blocks)) % (2 * half_blocks)
    attended = attend(own, other, lists, block_counts[0], head_size)
    return lax.all_to_all(attended, "wide", split_axis=0, concat_axis=1, tiled=True)


def solution(mesh):
    in_specs = (
        P(("groups", "narrow", "wide"), None),
        P(("groups", "narrow", "wide"), None),
        P(("groups", "narrow", "wide"), None),
        P(("groups", "wide"), "narrow", None),
        P(("groups", "wide"), "narrow"),
    )
    out_specs = P(("groups", "narrow", "wide"), None)
    return jax.shard_map(
        per_device, mesh=mesh, in_specs=in_specs, out_specs=out_specs, check_vma=False
    )
```

time: 93.4 us -> 107 us (1.15)
  blocking collectives: 62.6 us -> 82 us
  Pallas kernels: 21.9 us -> 16.3 us
    all_to_all x1, blocking collectives: 18.5 us -> 37.9 us  [per_device(): lax.all_to_all(attended, 'wide', split_axis=0, concat_axis=1, tiled=True)]
    pallas_call x1, Pallas kernels: 21.9 us -> 16.3 us  [attend(): pl.pallas_call(kernel, grid_spec=grid_spec, out_shape=jax.ShapeDtypeStruc...]
where the time goes in v3:
time: 107 us
  blocking collectives  82 us (77%)
  Pallas kernels  16.3 us (15%)
  local copies, waits for them, and re-layouts  5.44 us (5%)
  waiting for transfers between devices  2.25 us (2%)
    all_to_all x1, blocking collectives, per_device(): lax.all_to_all(stacked, 'wide', split_axis=1, concat_axis=0, tiled=True)  44.1 us
    all_to_all x1, blocking collectives, per_device(): lax.all_to_all(attended, 'wide', split_axis=0, concat_axis=1, tiled=True)  37.9 us
    pallas_call x1, Pallas kernels, attend(): pl.pallas_call(kernel, grid_spec=grid_spec, out_shape=jax.ShapeDtypeStruc...  16.3 us
    reshape x2, local copies, waits for them, and re-layouts, per_device(): a.reshape(rows, width, head_size)  2.48 us
    ppermute x1, waiting for transfers between devices, per_device(): other = lax.ppermute(own[:, head_size:], 'narrow', [(0, 1), (1, 0)])  2.25 us
  transfers between devices with their start and end apart: 1, of which 1 were waited for; matrix products, arithmetic and copies ran while one was open for 1% of the time, Pallas kernels for 0%

profile of v3, /device:TPU:0, one launch (start us, length us, event | category | flops | bytes accessed | tf_op | source)
XLA Modules:
  0.0 106.9 jit_solution(2696149312486559640)
XLA Ops:
  0.0 0.0 copy-start
  0.0 1.2 %copy_bitcast_fusion.3 = bf16[256,8,128]{2,0,1:T(8,128)(2,1)S(1)} fusion(bf16[256,1024]{1,0:T(8,128)(2,1)} %param.5), kind=kLoop, calls=%fused_computation.4 | loop fusion | bytes 1048576 | tf_op jit(solution)/shard_map/reshape | solution.py:130
  1.2 0.0 copy-done
  1.2 1.3 %copy_bitcast_fusion.1 = (bf16[256,8,128]{2,0,1:T(8,128)(2,1)S(1)}, bf16[256,8,128]{2,0,1:T(8,128)(2,1)S(1)}) fusion(bf16[256,1024]{1,0:T(8,128)(2,1)S(1)} %copy-done, bf16[256,1024]{1,0:T(8,128)(2,1)} %param.7), kind=kLoop, calls=%fused_computation.2 | loop fusion | bytes 2097152 | tf_op jit(solution)/shard_map/reshape | solution.py:130
  2.5 0.2 pad_maximum_fusion
  2.7 44.1 %all_to_all.34 = bf16[256,8,384]{2,0,1:T(8,128)(2,1)S(1)} all-to-all(bf16[256,8,384]{2,0,1:T(8,128)(2,1)S(1)} %pad_maximum_fusion), channel_id=1, replica_groups=mesh['groups'=2,'wide'=8,'narrow'=2] {'wide'}, dimensions={1} | all-to-all | bytes 3145728 | tf_op jit(solution)/shard_map/all_to_all | solution.py:132
  46.8 0.0 copy-start.1
  46.8 0.0 copy-start.3
  46.8 1.1 %slice.4 = bf16[2048,256]{1,0:T(8,128)(2,1)} slice(bf16[2048,384]{1,0:T(8,128)(2,1)S(1)} %bitcast.32), slice={[0:2048], [128:384]} | slice | bytes 2097152 | tf_op jit(solution)/shard_map/slice | solution.py:134
  47.9 0.0 collective-permute-start
  47.9 0.0 copy-done.3
  47.9 0.6 add_select_fusion.lists_ref
  48.5 2.3 %collective-permute-done.other_ref = bf16[2048,256]{1,0:T(8,128)(2,1)S(1)} collective-permute-done((bf16[2048,256]{1,0:T(8,128)(2,1)}, bf16[2048,256]{1,0:T(8,128)(2,1)S(1)}, u32[]{:S(2)}, u32[]{:S(2)}) %collective-permute-start) | collective-permute-done | bytes 1048608 | tf_op jit(solution)/shard_map/ppermute | solution.py:134
  50.8 0.0 copy-start.2
  50.8 0.0 copy-done.1
  50.8 1.0 copy-done.2
  51.8 16.3 %shard_map.55 = bf16[2048,128]{1,0:T(8,128)(2,1)} custom-call(s32[16,16]{1,0:T(8,128)} %add_select_fusion.lists_ref, s32[16]{0:T(128)} %bitcast.35, bf16[2048,384]{1,0:T(8,128)(2,1)} %bitcast.33, bf16[2048,256]{1,0:T(8,128)(2,1)} %copy-done.2), custom_call_target="tpu_custom_call" | custom-call | tf_op jit(solution)/shard_map/pallas_call | solution.py:117
  68.1 37.9 %all_to_all.35 = bf16[8,256,128]{2,1,0:T(8,128)(2,1)S(1)} all-to-all(bf16[8,256,128]{2,1,0:T(8,128)(2,1)} %bitcast.34), channel_id=1, replica_groups=mesh['groups'=2,'wide'=8,'narrow'=2] {'wide'}, dimensions={0} | all-to-all | bytes 1048576 | tf_op jit(solution)/shard_map/all_to_all | solution.py:139
  106.1 0.9 copy_bitcast_fusion
Async XLA Ops:
  0.0 1.2 %copy-start = (bf16[256,1024]{1,0:T(8,128)(2,1)S(1)}, bf16[256,1024]{1,0:T(8,128)(2,1)}, u32[]{:S(2)}) copy-start(bf16[256,1024]{1,0:T(8,128)(2,1)} %param.6) | copy-start | bytes 1572868
  46.8 4.0 %copy-start.1 = (bf16[256,8,384]{2,0,1:T(8,128)(2,1)}, bf16[256,8,384]{2,0,1:T(8,128)(2,1)S(1)}, u32[]{:S(2)}) copy-start(bf16[256,8,384]{2,0,1:T(8,128)(2,1)S(1)} %all_to_all.34) | copy-start | bytes 4718596
  46.8 1.1 %copy-start.3 = (s32[1,16,16]{2,1,0:T(8,128)S(1)}, s32[1,16,16]{2,1,0:T(8,128)}, u32[]{:S(2)}) copy-start(s32[1,16,16]{2,1,0:T(8,128)} %param.8) | copy-start | bytes 3076
  47.9 2.9 %collective-permute-start = (bf16[2048,256]{1,0:T(8,128)(2,1)}, bf16[2048,256]{1,0:T(8,128)(2,1)S(1)}, u32[]{:S(2)}, u32[]{:S(2)}) collective-permute-start(bf16[2048,256]{1,0:T(8,128)(2,1)} %slice.4), channel_id=1, source_target_pairs={{0,1},{1,0},{2,3},{3,2},{4,5},{5,4},{6,7},{7,6},{8,9},{9,8},{10,11... | collective-permute-start | bytes 3145736 | tf_op jit(solution)/shard_map/ppermute | solution.py:134
  50.8 1.0 copy-start.2

commit v4 on v2

v4 whole, which is shorter than its diff:
```python
import functools
import math

import jax
import jax.numpy as jnp
from jax import lax
from jax.experimental import pallas as pl
from jax.experimental.pallas import tpu as pltpu
from jax.sharding import PartitionSpec as P

BLOCK = 128
SUBLANES = 8


def attend_kernel(
    lists_ref,
    counts_ref,
    narrow_ref,
    q_ref,
    own_ref,
    other_ref,
    o_ref,
    table,
    kbuf,
    vbuf,
    mask,
    sems,
    *,
    inverse_root,
    head_size,
):
    b = pl.program_id(0)
    half_rows = other_ref.shape[0]
    n = narrow_ref[0]

    @pl.when(b == 0)
    def _():
        own_copy = pltpu.make_async_copy(
            own_ref.at[:, pl.ds(head_size, 2 * head_size)],
            table.at[pl.ds(n * half_rows, half_rows), :],
            sems.at[0],
        )
        other_copy = pltpu.make_async_copy(
            other_ref, table.at[pl.ds((1 - n) * half_rows, half_rows), :], sems.at[1]
        )
        own_copy.start()
        other_copy.start()
        own_copy.wait()
        other_copy.wait()

    count = counts_ref[b]
    slots = lists_ref.shape[1]
    key_blocks = table.shape[0] // BLOCK
    first = lists_ref[b, 0]
    for j in range(slots):
        index = jnp.where(j < count, lists_ref[b, j], first)
        index = jnp.minimum(jnp.maximum(index, 0), key_blocks - 1)
        start = pl.multiple_of(index * BLOCK, BLOCK)
        kbuf[pl.ds(j * BLOCK, BLOCK), :] = table[pl.ds(start, BLOCK), pl.ds(0, head_size)]
        vbuf[pl.ds(j * BLOCK, BLOCK), :] = table[pl.ds(start, BLOCK), pl.ds(head_size, head_size)]
    slot_of = lax.broadcasted_iota(jnp.int32, mask.shape, 1) // BLOCK
    mask[...] = jnp.where(slot_of < count, 1.0, 0.0).astype(mask.dtype)

    logit_scores = (
        lax.dot_general(
            q_ref[...],
            kbuf[...],
            (((1,), (1,)), ((), ())),
            preferred_element_type=jnp.float32,
        )
        * inverse_root
    )
    row_max = jnp.max(logit_scores, axis=1, keepdims=True)
    weights = jnp.exp(logit_scores - row_max)
    width = weights.shape[1]
    weights = (weights.reshape(-1, SUBLANES, width) * mask[...]).reshape(-1, width)
    row_total = jnp.sum(weights, axis=1, keepdims=True)
    weighted_sum = jnp.dot(
        weights.astype(jnp.bfloat16), vbuf[...], preferred_element_type=jnp.float32
    )
    o_ref[...] = (weighted_sum / row_total).astype(o_ref.dtype)


def attend(own, other, lists, counts, narrow, head_size):
    rows = own.shape[0]
    query_blocks = rows // BLOCK
    slots = lists.shape[1]
    kernel = functools.partial(
        attend_kernel, inverse_root=1.0 / math.sqrt(head_size), head_size=head_size
    )
    grid_spec = pltpu.PrefetchScalarGridSpec(
        num_scalar_prefetch=3,
        grid=(query_blocks,),
        in_specs=[
            pl.BlockSpec((BLOCK, head_size), lambda b, *_: (b, 0)),
            pl.BlockSpec(memory_space=pl.ANY),
            pl.BlockSpec(memory_space=pl.ANY),
        ],
        out_specs=pl.BlockSpec((BLOCK, head_size), lambda b, *_: (b, 0)),
        scratch_shapes=[
            pltpu.VMEM((2 * other.shape[0], 2 * head_size), own.dtype),
            pltpu.VMEM((slots * BLOCK, head_size), own.dtype),
            pltpu.VMEM((slots * BLOCK, head_size), own.dtype),
            pltpu.VMEM((SUBLANES, slots * BLOCK), jnp.float32),
            pltpu.SemaphoreType.DMA((2,)),
        ],
    )
    return pl.pallas_call(
        kernel,
        grid_spec=grid_spec,
        out_shape=jax.ShapeDtypeStruct((rows, head_size), jnp.bfloat16),
        compiler_params=pltpu.CompilerParams(dimension_semantics=("arbitrary",)),
    )(lists, counts, narrow, own, own, other)


def per_device(queries, keys, values, block_lists, block_counts):
    rows = queries.shape[0]
    width = lax.axis_size("wide")
    head_size = queries.shape[1] // width
    stacked = jnp.concatenate(
        [a.reshape(rows, width, head_size) for a in (queries, keys, values)], axis=2
    )
    own = lax.all_to_all(stacked, "wide", split_axis=1, concat_axis=0, tiled=True)
    own = own.reshape(rows * width, 3 * head_size)
    other = lax.ppermute(own[:, head_size:], "narrow", [(0, 1), (1, 0)])
    narrow = lax.axis_index("narrow").astype(jnp.int32).reshape(1)
    attended = attend(own, other, block_lists[0], block_counts[0], narrow, head_size)
    return lax.all_to_all(attended, "wide", split_axis=0, concat_axis=1, tiled=True)


def solution(mesh):
    in_specs = (
        P(("groups", "narrow", "wide"), None),
        P(("groups", "narrow", "wide"), None),
        P(("groups", "narrow", "wide"), None),
        P(("groups", "wide"), "narrow", None),
        P(("groups", "wide"), "narrow"),
    )
    out_specs = P(("groups", "narrow", "wide"), None)
    return jax.shard_map(
        per_device, mesh=mesh, in_specs=in_specs, out_specs=out_specs, check_vma=False
    )
```

time: 93.4 us -> 87.5 us (0.937)
  Pallas kernels: 21.9 us -> 17.9 us
  local copies, waits for them, and re-layouts: 5.44 us -> 3.43 us
    pallas_call x1, Pallas kernels: 21.9 us -> 17.9 us  [attend(): pl.pallas_call(kernel, grid_spec=grid_spec, out_shape=jax.ShapeDtypeStruc...]
    slice x1, local copies, waits for them, and re-layouts: 1.1 us -> 0.07 us  [per_device(): other = lax.ppermute(own[:, head_size:], 'narrow', [(0, 1), (1, 0)])]
    unnamed x8 -> x4, local copies, waits for them, and re-layouts: 0.98 us -> 0.01 us
  transfers between devices with their start and end apart: 1 -> 1, of which waited for: 1 -> 1; matrix products, arithmetic and copies ran while one was open for 1% -> 0% of each run, Pallas kernels for 0% -> 0%
where the time goes in v4:
time: 87.5 us; the launch traced here: 87 us
  blocking collectives  62.6 us (72%)
  Pallas kernels  17.9 us (20%)
  local copies, waits for them, and re-layouts  3.43 us (4%)
  waiting for transfers between devices  2.77 us (3%)
    all_to_all x1, blocking collectives, per_device(): lax.all_to_all(stacked, 'wide', split_axis=1, concat_axis=0, tiled=True)  44.1 us
    all_to_all x1, blocking collectives, per_device(): lax.all_to_all(attended, 'wide', split_axis=0, concat_axis=1, tiled=True)  18.5 us
    pallas_call x1, Pallas kernels, attend(): pl.pallas_call(kernel, grid_spec=grid_spec, out_shape=jax.ShapeDtypeStruc...  17.9 us
    ppermute x1, waiting for transfers between devices, per_device(): other = lax.ppermute(own[:, head_size:], 'narrow', [(0, 1), (1, 0)])  2.77 us
    reshape x2, local copies, waits for them, and re-layouts, per_device(): a.reshape(rows, width, head_size)  2.48 us
  transfers between devices with their start and end apart: 1, of which 1 were waited for; matrix products, arithmetic and copies ran while one was open for 0% of the time, Pallas kernels for 0%

profile of v4, /device:TPU:0, one launch (start us, length us, event | category | flops | bytes accessed | tf_op | source)
XLA Modules:
  0.0 87.0 jit_solution(3723576708061705933)
XLA Ops:
  0.0 0.0 copy-start
  0.0 1.2 %copy_bitcast_fusion.3 = bf16[256,8,128]{2,0,1:T(8,128)(2,1)S(1)} fusion(bf16[256,1024]{1,0:T(8,128)(2,1)} %param.5), kind=kLoop, calls=%fused_computation.4 | loop fusion | bytes 1048576 | tf_op jit(solution)/shard_map/reshape | solution.py:121
  1.2 0.0 copy-done
  1.2 1.3 %copy_bitcast_fusion.1 = (bf16[256,8,128]{2,0,1:T(8,128)(2,1)S(1)}, bf16[256,8,128]{2,0,1:T(8,128)(2,1)S(1)}) fusion(bf16[256,1024]{1,0:T(8,128)(2,1)S(1)} %copy-done, bf16[256,1024]{1,0:T(8,128)(2,1)} %param.7), kind=kLoop, calls=%fused_computation.2 | loop fusion | bytes 2097152 | tf_op jit(solution)/shard_map/reshape | solution.py:121
  2.5 0.2 pad_maximum_fusion
  2.7 44.1 %all_to_all.34 = bf16[256,8,384]{2,0,1:T(8,128)(2,1)S(1)} all-to-all(bf16[256,8,384]{2,0,1:T(8,128)(2,1)S(1)} %pad_maximum_fusion), channel_id=1, replica_groups=mesh['groups'=2,'wide'=8,'narrow'=2] {'wide'}, dimensions={1} | all-to-all | bytes 3145728 | tf_op jit(solution)/shard_map/all_to_all | solution.py:123
  46.8 0.0 copy-start.1
  46.8 0.1 slice.4
  46.9 0.1 collective-permute-start
  47.0 2.8 %collective-permute-done.other_ref = bf16[2048,256]{1,0:T(8,128)(2,1)} collective-permute-done((bf16[2048,256]{1,0:T(8,128)(2,1)S(1)}, bf16[2048,256]{1,0:T(8,128)(2,1)}, u32[]{:S(2)}, u32[]{:S(2)}) %collective-permute-start) | collective-permute-done | bytes 1048608 | tf_op jit(solution)/shard_map/ppermute | solution.py:125
  49.8 0.0 copy-done.1
  49.8 17.9 %shard_map.55 = bf16[2048,128]{1,0:T(8,128)(2,1)} custom-call(s32[16,16]{1,0:T(8,128)} %bitcast.34, s32[16]{0:T(128)} %bitcast.35, s32[1]{0:T(128)} %bitcast.2.narrow_ref, bf16[2048,384]{1,0:T(8,128)(2,1)} %bitcast.31, bf16[2048,384]{1,0:T(8,128)(2,1)} %bitcast.32, bf16[2048,256]{1,0:T(8,128)(2,1)} %collective-permute-done.other_ref), custom_call_target="tpu_custom_call" | custom-call | tf_op jit(solution)/shard_map/pallas_call | solution.py:108
  67.7 18.5 %all_to_all.35 = bf16[8,256,128]{2,1,0:T(8,128)(2,1)S(1)} all-to-all(bf16[8,256,128]{2,1,0:T(8,128)(2,1)} %bitcast.33), channel_id=1, replica_groups=mesh['groups'=2,'wide'=8,'narrow'=2] {'wide'}, dimensions={0} | all-to-all | bytes 1048576 | tf_op jit(solution)/shard_map/all_to_all | solution.py:128
  86.1 0.9 %copy_bitcast_fusion = bf16[256,1024]{1,0:T(8,128)(2,1)} fusion(bf16[8,256,128]{2,1,0:T(8,128)(2,1)S(1)} %all_to_all.35), kind=kLoop, calls=%fused_computation.1 | loop fusion | bytes 1048576 | tf_op jit(solution)/shard_map/all_to_all | solution.py:128
Async XLA Ops:
  0.0 1.2 %copy-start = (bf16[256,1024]{1,0:T(8,128)(2,1)S(1)}, bf16[256,1024]{1,0:T(8,128)(2,1)}, u32[]{:S(2)}) copy-start(bf16[256,1024]{1,0:T(8,128)(2,1)} %param.6) | copy-start | bytes 1572868
  46.8 2.9 %copy-start.1 = (bf16[256,8,384]{2,0,1:T(8,128)(2,1)}, bf16[256,8,384]{2,0,1:T(8,128)(2,1)S(1)}, u32[]{:S(2)}) copy-start(bf16[256,8,384]{2,0,1:T(8,128)(2,1)S(1)} %all_to_all.34) | copy-start | bytes 4718596
  46.9 2.9 %collective-permute-start = (bf16[2048,256]{1,0:T(8,128)(2,1)S(1)}, bf16[2048,256]{1,0:T(8,128)(2,1)}, u32[]{:S(2)}, u32[]{:S(2)}) collective-permute-start(bf16[2048,256]{1,0:T(8,128)(2,1)S(1)} %slice.4), channel_id=1, source_target_pairs={{0,1},{1,0},{2,3},{3,2},{4,5},{5,4},{6,7},{7,6},{8,9},{9,8},{10,11... | collective-permute-start | bytes 3145736 | tf_op jit(solution)/shard_map/ppermute | solution.py:125

commit v5 on v4

--- a/solution.py
+++ b/solution.py
@@ -16,6 +16,7 @@
     lists_ref,
     counts_ref,
     narrow_ref,
+    order_ref,
     q_ref,
     own_ref,
     other_ref,
@@ -29,11 +30,12 @@
     inverse_root,
     head_size,
 ):
-    b = pl.program_id(0)
+    step = pl.program_id(0)
+    b = order_ref[step]
     half_rows = other_ref.shape[0]
     n = narrow_ref[0]
 
-    @pl.when(b == 0)
+    @pl.when(step == 0)
     def _():
         own_copy = pltpu.make_async_copy(
             own_ref.at[:, pl.ds(head_size, 2 * head_size)],
@@ -81,18 +83,18 @@
     o_ref[...] = (weighted_sum / row_total).astype(o_ref.dtype)
 
 
-def attend(own, other, lists, counts, narrow, head_size):
-    rows = own.shape[0]
-    query_blocks = rows // BLOCK
+def attend(own, other, lists, counts, narrow, order, head_size):
+    query_blocks = order.shape[0]
+    rows = query_blocks * BLOCK
     slots = lists.shape[1]
     kernel = functools.partial(
         attend_kernel, inverse_root=1.0 / math.sqrt(head_size), head_size=head_size
     )
     grid_spec = pltpu.PrefetchScalarGridSpec(
-        num_scalar_prefetch=3,
+        num_scalar_prefetch=4,
         grid=(query_blocks,),
         in_specs=[
-            pl.BlockSpec((BLOCK, head_size), lambda b, *_: (b, 0)),
+            pl.BlockSpec((BLOCK, head_size), lambda b, lists, counts, narrow, order: (order[b], 0)),
             pl.BlockSpec(memory_space=pl.ANY),
             pl.BlockSpec(memory_space=pl.ANY),
         ],
@@ -110,7 +112,12 @@
         grid_spec=grid_spec,
         out_shape=jax.ShapeDtypeStruct((rows, head_size), jnp.bfloat16),
         compiler_params=pltpu.CompilerParams(dimension_semantics=("arbitrary",)),
-    )(lists, counts, narrow, own, own, other)
+        cost_estimate=pl.CostEstimate(
+            flops=4 * rows * slots * BLOCK * head_size,
+            transcendentals=rows * slots * BLOCK,
+            bytes_accessed=2 * other.size * other.dtype.itemsize + 2 * rows * head_size * 2,
+        ),
+    )(lists, counts, narrow, order, own, own, other)
 
 
 def per_device(queries, keys, values, block_lists, block_counts):
@@ -124,8 +131,31 @@
     own = own.reshape(rows * width, 3 * head_size)
     other = lax.ppermute(own[:, head_size:], "narrow", [(0, 1), (1, 0)])
     narrow = lax.axis_index("narrow").astype(jnp.int32).reshape(1)
-    attended = attend(own, other, block_lists[0], block_counts[0], narrow, head_size)
-    return lax.all_to_all(attended, "wide", split_axis=0, concat_axis=1, tiled=True)
+    w = lax.axis_index("wide").astype(jnp.int32)
+    chunk_blocks = rows // BLOCK
+    shifts = list(range(1, width)) + [0]
+    early = shifts[: width // 2]
+    late = shifts[width // 2 :]
+
+    def block_order(group):
+        group_shifts = jnp.array(group, jnp.int32)
+        dest = (w + group_shifts) % width
+        return (dest[:, None] * chunk_blocks + jnp.arange(chunk_blocks, dtype=jnp.int32)).reshape(-1)
+
+    received = [None] * width
+    for group in (early, late):
+        attended = attend(
+            own, other, block_lists[0], block_counts[0], narrow, block_order(group), head_size
+        )
+        for i, s in enumerate(group):
+            chunk = attended[i * rows : (i + 1) * rows]
+            if s:
+                chunk = lax.ppermute(chunk, "wide", [(d, (d + s) % width) for d in range(width)])
+            received[s] = chunk
+    by_source = jnp.stack(received)
+    sources = (w - jnp.arange(width, dtype=jnp.int32)) % width
+    placed = jnp.zeros_like(by_source).at[sources].set(by_source)
+    return placed.transpose(1, 0, 2).reshape(rows, width * head_size)
 
 
 def solution(mesh):

time: 87.5 us -> 93.8 us (1.072)
  blocking collectives: 62.6 us -> 44.1 us
  starting transfers between devices: 0.07 us -> 10.8 us
  local copies, waits for them, and re-layouts: 3.43 us -> 10.7 us
  Pallas kernels: 17.9 us -> 21.7 us
  waiting for transfers between devices: 2.77 us -> 5.15 us
    all_to_all x1 -> x0, blocking collectives: 18.5 us -> none  [per_device(): lax.all_to_all(attended, 'wide', split_axis=0, concat_axis=1, tiled=True)]
    ppermute x0 -> x7, starting transfers between devices: none -> 10.8 us  [per_device(): lax.ppermute(chunk, 'wide', [(d, (d + s) % width) for d in range(width)])]
    pallas_call x1 -> x2, Pallas kernels: 17.9 us -> 21.7 us  [attend(): pl.pallas_call(kernel, grid_spec=grid_spec, out_shape=jax.ShapeDtypeStruc...]
    ppermute x0 -> x7, waiting for transfers between devices: none -> 3.71 us  [per_device(): lax.ppermute(chunk, 'wide', [(d, (d + s) % width) for d in range(width)])]
    unnamed x4 -> x17, local copies, waits for them, and re-layouts: 0.01 us -> 1.93 us
    slice x0 -> x2, local copies, waits for them, and re-layouts: none -> 1.88 us  [per_device(): chunk = attended[i * rows:(i + 1) * rows]]
    ppermute x1, waiting for transfers between devices: 2.77 us -> 1.44 us  [per_device(): other = lax.ppermute(own[:, head_size:], 'narrow', [(0, 1), (1, 0)])]
    add x0 -> x2, local copies, waits for them, and re-layouts: none -> 1.24 us  [block_order(): dest[:, None] * chunk_blocks + jnp.arange(chunk_blocks, dtype=jnp.int32)]
  transfers between devices with their start and end apart: 1 -> 8, of which waited for: 1 -> 5; matrix products, arithmetic and copies ran while one was open for 0% -> 4% of each run, Pallas kernels for 0% -> 12%
where the time goes in v5:
time: 93.8 us; the launch traced here: 93 us
  blocking collectives  44.1 us (47%)
  Pallas kernels  21.7 us (23%)
  starting transfers between devices  10.8 us (12%)
  local copies, waits for them, and re-layouts  10.7 us (11%)
  waiting for transfers between devices  5.15 us (5%)
    all_to_all x1, blocking collectives, per_device(): lax.all_to_all(stacked, 'wide', split_axis=1, concat_axis=0, tiled=True)  44.1 us
    pallas_call x2, Pallas kernels, attend(): pl.pallas_call(kernel, grid_spec=grid_spec, out_shape=jax.ShapeDtypeStruc...  21.7 us
    ppermute x7, starting transfers between devices, per_device(): lax.ppermute(chunk, 'wide', [(d, (d + s) % width) for d in range(width)])  10.8 us
    ppermute x7, waiting for transfers between devices, per_device(): lax.ppermute(chunk, 'wide', [(d, (d + s) % width) for d in range(width)])  3.71 us
    reshape x2, local copies, waits for them, and re-layouts, per_device(): a.reshape(rows, width, head_size)  2.48 us
    unnamed x17, local copies, waits for them, and re-layouts  1.93 us
    slice x2, local copies, waits for them, and re-layouts, per_device(): chunk = attended[i * rows:(i + 1) * rows]  1.88 us
  transfers between devices with their start and end apart: 8, of which 5 were waited for; matrix products, arithmetic and copies ran while one was open for 4% of the time, Pallas kernels for 12%

profile of v5, /device:TPU:0, one launch (start us, length us, event | category | flops | bytes accessed | tf_op | source)
XLA Modules:
  0.0 93.0 jit_solution(13366087208287213749)
XLA Ops:
  0.0 1.2 %copy_bitcast_fusion.2 = bf16[256,8,128]{2,0,1:T(8,128)(2,1)S(1)} fusion(bf16[256,1024]{1,0:T(8,128)(2,1)} %param.7), kind=kLoop, calls=%fused_computation.4 | loop fusion | bytes 1048576 | tf_op jit(solution)/shard_map/reshape | solution.py:128
  1.2 1.3 %copy_bitcast_fusion = (bf16[256,8,128]{2,0,1:T(8,128)(2,1)S(1)}, bf16[256,8,128]{2,0,1:T(8,128)(2,1)S(1)}) fusion(bf16[256,1024]{1,0:T(8,128)(2,1)S(1)} %copy-done, bf16[256,1024]{1,0:T(8,128)(2,1)} %param.9), kind=kLoop, calls=%fused_computation.2 | loop fusion | bytes 2097152 | tf_op jit(solution)/shard_map/reshape | solution.py:128
  2.5 0.2 pad_maximum_fusion
  2.7 44.1 %all_to_all.15 = bf16[256,8,384]{2,0,1:T(8,128)(2,1)S(1)} all-to-all(bf16[256,8,384]{2,0,1:T(8,128)(2,1)S(1)} %pad_maximum_fusion), channel_id=1, replica_groups=mesh['groups'=2,'wide'=8,'narrow'=2] {'wide'}, dimensions={1} | all-to-all | bytes 3145728 | tf_op jit(solution)/shard_map/all_to_all | solution.py:130
  46.8 1.1 %slice.36 = bf16[2048,256]{1,0:T(8,128)(2,1)} slice(bf16[2048,384]{1,0:T(8,128)(2,1)S(1)} %bitcast.45), slice={[0:2048], [128:384]} | slice | bytes 2097152 | tf_op jit(solution)/shard_map/slice | solution.py:132
  47.9 0.1 iota_add_fusion
  48.0 0.7 add.91.order_ref
  48.6 0.1 iota_add_fusion.1
  48.7 0.6 add.85.order_ref
  49.3 1.4 %collective-permute-done.other_ref = bf16[2048,256]{1,0:T(8,128)(2,1)S(1)} collective-permute-done((bf16[2048,256]{1,0:T(8,128)(2,1)}, bf16[2048,256]{1,0:T(8,128)(2,1)S(1)}, u32[]{:S(2)}, u32[]{:S(2)}) %collective-permute-start) | collective-permute-done | bytes 1048608 | tf_op jit(solution)/shard_map/ppermute | solution.py:132
  50.8 1.0 %copy-done.2 = bf16[2048,256]{1,0:T(8,128)(2,1)} copy-done((bf16[2048,256]{1,0:T(8,128)(2,1)}, bf16[2048,256]{1,0:T(8,128)(2,1)S(1)}, u32[]{:S(2)}) %copy-start.2) | copy-done | bytes 1048600
  51.7 10.9 %shard_map.74 = bf16[1024,128]{1,0:T(8,128)(2,1)} custom-call(s32[16,16]{1,0:T(8,128)} %bitcast.52, s32[16]{0:T(128)} %bitcast.54, s32[1]{0:T(128)} %bitcast.3.narrow_ref, s32[8]{0:T(128)} %add.91.order_ref, bf16[2048,384]{1,0:T(8,128)(2,1)} %bitcast.46, bf16[2048,384]{1,0:T(8,128)(2,1)} %bitcast.47, bf16[2048,256]{1,0:T(8,128)(2,1)} %copy-done.2), custom_call_target="tpu_custom_call" | custom-call | flops 1073741824 | bytes 2621440 | tf_op jit(solution)/shard_map/pallas_call | solution.py:110
  62.6 1.0 %fusion.8 = (bf16[256,128]{1,0:T(8,128)(2,1)S(1)}, bf16[256,128]{1,0:T(8,128)(2,1)S(1)}, bf16[256,128]{1,0:T(8,128)(2,1)S(1)}, bf16[256,128]{1,0:T(8,128)(2,1)S(1)}) fusion(bf16[1024,128]{1,0:T(8,128)(2,1)} %shard_map.74), kind=kLoop, calls=%fused_computation.33 | loop fusion | bytes 524288 | tf_op jit(solution)/shard_map/slice | solution.py:151
  63.6 1.5 %collective-permute-start.1 = (bf16[256,128]{1,0:T(8,128)(2,1)S(1)}, bf16[256,128]{1,0:T(8,128)(2,1)S(1)}, u32[]{:S(2)}, u32[]{:S(2)}) collective-permute-start(bf16[256,128]{1,0:T(8,128)(2,1)S(1)} %get-tuple-element.11), channel_id=1, source_target_pairs={{0,2},{2,4},{4,6},{6,8},{8,10},{10,12},{12,14},{14,0},{1,3},{3,5},... | collective-permute-start | bytes 196616 | tf_op jit(solution)/shard_map/ppermute | solution.py:153
  65.1 10.9 %shard_map.73 = bf16[1024,128]{1,0:T(8,128)(2,1)} custom-call(s32[16,16]{1,0:T(8,128)} %bitcast.53, s32[16]{0:T(128)} %bitcast.55, s32[1]{0:T(128)} %bitcast.3.narrow_ref, s32[8]{0:T(128)} %add.85.order_ref, bf16[2048,384]{1,0:T(8,128)(2,1)} %bitcast.48, bf16[2048,384]{1,0:T(8,128)(2,1)} %bitcast.49, bf16[2048,256]{1,0:T(8,128)(2,1)} %copy-done.2), custom_call_target="tpu_custom_call" | custom-call | flops 1073741824 | bytes 2621440 | tf_op jit(solution)/shard_map/pallas_call | solution.py:110
  75.9 0.9 fusion.7
  76.9 0.8 fusion
  77.7 0.0 collective-permute-start.2
  77.7 1.7 %collective-permute-start.3 = (bf16[256,128]{1,0:T(8,128)(2,1)S(1)}, bf16[256,128]{1,0:T(8,128)(2,1)S(1)}, u32[]{:S(2)}, u32[]{:S(2)}) collective-permute-start(bf16[256,128]{1,0:T(8,128)(2,1)S(1)} %get-tuple-element.9), channel_id=1, source_target_pairs={{0,6},{2,8},{4,10},{6,12},{8,14},{10,0},{12,2},{14,4},{1,7},{3,9},... | collective-permute-start | bytes 196616 | tf_op jit(solution)/shard_map/ppermute | solution.py:153
  79.4 3.2 %collective-permute-start.4 = (bf16[256,128]{1,0:T(8,128)(2,1)S(1)}, bf16[256,128]{1,0:T(8,128)(2,1)S(1)}, u32[]{:S(2)}, u32[]{:S(2)}) collective-permute-start(bf16[256,128]{1,0:T(8,128)(2,1)S(1)} %get-tuple-element.8), channel_id=1, source_target_pairs={{0,8},{2,10},{4,12},{6,14},{8,0},{10,2},{12,4},{14,6},{1,9},{3,11}... | collective-permute-start | bytes 196616 | tf_op jit(solution)/shard_map/ppermute | solution.py:153
  82.7 0.9 collective-permute-start.5
  83.5 0.0 collective-permute-done.1
  83.5 1.8 %collective-permute-start.6 = (bf16[256,128]{1,0:T(8,128)(2,1)S(1)}, bf16[256,128]{1,0:T(8,128)(2,1)S(1)}, u32[]{:S(2)}, u32[]{:S(2)}) collective-permute-start(bf16[256,128]{1,0:T(8,128)(2,1)S(1)} %get-tuple-element.6), channel_id=1, source_target_pairs={{0,12},{2,14},{4,0},{6,2},{8,4},{10,6},{12,8},{14,10},{1,13},{3,15... | collective-permute-start | bytes 196616 | tf_op jit(solution)/shard_map/ppermute | solution.py:153
  85.4 1.7 %collective-permute-start.7 = (bf16[256,128]{1,0:T(8,128)(2,1)S(1)}, bf16[256,128]{1,0:T(8,128)(2,1)S(1)}, u32[]{:S(2)}, u32[]{:S(2)}) collective-permute-start(bf16[256,128]{1,0:T(8,128)(2,1)S(1)} %get-tuple-element.5), channel_id=1, source_target_pairs={{0,14},{2,0},{4,2},{6,4},{8,6},{10,8},{12,10},{14,12},{1,15},{3,1}... | collective-permute-start | bytes 196616 | tf_op jit(solution)/shard_map/ppermute | solution.py:153
  87.1 1.0 %collective-permute-done.3 = bf16[256,128]{1,0:T(8,128)(2,1)S(1)} collective-permute-done((bf16[256,128]{1,0:T(8,128)(2,1)S(1)}, bf16[256,128]{1,0:T(8,128)(2,1)S(1)}, u32[]{:S(2)}, u32[]{:S(2)}) %collective-permute-start.3) | collective-permute-done | bytes 65568 | tf_op jit(solution)/shard_map/ppermute | solution.py:153
  88.1 1.2 %collective-permute-done.4 = bf16[256,128]{1,0:T(8,128)(2,1)S(1)} collective-permute-done((bf16[256,128]{1,0:T(8,128)(2,1)S(1)}, bf16[256,128]{1,0:T(8,128)(2,1)S(1)}, u32[]{:S(2)}, u32[]{:S(2)}) %collective-permute-start.4) | collective-permute-done | bytes 65568 | tf_op jit(solution)/shard_map/ppermute | solution.py:153
  89.3 0.4 collective-permute-done.5
  89.7 1.1 %collective-permute-done.6 = bf16[256,128]{1,0:T(8,128)(2,1)S(1)} collective-permute-done((bf16[256,128]{1,0:T(8,128)(2,1)S(1)}, bf16[256,128]{1,0:T(8,128)(2,1)S(1)}, u32[]{:S(2)}, u32[]{:S(2)}) %collective-permute-start.6) | collective-permute-done | bytes 65568 | tf_op jit(solution)/shard_map/ppermute | solution.py:153
  90.9 0.1 broadcast_in_dim.2
  91.0 0.9 scatter_fusion
  91.8 0.2 copy.17
  92.0 1.0 %copy.18 = bf16[256,1024]{1,0:T(8,128)(2,1)} copy(bf16[256,1024]{0,1:T(8,128)(2,1)S(1)} %bitcast.51) | data formatting | bytes 1048576 | tf_op jit(solution)/shard_map/reshape | solution.py:158
  (21 shorter events, 0.1 us)
Async XLA Ops:
  0.0 1.2 %copy-start = (bf16[256,1024]{1,0:T(8,128)(2,1)S(1)}, bf16[256,1024]{1,0:T(8,128)(2,1)}, u32[]{:S(2)}) copy-start(bf16[256,1024]{1,0:T(8,128)(2,1)} %param.8) | copy-start | bytes 1572868
  46.8 3.9 %copy-start.1 = (bf16[256,8,384]{2,0,1:T(8,128)(2,1)}, bf16[256,8,384]{2,0,1:T(8,128)(2,1)S(1)}, u32[]{:S(2)}) copy-start(bf16[256,8,384]{2,0,1:T(8,128)(2,1)S(1)} %all_to_all.15) | copy-start | bytes 4718596
  46.8 1.1 %copy-start.3 = (s32[4]{0:T(128)S(1)}, s32[4]{0:T(128)}, u32[]{:S(2)}) copy-start(s32[4]{0:T(128)} %constant.46.clone) | copy-start | bytes 52
  46.8 1.1 %copy-start.4 = (s32[4]{0:T(128)S(1)}, s32[4]{0:T(128)}, u32[]{:S(2)}) copy-start(s32[4]{0:T(128)} %constant.47.clone) | copy-start | bytes 52
  47.9 2.9 %collective-permute-start = (bf16[2048,256]{1,0:T(8,128)(2,1)}, bf16[2048,256]{1,0:T(8,128)(2,1)S(1)}, u32[]{:S(2)}, u32[]{:S(2)}) collective-permute-start(bf16[2048,256]{1,0:T(8,128)(2,1)} %slice.36), channel_id=1, source_target_pairs={{0,1},{1,0},{2,3},{3,2},{4,5},{5,4},{6,7},{7,6},{8,9},{9,8},{10,11... | collective-permute-start | bytes 3145736 | tf_op jit(solution)/shard_map/ppermute | solution.py:132
  50.8 1.0 %copy-start.2 = (bf16[2048,256]{1,0:T(8,128)(2,1)}, bf16[2048,256]{1,0:T(8,128)(2,1)S(1)}, u32[]{:S(2)}) copy-start(bf16[2048,256]{1,0:T(8,128)(2,1)S(1)} %collective-permute-done.other_ref) | copy-start | bytes 3145732
  63.6 20.0 %collective-permute-start.1 = (bf16[256,128]{1,0:T(8,128)(2,1)S(1)}, bf16[256,128]{1,0:T(8,128)(2,1)S(1)}, u32[]{:S(2)}, u32[]{:S(2)}) collective-permute-start(bf16[256,128]{1,0:T(8,128)(2,1)S(1)} %get-tuple-element.11), channel_id=1, source_target_pairs={{0,2},{2,4},{4,6},{6,8},{8,10},{10,12},{12,14},{14,0},{1,3},{3,5},... | collective-permute-start | bytes 196616 | tf_op jit(solution)/shard_map/ppermute | solution.py:153
  77.7 7.7 %collective-permute-start.2 = (bf16[256,128]{1,0:T(8,128)(2,1)S(1)}, bf16[256,128]{1,0:T(8,128)(2,1)S(1)}, u32[]{:S(2)}, u32[]{:S(2)}) collective-permute-start(bf16[256,128]{1,0:T(8,128)(2,1)S(1)} %get-tuple-element.10), channel_id=1, source_target_pairs={{0,4},{2,6},{4,8},{6,10},{8,12},{10,14},{12,0},{14,2},{1,5},{3,7},... | collective-permute-start | bytes 196616 | tf_op jit(solution)/shard_map/ppermute | solution.py:153
  77.7 10.3 %collective-permute-start.3 = (bf16[256,128]{1,0:T(8,128)(2,1)S(1)}, bf16[256,128]{1,0:T(8,128)(2,1)S(1)}, u32[]{:S(2)}, u32[]{:S(2)}) collective-permute-start(bf16[256,128]{1,0:T(8,128)(2,1)S(1)} %get-tuple-element.9), channel_id=1, source_target_pairs={{0,6},{2,8},{4,10},{6,12},{8,14},{10,0},{12,2},{14,4},{1,7},{3,9},... | collective-permute-start | bytes 196616 | tf_op jit(solution)/shard_map/ppermute | solution.py:153
  79.4 9.9 %collective-permute-start.4 = (bf16[256,128]{1,0:T(8,128)(2,1)S(1)}, bf16[256,128]{1,0:T(8,128)(2,1)S(1)}, u32[]{:S(2)}, u32[]{:S(2)}) collective-permute-start(bf16[256,128]{1,0:T(8,128)(2,1)S(1)} %get-tuple-element.8), channel_id=1, source_target_pairs={{0,8},{2,10},{4,12},{6,14},{8,0},{10,2},{12,4},{14,6},{1,9},{3,11}... | collective-permute-start | bytes 196616 | tf_op jit(solution)/shard_map/ppermute | solution.py:153
  82.7 7.0 %collective-permute-start.5 = (bf16[256,128]{1,0:T(8,128)(2,1)S(1)}, bf16[256,128]{1,0:T(8,128)(2,1)S(1)}, u32[]{:S(2)}, u32[]{:S(2)}) collective-permute-start(bf16[256,128]{1,0:T(8,128)(2,1)S(1)} %get-tuple-element.7), channel_id=1, source_target_pairs={{0,10},{2,12},{4,14},{6,0},{8,2},{10,4},{12,6},{14,8},{1,11},{3,13... | collective-permute-start | bytes 196616 | tf_op jit(solution)/shard_map/ppermute | solution.py:153
  83.5 7.3 %collective-permute-start.6 = (bf16[256,128]{1,0:T(8,128)(2,1)S(1)}, bf16[256,128]{1,0:T(8,128)(2,1)S(1)}, u32[]{:S(2)}, u32[]{:S(2)}) collective-permute-start(bf16[256,128]{1,0:T(8,128)(2,1)S(1)} %get-tuple-element.6), channel_id=1, source_target_pairs={{0,12},{2,14},{4,0},{6,2},{8,4},{10,6},{12,8},{14,10},{1,13},{3,15... | collective-permute-start | bytes 196616 | tf_op jit(solution)/shard_map/ppermute | solution.py:153
  85.4 5.4 %collective-permute-start.7 = (bf16[256,128]{1,0:T(8,128)(2,1)S(1)}, bf16[256,128]{1,0:T(8,128)(2,1)S(1)}, u32[]{:S(2)}, u32[]{:S(2)}) collective-permute-start(bf16[256,128]{1,0:T(8,128)(2,1)S(1)} %get-tuple-element.5), channel_id=1, source_target_pairs={{0,14},{2,0},{4,2},{6,4},{8,6},{10,8},{12,10},{14,12},{1,15},{3,1}... | collective-permute-start | bytes 196616 | tf_op jit(solution)/shard_map/ppermute | solution.py:153

commit v6 on v4

--- a/solution.py
+++ b/solution.py
@@ -10,6 +10,7 @@
 
 BLOCK = 128
 SUBLANES = 8
+GROUP = 8
 
 
 def attend_kernel(
@@ -29,11 +30,11 @@
     inverse_root,
     head_size,
 ):
-    b = pl.program_id(0)
+    step = pl.program_id(0)
     half_rows = other_ref.shape[0]
     n = narrow_ref[0]
 
-    @pl.when(b == 0)
+    @pl.when(step == 0)
     def _():
         own_copy = pltpu.make_async_copy(
             own_ref.at[:, pl.ds(head_size, 2 * head_size)],
@@ -48,60 +49,68 @@
         own_copy.wait()
         other_copy.wait()
 
-    count = counts_ref[b]
+    group = q_ref.shape[0] // BLOCK
     slots = lists_ref.shape[1]
     key_blocks = table.shape[0] // BLOCK
-    first = lists_ref[b, 0]
-    for j in range(slots):
-        index = jnp.where(j < count, lists_ref[b, j], first)
-        index = jnp.minimum(jnp.maximum(index, 0), key_blocks - 1)
-        start = pl.multiple_of(index * BLOCK, BLOCK)
-        kbuf[pl.ds(j * BLOCK, BLOCK), :] = table[pl.ds(start, BLOCK), pl.ds(0, head_size)]
-        vbuf[pl.ds(j * BLOCK, BLOCK), :] = table[pl.ds(start, BLOCK), pl.ds(head_size, head_size)]
-    slot_of = lax.broadcasted_iota(jnp.int32, mask.shape, 1) // BLOCK
-    mask[...] = jnp.where(slot_of < count, 1.0, 0.0).astype(mask.dtype)
+    for g in range(group):
+        b = step * group + g
+        count = counts_ref[b]
+        first = lists_ref[b, 0]
+        for j in range(slots):
+            index = jnp.where(j < count, lists_ref[b, j], first)
+            index = jnp.minimum(jnp.maximum(index, 0), key_blocks - 1)
+            start = pl.multiple_of(index * BLOCK, BLOCK)
+            kbuf[g, pl.ds(j * BLOCK, BLOCK), :] = table[pl.ds(start, BLOCK), pl.ds(0, head_size)]
+            vbuf[g, pl.ds(j * BLOCK, BLOCK), :] = table[
+                pl.ds(start, BLOCK), pl.ds(head_size, head_size)
+            ]
+        slot_of = lax.broadcasted_iota(jnp.int32, mask.shape[1:], 1) // BLOCK
+        mask[g] = jnp.where(slot_of < count, 1.0, 0.0).astype(mask.dtype)
 
-    logit_scores = (
-        lax.dot_general(
-            q_ref[...],
-            kbuf[...],
-            (((1,), (1,)), ((), ())),
-            preferred_element_type=jnp.float32,
+    for g in range(group):
+        rows = pl.ds(g * BLOCK, BLOCK)
+        logit_scores = (
+            lax.dot_general(
+                q_ref[rows, :],
+                kbuf[g],
+                (((1,), (1,)), ((), ())),
+                preferred_element_type=jnp.float32,
+            )
+            * inverse_root
         )
-        * inverse_root
-    )
-    row_max = jnp.max(logit_scores, axis=1, keepdims=True)
-    weights = jnp.exp(logit_scores - row_max)
-    width = weights.shape[1]
-    weights = (weights.reshape(-1, SUBLANES, width) * mask[...]).reshape(-1, width)
-    row_total = jnp.sum(weights, axis=1, keepdims=True)
-    weighted_sum = jnp.dot(
-        weights.astype(jnp.bfloat16), vbuf[...], preferred_element_type=jnp.float32
-    )
-    o_ref[...] = (weighted_sum / row_total).astype(o_ref.dtype)
+        row_max = jnp.max(logit_scores, axis=1, keepdims=True)
+        weights = jnp.exp(logit_scores - row_max)
+        width = weights.shape[1]
+        weights = (weights.reshape(-1, SUBLANES, width) * mask[g]).reshape(-1, width)
+        row_total = jnp.sum(weights, axis=1, keepdims=True)
+        weighted_sum = jnp.dot(
+            weights.astype(jnp.bfloat16), vbuf[g], preferred_element_type=jnp.float32
+        )
+        o_ref[rows, :] = (weighted_sum / row_total).astype(o_ref.dtype)
 
 
 def attend(own, other, lists, counts, narrow, head_size):
     rows = own.shape[0]
     query_blocks = rows // BLOCK
+    group = max(g for g in range(1, GROUP + 1) if query_blocks % g == 0)
     slots = lists.shape[1]
     kernel = functools.partial(
         attend_kernel, inverse_root=1.0 / math.sqrt(head_size), head_size=head_size
     )
     grid_spec = pltpu.PrefetchScalarGridSpec(
         num_scalar_prefetch=3,
-        grid=(query_blocks,),
+        grid=(query_blocks // group,),
         in_specs=[
-            pl.BlockSpec((BLOCK, head_size), lambda b, *_: (b, 0)),
+            pl.BlockSpec((group * BLOCK, head_size), lambda b, *_: (b, 0)),
             pl.BlockSpec(memory_space=pl.ANY),
             pl.BlockSpec(memory_space=pl.ANY),
         ],
-        out_specs=pl.BlockSpec((BLOCK, head_size), lambda b, *_: (b, 0)),
+        out_specs=pl.BlockSpec((group * BLOCK, head_size), lambda b, *_: (b, 0)),
         scratch_shapes=[
             pltpu.VMEM((2 * other.shape[0], 2 * head_size), own.dtype),
-            pltpu.VMEM((slots * BLOCK, head_size), own.dtype),
-            pltpu.VMEM((slots * BLOCK, head_size), own.dtype),
-            pltpu.VMEM((SUBLANES, slots * BLOCK), jnp.float32),
+            pltpu.VMEM((group, slots * BLOCK, head_size), own.dtype),
+            pltpu.VMEM((group, slots * BLOCK, head_size), own.dtype),
+            pltpu.VMEM((group, SUBLANES, slots * BLOCK), jnp.float32),
             pltpu.SemaphoreType.DMA((2,)),
         ],
     )

time: 87.5 us -> 83.8 us (0.958)
  Pallas kernels: 17.9 us -> 14.3 us
    pallas_call x1, Pallas kernels: 17.9 us -> 14.3 us  [attend(): pl.pallas_call(kernel, grid_spec=grid_spec, out_shape=jax.ShapeDtypeStruc...]
where the time goes in v6:
time: 83.8 us; the launch traced here: 83.4 us
  blocking collectives  62.6 us (75%)
  Pallas kernels  14.3 us (17%)
  local copies, waits for them, and re-layouts  3.43 us (4%)
  waiting for transfers between devices  2.77 us (3%)
    all_to_all x1, blocking collectives, per_device(): lax.all_to_all(stacked, 'wide', split_axis=1, concat_axis=0, tiled=True)  44.1 us
    all_to_all x1, blocking collectives, per_device(): lax.all_to_all(attended, 'wide', split_axis=0, concat_axis=1, tiled=True)  18.5 us
    pallas_call x1, Pallas kernels, attend(): pl.pallas_call(kernel, grid_spec=grid_spec, out_shape=jax.ShapeDtypeStruc...  14.3 us
    ppermute x1, waiting for transfers between devices, per_device(): other = lax.ppermute(own[:, head_size:], 'narrow', [(0, 1), (1, 0)])  2.77 us
    reshape x2, local copies, waits for them, and re-layouts, per_device(): a.reshape(rows, width, head_size)  2.48 us
  transfers between devices with their start and end apart: 1, of which 1 were waited for; matrix products, arithmetic and copies ran while one was open for 0% of the time, Pallas kernels for 0%

profile of v6, /device:TPU:0, one launch (start us, length us, event | category | flops | bytes accessed | tf_op | source)
XLA Modules:
  0.0 83.4 jit_solution(3167548365291733369)
XLA Ops:
  0.0 0.0 copy-start
  0.0 1.2 %copy_bitcast_fusion.3 = bf16[256,8,128]{2,0,1:T(8,128)(2,1)S(1)} fusion(bf16[256,1024]{1,0:T(8,128)(2,1)} %param.5), kind=kLoop, calls=%fused_computation.4 | loop fusion | bytes 1048576 | tf_op jit(solution)/shard_map/reshape | solution.py:130
  1.2 0.0 copy-done
  1.2 1.3 %copy_bitcast_fusion.1 = (bf16[256,8,128]{2,0,1:T(8,128)(2,1)S(1)}, bf16[256,8,128]{2,0,1:T(8,128)(2,1)S(1)}) fusion(bf16[256,1024]{1,0:T(8,128)(2,1)S(1)} %copy-done, bf16[256,1024]{1,0:T(8,128)(2,1)} %param.7), kind=kLoop, calls=%fused_computation.2 | loop fusion | bytes 2097152 | tf_op jit(solution)/shard_map/reshape | solution.py:130
  2.5 0.2 pad_maximum_fusion
  2.7 44.1 %all_to_all.34 = bf16[256,8,384]{2,0,1:T(8,128)(2,1)S(1)} all-to-all(bf16[256,8,384]{2,0,1:T(8,128)(2,1)S(1)} %pad_maximum_fusion), channel_id=1, replica_groups=mesh['groups'=2,'wide'=8,'narrow'=2] {'wide'}, dimensions={1} | all-to-all | bytes 3145728 | tf_op jit(solution)/shard_map/all_to_all | solution.py:132
  46.8 0.0 copy-start.1
  46.8 0.1 slice.4
  46.9 0.1 collective-permute-start
  47.0 2.8 %collective-permute-done.other_ref = bf16[2048,256]{1,0:T(8,128)(2,1)} collective-permute-done((bf16[2048,256]{1,0:T(8,128)(2,1)S(1)}, bf16[2048,256]{1,0:T(8,128)(2,1)}, u32[]{:S(2)}, u32[]{:S(2)}) %collective-permute-start) | collective-permute-done | bytes 1048608 | tf_op jit(solution)/shard_map/ppermute | solution.py:134
  49.8 0.0 copy-done.1
  49.8 14.3 %shard_map.55 = bf16[2048,128]{1,0:T(8,128)(2,1)} custom-call(s32[16,16]{1,0:T(8,128)} %bitcast.34, s32[16]{0:T(128)} %bitcast.35, s32[1]{0:T(128)} %bitcast.2.narrow_ref, bf16[2048,384]{1,0:T(8,128)(2,1)} %bitcast.31, bf16[2048,384]{1,0:T(8,128)(2,1)} %bitcast.32, bf16[2048,256]{1,0:T(8,128)(2,1)} %collective-permute-done.other_ref), custom_call_target="tpu_custom_call" | custom-call | tf_op jit(solution)/shard_map/pallas_call | solution.py:117
  64.0 18.5 %all_to_all.35 = bf16[8,256,128]{2,1,0:T(8,128)(2,1)S(1)} all-to-all(bf16[8,256,128]{2,1,0:T(8,128)(2,1)} %bitcast.33), channel_id=1, replica_groups=mesh['groups'=2,'wide'=8,'narrow'=2] {'wide'}, dimensions={0} | all-to-all | bytes 1048576 | tf_op jit(solution)/shard_map/all_to_all | solution.py:137
  82.5 0.9 %copy_bitcast_fusion = bf16[256,1024]{1,0:T(8,128)(2,1)} fusion(bf16[8,256,128]{2,1,0:T(8,128)(2,1)S(1)} %all_to_all.35), kind=kLoop, calls=%fused_computation.1 | loop fusion | bytes 1048576 | tf_op jit(solution)/shard_map/all_to_all | solution.py:137
Async XLA Ops:
  0.0 1.2 %copy-start = (bf16[256,1024]{1,0:T(8,128)(2,1)S(1)}, bf16[256,1024]{1,0:T(8,128)(2,1)}, u32[]{:S(2)}) copy-start(bf16[256,1024]{1,0:T(8,128)(2,1)} %param.6) | copy-start | bytes 1572868
  46.8 2.9 %copy-start.1 = (bf16[256,8,384]{2,0,1:T(8,128)(2,1)}, bf16[256,8,384]{2,0,1:T(8,128)(2,1)S(1)}, u32[]{:S(2)}) copy-start(bf16[256,8,384]{2,0,1:T(8,128)(2,1)S(1)} %all_to_all.34) | copy-start | bytes 4718596
  46.9 2.9 %collective-permute-start = (bf16[2048,256]{1,0:T(8,128)(2,1)S(1)}, bf16[2048,256]{1,0:T(8,128)(2,1)}, u32[]{:S(2)}, u32[]{:S(2)}) collective-permute-start(bf16[2048,256]{1,0:T(8,128)(2,1)S(1)} %slice.4), channel_id=1, source_target_pairs={{0,1},{1,0},{2,3},{3,2},{4,5},{5,4},{6,7},{7,6},{8,9},{9,8},{10,11... | collective-permute-start | bytes 3145736 | tf_op jit(solution)/shard_map/ppermute | solution.py:134

commit v7 on v6

--- a/solution.py
+++ b/solution.py
@@ -2,6 +2,7 @@
 import math
 
 import jax
+import numpy as np
 import jax.numpy as jnp
 from jax import lax
 from jax.experimental import pallas as pl
@@ -17,6 +18,7 @@
     lists_ref,
     counts_ref,
     narrow_ref,
+    order_ref,
     q_ref,
     own_ref,
     other_ref,
@@ -49,11 +51,11 @@
         own_copy.wait()
         other_copy.wait()
 
-    group = q_ref.shape[0] // BLOCK
+    group = o_ref.shape[0] // BLOCK
     slots = lists_ref.shape[1]
     key_blocks = table.shape[0] // BLOCK
     for g in range(group):
-        b = step * group + g
+        b = order_ref[step * group + g]
         count = counts_ref[b]
         first = lists_ref[b, 0]
         for j in range(slots):
@@ -69,9 +71,11 @@
 
     for g in range(group):
         rows = pl.ds(g * BLOCK, BLOCK)
+        b = order_ref[step * group + g]
+        q_rows = pl.ds(pl.multiple_of(b * BLOCK, BLOCK), BLOCK)
         logit_scores = (
             lax.dot_general(
-                q_ref[rows, :],
+                q_ref[q_rows, pl.ds(0, head_size)],
                 kbuf[g],
                 (((1,), (1,)), ((), ())),
                 preferred_element_type=jnp.float32,
@@ -89,19 +93,19 @@
         o_ref[rows, :] = (weighted_sum / row_total).astype(o_ref.dtype)
 
 
-def attend(own, other, lists, counts, narrow, head_size):
-    rows = own.shape[0]
-    query_blocks = rows // BLOCK
+def attend(own, other, lists, counts, narrow, order, head_size):
+    query_blocks = order.shape[0]
+    rows = query_blocks * BLOCK
     group = max(g for g in range(1, GROUP + 1) if query_blocks % g == 0)
     slots = lists.shape[1]
     kernel = functools.partial(
         attend_kernel, inverse_root=1.0 / math.sqrt(head_size), head_size=head_size
     )
     grid_spec = pltpu.PrefetchScalarGridSpec(
-        num_scalar_prefetch=3,
+        num_scalar_prefetch=4,
         grid=(query_blocks // group,),
         in_specs=[
-            pl.BlockSpec((group * BLOCK, head_size), lambda b, *_: (b, 0)),
+            pl.BlockSpec(own.shape, lambda b, *_: (0, 0)),
             pl.BlockSpec(memory_space=pl.ANY),
             pl.BlockSpec(memory_space=pl.ANY),
         ],
@@ -119,7 +123,7 @@
         grid_spec=grid_spec,
         out_shape=jax.ShapeDtypeStruct((rows, head_size), jnp.bfloat16),
         compiler_params=pltpu.CompilerParams(dimension_semantics=("arbitrary",)),
-    )(lists, counts, narrow, own, own, other)
+    )(lists, counts, narrow, order, own, own, other)
 
 
 def per_device(queries, keys, values, block_lists, block_counts):
@@ -133,8 +137,23 @@
     own = own.reshape(rows * width, 3 * head_size)
     other = lax.ppermute(own[:, head_size:], "narrow", [(0, 1), (1, 0)])
     narrow = lax.axis_index("narrow").astype(jnp.int32).reshape(1)
-    attended = attend(own, other, block_lists[0], block_counts[0], narrow, head_size)
-    return lax.all_to_all(attended, "wide", split_axis=0, concat_axis=1, tiled=True)
+    chunk_blocks = rows // BLOCK
+    split = max(chunk_blocks // 2, 1)
+    parts = []
+    for part in (range(split), range(split, chunk_blocks)):
+        if not len(part):
+            continue
+        order = (
+            np.arange(width)[:, None] * chunk_blocks + np.array(list(part))[None, :]
+        ).reshape(-1)
+        attended = attend(
+            own, other, block_lists[0], block_counts[0], narrow, jnp.asarray(order, jnp.int32),
+            head_size,
+        )
+        attended = attended.reshape(width, len(part) * BLOCK, head_size)
+        parts.append(lax.all_to_all(attended, "wide", split_axis=0, concat_axis=0, tiled=True))
+    by_head = jnp.concatenate(parts, axis=1)
+    return by_head.transpose(1, 0, 2).reshape(rows, width * head_size)
 
 
 def solution(mesh):

time: 83.8 us -> 90.7 us (1.082)
  Pallas kernels: 14.3 us -> 19.1 us
  blocking collectives: 62.6 us -> 58.8 us
  starting transfers between devices: 0.07 us -> 3.6 us
  other arithmetic: 0.22 us -> 1.6 us
  local copies, waits for them, and re-layouts: 3.43 us -> 4.58 us
    pallas_call x1 -> x2, Pallas kernels: 14.3 us -> 19.1 us  [attend(): pl.pallas_call(kernel, grid_spec=grid_spec, out_shape=jax.ShapeDtypeStruc...]
    all_to_all x1, blocking collectives: 18.5 us -> 14.7 us  [per_device(): lax.all_to_all(attended, 'wide', split_axis=0, concat_axis=0, tiled=True)]
    all_to_all x0 -> x1, starting transfers between devices: none -> 3.6 us  [per_device(): lax.all_to_all(attended, 'wide', split_axis=0, concat_axis=0, tiled=True)]
    slice x1, local copies, waits for them, and re-layouts: 0.07 us -> 1.11 us  [per_device(): other = lax.ppermute(own[:, head_size:], 'narrow', [(0, 1), (1, 0)])]
    unnamed x4 -> x6, local copies, waits for them, and re-layouts: 0.01 us -> 0.99 us
  transfers between devices with their start and end apart: 1 -> 2, of which waited for: 1 -> 1; matrix products, arithmetic and copies ran while one was open for 0% -> 1% of each run, Pallas kernels for 0% -> 11%
where the time goes in v7:
time: 90.7 us; the launch traced here: 90.1 us
  blocking collectives  58.8 us (65%)
  Pallas kernels  19.1 us (21%)
  local copies, waits for them, and re-layouts  4.58 us (5%)
  starting transfers between devices  3.6 us (4%)
  waiting for transfers between devices  2.36 us (3%)
  other arithmetic  1.6 us (2%)
    all_to_all x1, blocking collectives, per_device(): lax.all_to_all(stacked, 'wide', split_axis=1, concat_axis=0, tiled=True)  44.1 us
    pallas_call x2, Pallas kernels, attend(): pl.pallas_call(kernel, grid_spec=grid_spec, out_shape=jax.ShapeDtypeStruc...  19.1 us
    all_to_all x1, blocking collectives, per_device(): lax.all_to_all(attended, 'wide', split_axis=0, concat_axis=0, tiled=True)  14.7 us
    all_to_all x1, starting transfers between devices, per_device(): lax.all_to_all(attended, 'wide', split_axis=0, concat_axis=0, tiled=True)  3.6 us
    reshape x2, local copies, waits for them, and re-layouts, per_device(): a.reshape(rows, width, head_size)  2.48 us
    ppermute x1, waiting for transfers between devices, per_device(): other = lax.ppermute(own[:, head_size:], 'narrow', [(0, 1), (1, 0)])  2.35 us
  transfers between devices with their start and end apart: 2, of which 1 were waited for; matrix products, arithmetic and copies ran while one was open for 1% of the time, Pallas kernels for 11%

profile of v7, /device:TPU:0, one launch (start us, length us, event | category | flops | bytes accessed | tf_op | source)
XLA Modules:
  0.0 90.1 jit_solution(11855833187743480604)
XLA Ops:
  0.0 0.0 copy-start
  0.0 1.2 %copy_bitcast_fusion.3 = bf16[256,8,128]{2,0,1:T(8,128)(2,1)S(1)} fusion(bf16[256,1024]{1,0:T(8,128)(2,1)} %param.7), kind=kLoop, calls=%fused_computation.4 | loop fusion | bytes 1048576 | tf_op jit(solution)/shard_map/reshape | solution.py:134
  1.2 0.0 copy-done
  1.2 1.3 %copy_bitcast_fusion.1 = (bf16[256,8,128]{2,0,1:T(8,128)(2,1)S(1)}, bf16[256,8,128]{2,0,1:T(8,128)(2,1)S(1)}) fusion(bf16[256,1024]{1,0:T(8,128)(2,1)S(1)} %copy-done, bf16[256,1024]{1,0:T(8,128)(2,1)} %param.9), kind=kLoop, calls=%fused_computation.2 | loop fusion | bytes 2097152 | tf_op jit(solution)/shard_map/reshape | solution.py:134
  2.5 0.2 pad_maximum_fusion
  2.7 44.1 %all_to_all.25 = bf16[256,8,384]{2,0,1:T(8,128)(2,1)S(1)} all-to-all(bf16[256,8,384]{2,0,1:T(8,128)(2,1)S(1)} %pad_maximum_fusion), channel_id=1, replica_groups=mesh['groups'=2,'wide'=8,'narrow'=2] {'wide'}, dimensions={1} | all-to-all | bytes 3145728 | tf_op jit(solution)/shard_map/all_to_all | solution.py:136
  46.8 0.0 copy-start.1
  46.8 1.1 %slice.4 = bf16[2048,256]{1,0:T(8,128)(2,1)} slice(bf16[2048,384]{1,0:T(8,128)(2,1)S(1)} %bitcast.31), slice={[0:2048], [128:384]} | slice | bytes 2097152 | tf_op jit(solution)/shard_map/slice | solution.py:138
  47.9 0.0 collective-permute-start
  47.9 0.5 iota_multiply_fusion.order_ref
  48.4 2.4 %collective-permute-done.other_ref = bf16[2048,256]{1,0:T(8,128)(2,1)S(1)} collective-permute-done((bf16[2048,256]{1,0:T(8,128)(2,1)}, bf16[2048,256]{1,0:T(8,128)(2,1)S(1)}, u32[]{:S(2)}, u32[]{:S(2)}) %collective-permute-start) | collective-permute-done | bytes 1048608 | tf_op jit(solution)/shard_map/ppermute | solution.py:138
  50.8 0.0 copy-start.2
  50.8 0.0 copy-done.1
  50.8 1.0 %copy-done.2 = bf16[2048,256]{1,0:T(8,128)(2,1)} copy-done((bf16[2048,256]{1,0:T(8,128)(2,1)}, bf16[2048,256]{1,0:T(8,128)(2,1)S(1)}, u32[]{:S(2)}) %copy-start.2) | copy-done | bytes 1048600
  51.8 9.5 %shard_map.73 = bf16[1024,128]{1,0:T(8,128)(2,1)} custom-call(s32[16,16]{1,0:T(8,128)} %bitcast.38, s32[16]{0:T(128)} %bitcast.40, s32[1]{0:T(128)} %bitcast.2.narrow_ref, s32[8]{0:T(128)} %iota_multiply_fusion.order_ref, bf16[2048,384]{1,0:T(8,128)(2,1)} %bitcast.32, bf16[2048,384]{1,0:T(8,128)(2,1)} %bitcast.33, bf16[2048,256]{1,0:T(8,128)(2,1)} %copy-done.2), custom_call_target="tpu_custom_call" | custom-call | tf_op jit(solution)/shard_map/pallas_call | solution.py:121
  61.3 3.6 %all-to-all-start.1 = ((bf16[8,128,128]{2,1,0:T(8,128)(2,1)}), bf16[8,128,128]{2,1,0:T(8,128)(2,1)S(1)}, u32[]{:S(2)}, u32[]{:S(2)}) async-start(bf16[8,128,128]{2,1,0:T(8,128)(2,1)} %bitcast.36), calls=%async_computation.1 | async-start | bytes 524288 | tf_op jit(solution)/shard_map/all_to_all | solution.py:154
  64.9 9.6 %shard_map.74 = bf16[1024,128]{1,0:T(8,128)(2,1)} custom-call(s32[16,16]{1,0:T(8,128)} %bitcast.39, s32[16]{0:T(128)} %bitcast.41, s32[1]{0:T(128)} %bitcast.2.narrow_ref, s32[8]{0:T(128)} %constant.10.clone.order_ref, bf16[2048,384]{1,0:T(8,128)(2,1)} %bitcast.34, bf16[2048,384]{1,0:T(8,128)(2,1)} %bitcast.35, bf16[2048,256]{1,0:T(8,128)(2,1)} %copy-done.2), custom_call_target="tpu_custom_call" | custom-call | tf_op jit(solution)/shard_map/pallas_call | solution.py:121
  74.5 0.0 all-to-all-done.1
  74.5 14.7 %all_to_all.26 = bf16[8,128,128]{2,1,0:T(8,128)(2,1)S(1)} all-to-all(bf16[8,128,128]{2,1,0:T(8,128)(2,1)} %bitcast.37), channel_id=1, replica_groups=mesh['groups'=2,'wide'=8,'narrow'=2] {'wide'}, dimensions={0} | all-to-all | bytes 524288 | tf_op jit(solution)/shard_map/all_to_all | solution.py:154
  89.2 0.9 copy_bitcast_fusion
Async XLA Ops:
  0.0 1.2 %copy-start = (bf16[256,1024]{1,0:T(8,128)(2,1)S(1)}, bf16[256,1024]{1,0:T(8,128)(2,1)}, u32[]{:S(2)}) copy-start(bf16[256,1024]{1,0:T(8,128)(2,1)} %param.8) | copy-start | bytes 1572868
  46.8 4.0 %copy-start.1 = (bf16[256,8,384]{2,0,1:T(8,128)(2,1)}, bf16[256,8,384]{2,0,1:T(8,128)(2,1)S(1)}, u32[]{:S(2)}) copy-start(bf16[256,8,384]{2,0,1:T(8,128)(2,1)S(1)} %all_to_all.25) | copy-start | bytes 4718596
  47.9 2.9 %collective-permute-start = (bf16[2048,256]{1,0:T(8,128)(2,1)}, bf16[2048,256]{1,0:T(8,128)(2,1)S(1)}, u32[]{:S(2)}, u32[]{:S(2)}) collective-permute-start(bf16[2048,256]{1,0:T(8,128)(2,1)} %slice.4), channel_id=1, source_target_pairs={{0,1},{1,0},{2,3},{3,2},{4,5},{5,4},{6,7},{7,6},{8,9},{9,8},{10,11... | collective-permute-start | bytes 3145736 | tf_op jit(solution)/shard_map/ppermute | solution.py:138
  50.8 1.0 %copy-start.2 = (bf16[2048,256]{1,0:T(8,128)(2,1)}, bf16[2048,256]{1,0:T(8,128)(2,1)S(1)}, u32[]{:S(2)}) copy-start(bf16[2048,256]{1,0:T(8,128)(2,1)S(1)} %collective-permute-done.other_ref) | copy-start | bytes 3145732
  61.3 13.2 %all-to-all-start.1 = ((bf16[8,128,128]{2,1,0:T(8,128)(2,1)}), bf16[8,128,128]{2,1,0:T(8,128)(2,1)S(1)}, u32[]{:S(2)}, u32[]{:S(2)}) async-start(bf16[8,128,128]{2,1,0:T(8,128)(2,1)} %bitcast.36), calls=%async_computation.1 | async-start | bytes 524288 | tf_op jit(solution)/shard_map/all_to_all | solution.py:154

commit v8 on v6

--- a/solution.py
+++ b/solution.py
@@ -9,7 +9,6 @@
 from jax.sharding import PartitionSpec as P
 
 BLOCK = 128
-SUBLANES = 8
 GROUP = 8
 
 
@@ -24,7 +23,6 @@
     table,
     kbuf,
     vbuf,
-    mask,
     sems,
     *,
     inverse_root,
@@ -51,7 +49,13 @@
 
     group = q_ref.shape[0] // BLOCK
     slots = lists_ref.shape[1]
-    key_blocks = table.shape[0] // BLOCK
+    key_blocks = 2 * half_rows // BLOCK
+    zero_block = key_blocks
+
+    @pl.when(step == 0)
+    def _():
+        table[pl.ds(zero_block * BLOCK, BLOCK), :] = jnp.zeros((BLOCK, table.shape[1]), table.dtype)
+
     for g in range(group):
         b = step * group + g
         count = counts_ref[b]
@@ -59,30 +63,30 @@
         for j in range(slots):
             index = jnp.where(j < count, lists_ref[b, j], first)
             index = jnp.minimum(jnp.maximum(index, 0), key_blocks - 1)
+            value_index = jnp.where(j < count, index, zero_block)
             start = pl.multiple_of(index * BLOCK, BLOCK)
+            value_start = pl.multiple_of(value_index * BLOCK, BLOCK)
             kbuf[g, pl.ds(j * BLOCK, BLOCK), :] = table[pl.ds(start, BLOCK), pl.ds(0, head_size)]
             vbuf[g, pl.ds(j * BLOCK, BLOCK), :] = table[
-                pl.ds(start, BLOCK), pl.ds(head_size, head_size)
+                pl.ds(value_start, BLOCK), pl.ds(head_size, head_size)
             ]
-        slot_of = lax.broadcasted_iota(jnp.int32, mask.shape[1:], 1) // BLOCK
-        mask[g] = jnp.where(slot_of < count, 1.0, 0.0).astype(mask.dtype)
 
+    exponent_scale = inverse_root * math.log2(math.e)
     for g in range(group):
         rows = pl.ds(g * BLOCK, BLOCK)
-        logit_scores = (
-            lax.dot_general(
-                q_ref[rows, :],
-                kbuf[g],
-                (((1,), (1,)), ((), ())),
-                preferred_element_type=jnp.float32,
-            )
-            * inverse_root
+        count = counts_ref[step * group + g]
+        raw_scores = lax.dot_general(
+            q_ref[rows, :],
+            kbuf[g],
+            (((1,), (1,)), ((), ())),
+            preferred_element_type=jnp.float32,
         )
-        row_max = jnp.max(logit_scores, axis=1, keepdims=True)
-        weights = jnp.exp(logit_scores - row_max)
-        width = weights.shape[1]
-        weights = (weights.reshape(-1, SUBLANES, width) * mask[g]).reshape(-1, width)
-        row_total = jnp.sum(weights, axis=1, keepdims=True)
+        raw_max = jnp.max(raw_scores, axis=1, keepdims=True)
+        weights = jnp.exp2((raw_scores - raw_max) * exponent_scale)
+        padded = (slots - count).astype(jnp.float32)
+        row_total = jnp.sum(weights, axis=1, keepdims=True) - padded * jnp.sum(
+            weights[:, :BLOCK], axis=1, keepdims=True
+        )
         weighted_sum = jnp.dot(
             weights.astype(jnp.bfloat16), vbuf[g], preferred_element_type=jnp.float32
         )
@@ -107,10 +111,9 @@
         ],
         out_specs=pl.BlockSpec((group * BLOCK, head_size), lambda b, *_: (b, 0)),
         scratch_shapes=[
-            pltpu.VMEM((2 * other.shape[0], 2 * head_size), own.dtype),
+            pltpu.VMEM((2 * other.shape[0] + BLOCK, 2 * head_size), own.dtype),
             pltpu.VMEM((group, slots * BLOCK, head_size), own.dtype),
             pltpu.VMEM((group, slots * BLOCK, head_size), own.dtype),
-            pltpu.VMEM((group, SUBLANES, slots * BLOCK), jnp.float32),
             pltpu.SemaphoreType.DMA((2,)),
         ],
     )

time: 83.8 us -> 82.3 us (0.982)
  Pallas kernels: 14.3 us -> 12.8 us
    pallas_call x1, Pallas kernels: 14.3 us -> 12.8 us  [attend(): pl.pallas_call(kernel, grid_spec=grid_spec, out_shape=jax.ShapeDtypeStruc...]
where the time goes in v8:
time: 82.3 us; the launch traced here: 81.9 us
  blocking collectives  62.5 us (76%)
  Pallas kernels  12.8 us (16%)
  local copies, waits for them, and re-layouts  3.43 us (4%)
  waiting for transfers between devices  2.77 us (3%)
    all_to_all x1, blocking collectives, per_device(): lax.all_to_all(stacked, 'wide', split_axis=1, concat_axis=0, tiled=True)  44.1 us
    all_to_all x1, blocking collectives, per_device(): lax.all_to_all(attended, 'wide', split_axis=0, concat_axis=1, tiled=True)  18.5 us
    pallas_call x1, Pallas kernels, attend(): pl.pallas_call(kernel, grid_spec=grid_spec, out_shape=jax.ShapeDtypeStruc...  12.8 us
    ppermute x1, waiting for transfers between devices, per_device(): other = lax.ppermute(own[:, head_size:], 'narrow', [(0, 1), (1, 0)])  2.77 us
    reshape x2, local copies, waits for them, and re-layouts, per_device(): a.reshape(rows, width, head_size)  2.48 us
  transfers between devices with their start and end apart: 1, of which 1 were waited for; matrix products, arithmetic and copies ran while one was open for 0% of the time, Pallas kernels for 0%

profile of v8, /device:TPU:0, one launch (start us, length us, event | category | flops | bytes accessed | tf_op | source)
XLA Modules:
  0.0 81.9 jit_solution(7676281020944891118)
XLA Ops:
  0.0 0.0 copy-start
  0.0 1.2 %copy_bitcast_fusion.3 = bf16[256,8,128]{2,0,1:T(8,128)(2,1)S(1)} fusion(bf16[256,1024]{1,0:T(8,128)(2,1)} %param.5), kind=kLoop, calls=%fused_computation.4 | loop fusion | bytes 1048576 | tf_op jit(solution)/shard_map/reshape | solution.py:133
  1.2 0.0 copy-done
  1.2 1.3 %copy_bitcast_fusion.1 = (bf16[256,8,128]{2,0,1:T(8,128)(2,1)S(1)}, bf16[256,8,128]{2,0,1:T(8,128)(2,1)S(1)}) fusion(bf16[256,1024]{1,0:T(8,128)(2,1)S(1)} %copy-done, bf16[256,1024]{1,0:T(8,128)(2,1)} %param.7), kind=kLoop, calls=%fused_computation.2 | loop fusion | bytes 2097152 | tf_op jit(solution)/shard_map/reshape | solution.py:133
  2.5 0.2 pad_maximum_fusion
  2.7 44.1 %all_to_all.34 = bf16[256,8,384]{2,0,1:T(8,128)(2,1)S(1)} all-to-all(bf16[256,8,384]{2,0,1:T(8,128)(2,1)S(1)} %pad_maximum_fusion), channel_id=1, replica_groups=mesh['groups'=2,'wide'=8,'narrow'=2] {'wide'}, dimensions={1} | all-to-all | bytes 3145728 | tf_op jit(solution)/shard_map/all_to_all | solution.py:135
  46.8 0.0 copy-start.1
  46.8 0.1 slice.4
  46.9 0.1 collective-permute-start
  47.0 2.8 %collective-permute-done.other_ref = bf16[2048,256]{1,0:T(8,128)(2,1)} collective-permute-done((bf16[2048,256]{1,0:T(8,128)(2,1)S(1)}, bf16[2048,256]{1,0:T(8,128)(2,1)}, u32[]{:S(2)}, u32[]{:S(2)}) %collective-permute-start) | collective-permute-done | bytes 1048608 | tf_op jit(solution)/shard_map/ppermute | solution.py:137
  49.8 0.0 copy-done.1
  49.8 12.8 %shard_map.55 = bf16[2048,128]{1,0:T(8,128)(2,1)} custom-call(s32[16,16]{1,0:T(8,128)} %bitcast.34, s32[16]{0:T(128)} %bitcast.35, s32[1]{0:T(128)} %bitcast.2.narrow_ref, bf16[2048,384]{1,0:T(8,128)(2,1)} %bitcast.31, bf16[2048,384]{1,0:T(8,128)(2,1)} %bitcast.32, bf16[2048,256]{1,0:T(8,128)(2,1)} %collective-permute-done.other_ref), custom_call_target="tpu_custom_call" | custom-call | tf_op jit(solution)/shard_map/pallas_call | solution.py:120
  62.6 18.5 %all_to_all.35 = bf16[8,256,128]{2,1,0:T(8,128)(2,1)S(1)} all-to-all(bf16[8,256,128]{2,1,0:T(8,128)(2,1)} %bitcast.33), channel_id=1, replica_groups=mesh['groups'=2,'wide'=8,'narrow'=2] {'wide'}, dimensions={0} | all-to-all | bytes 1048576 | tf_op jit(solution)/shard_map/all_to_all | solution.py:140
  81.1 0.9 %copy_bitcast_fusion = bf16[256,1024]{1,0:T(8,128)(2,1)} fusion(bf16[8,256,128]{2,1,0:T(8,128)(2,1)S(1)} %all_to_all.35), kind=kLoop, calls=%fused_computation.1 | loop fusion | bytes 1048576 | tf_op jit(solution)/shard_map/all_to_all | solution.py:140
Async XLA Ops:
  0.0 1.2 %copy-start = (bf16[256,1024]{1,0:T(8,128)(2,1)S(1)}, bf16[256,1024]{1,0:T(8,128)(2,1)}, u32[]{:S(2)}) copy-start(bf16[256,1024]{1,0:T(8,128)(2,1)} %param.6) | copy-start | bytes 1572868
  46.8 2.9 %copy-start.1 = (bf16[256,8,384]{2,0,1:T(8,128)(2,1)}, bf16[256,8,384]{2,0,1:T(8,128)(2,1)S(1)}, u32[]{:S(2)}) copy-start(bf16[256,8,384]{2,0,1:T(8,128)(2,1)S(1)} %all_to_all.34) | copy-start | bytes 4718596
  46.9 2.9 %collective-permute-start = (bf16[2048,256]{1,0:T(8,128)(2,1)S(1)}, bf16[2048,256]{1,0:T(8,128)(2,1)}, u32[]{:S(2)}, u32[]{:S(2)}) collective-permute-start(bf16[2048,256]{1,0:T(8,128)(2,1)S(1)} %slice.4), channel_id=1, source_target_pairs={{0,1},{1,0},{2,3},{3,2},{4,5},{5,4},{6,7},{7,6},{8,9},{9,8},{10,11... | collective-permute-start | bytes 3145736 | tf_op jit(solution)/shard_map/ppermute | solution.py:137

commit v9 on v8

--- a/solution.py
+++ b/solution.py
@@ -9,7 +9,7 @@
 from jax.sharding import PartitionSpec as P
 
 BLOCK = 128
-GROUP = 8
+GROUP = 16
 
 
 def attend_kernel(

time: 82.3 us -> 82.3 us (level)
  no operation moved by 1% of the time
where the time goes in v9:
time: 82.3 us; the launch traced here: 81.8 us
  blocking collectives  62.6 us (76%)
  Pallas kernels  12.7 us (15%)
  local copies, waits for them, and re-layouts  3.43 us (4%)
  waiting for transfers between devices  2.77 us (3%)
    all_to_all x1, blocking collectives, per_device(): lax.all_to_all(stacked, 'wide', split_axis=1, concat_axis=0, tiled=True)  44.1 us
    all_to_all x1, blocking collectives, per_device(): lax.all_to_all(attended, 'wide', split_axis=0, concat_axis=1, tiled=True)  18.5 us
    pallas_call x1, Pallas kernels, attend(): pl.pallas_call(kernel, grid_spec=grid_spec, out_shape=jax.ShapeDtypeStruc...  12.7 us
    ppermute x1, waiting for transfers between devices, per_device(): other = lax.ppermute(own[:, head_size:], 'narrow', [(0, 1), (1, 0)])  2.77 us
    reshape x2, local copies, waits for them, and re-layouts, per_device(): a.reshape(rows, width, head_size)  2.48 us
  transfers between devices with their start and end apart: 1, of which 1 were waited for; matrix products, arithmetic and copies ran while one was open for 0% of the time, Pallas kernels for 0%

profile of v9, /device:TPU:0, one launch (start us, length us, event | category | flops | bytes accessed | tf_op | source)
XLA Modules:
  0.0 81.8 jit_solution(16972035942355711502)
XLA Ops:
  0.0 0.0 copy-start
  0.0 1.2 %copy_bitcast_fusion.3 = bf16[256,8,128]{2,0,1:T(8,128)(2,1)S(1)} fusion(bf16[256,1024]{1,0:T(8,128)(2,1)} %param.5), kind=kLoop, calls=%fused_computation.4 | loop fusion | bytes 1048576 | tf_op jit(solution)/shard_map/reshape | solution.py:133
  1.2 0.0 copy-done
  1.2 1.3 %copy_bitcast_fusion.1 = (bf16[256,8,128]{2,0,1:T(8,128)(2,1)S(1)}, bf16[256,8,128]{2,0,1:T(8,128)(2,1)S(1)}) fusion(bf16[256,1024]{1,0:T(8,128)(2,1)S(1)} %copy-done, bf16[256,1024]{1,0:T(8,128)(2,1)} %param.7), kind=kLoop, calls=%fused_computation.2 | loop fusion | bytes 2097152 | tf_op jit(solution)/shard_map/reshape | solution.py:133
  2.5 0.2 pad_maximum_fusion
  2.7 44.1 %all_to_all.34 = bf16[256,8,384]{2,0,1:T(8,128)(2,1)S(1)} all-to-all(bf16[256,8,384]{2,0,1:T(8,128)(2,1)S(1)} %pad_maximum_fusion), channel_id=1, replica_groups=mesh['groups'=2,'wide'=8,'narrow'=2] {'wide'}, dimensions={1} | all-to-all | bytes 3145728 | tf_op jit(solution)/shard_map/all_to_all | solution.py:135
  46.8 0.0 copy-start.1
  46.8 0.1 slice.4
  46.9 0.1 collective-permute-start
  47.0 2.8 %collective-permute-done.other_ref = bf16[2048,256]{1,0:T(8,128)(2,1)} collective-permute-done((bf16[2048,256]{1,0:T(8,128)(2,1)S(1)}, bf16[2048,256]{1,0:T(8,128)(2,1)}, u32[]{:S(2)}, u32[]{:S(2)}) %collective-permute-start) | collective-permute-done | bytes 1048608 | tf_op jit(solution)/shard_map/ppermute | solution.py:137
  49.8 0.0 copy-done.1
  49.8 12.7 %shard_map.55 = bf16[2048,128]{1,0:T(8,128)(2,1)} custom-call(s32[16,16]{1,0:T(8,128)} %bitcast.34, s32[16]{0:T(128)} %bitcast.35, s32[1]{0:T(128)} %bitcast.2.narrow_ref, bf16[2048,384]{1,0:T(8,128)(2,1)} %bitcast.31, bf16[2048,384]{1,0:T(8,128)(2,1)} %bitcast.32, bf16[2048,256]{1,0:T(8,128)(2,1)} %collective-permute-done.other_ref), custom_call_target="tpu_custom_call" | custom-call | tf_op jit(solution)/shard_map/pallas_call | solution.py:120
  62.5 18.5 %all_to_all.35 = bf16[8,256,128]{2,1,0:T(8,128)(2,1)S(1)} all-to-all(bf16[8,256,128]{2,1,0:T(8,128)(2,1)} %bitcast.33), channel_id=1, replica_groups=mesh['groups'=2,'wide'=8,'narrow'=2] {'wide'}, dimensions={0} | all-to-all | bytes 1048576 | tf_op jit(solution)/shard_map/all_to_all | solution.py:140
  81.0 0.9 %copy_bitcast_fusion = bf16[256,1024]{1,0:T(8,128)(2,1)} fusion(bf16[8,256,128]{2,1,0:T(8,128)(2,1)S(1)} %all_to_all.35), kind=kLoop, calls=%fused_computation.1 | loop fusion | bytes 1048576 | tf_op jit(solution)/shard_map/all_to_all | solution.py:140
Async XLA Ops:
  0.0 1.2 %copy-start = (bf16[256,1024]{1,0:T(8,128)(2,1)S(1)}, bf16[256,1024]{1,0:T(8,128)(2,1)}, u32[]{:S(2)}) copy-start(bf16[256,1024]{1,0:T(8,128)(2,1)} %param.6) | copy-start | bytes 1572868
  46.8 2.9 %copy-start.1 = (bf16[256,8,384]{2,0,1:T(8,128)(2,1)}, bf16[256,8,384]{2,0,1:T(8,128)(2,1)S(1)}, u32[]{:S(2)}) copy-start(bf16[256,8,384]{2,0,1:T(8,128)(2,1)S(1)} %all_to_all.34) | copy-start | bytes 4718596
  46.9 2.9 %collective-permute-start = (bf16[2048,256]{1,0:T(8,128)(2,1)S(1)}, bf16[2048,256]{1,0:T(8,128)(2,1)}, u32[]{:S(2)}, u32[]{:S(2)}) collective-permute-start(bf16[2048,256]{1,0:T(8,128)(2,1)S(1)} %slice.4), channel_id=1, source_target_pairs={{0,1},{1,0},{2,3},{3,2},{4,5},{5,4},{6,7},{7,6},{8,9},{9,8},{10,11... | collective-permute-start | bytes 3145736 | tf_op jit(solution)/shard_map/ppermute | solution.py:137

commit v10 on v8

--- a/solution.py
+++ b/solution.py
@@ -21,8 +21,6 @@
     other_ref,
     o_ref,
     table,
-    kbuf,
-    vbuf,
     sems,
     *,
     inverse_root,
@@ -56,40 +54,43 @@
     def _():
         table[pl.ds(zero_block * BLOCK, BLOCK), :] = jnp.zeros((BLOCK, table.shape[1]), table.dtype)
 
+    exponent_scale = inverse_root * math.log2(math.e)
     for g in range(group):
+        rows = pl.ds(g * BLOCK, BLOCK)
         b = step * group + g
         count = counts_ref[b]
         first = lists_ref[b, 0]
+        queries = q_ref[rows, :]
+        value_starts, parts = [], []
         for j in range(slots):
             index = jnp.where(j < count, lists_ref[b, j], first)
             index = jnp.minimum(jnp.maximum(index, 0), key_blocks - 1)
             value_index = jnp.where(j < count, index, zero_block)
             start = pl.multiple_of(index * BLOCK, BLOCK)
-            value_start = pl.multiple_of(value_index * BLOCK, BLOCK)
-            kbuf[g, pl.ds(j * BLOCK, BLOCK), :] = table[pl.ds(start, BLOCK), pl.ds(0, head_size)]
-            vbuf[g, pl.ds(j * BLOCK, BLOCK), :] = table[
-                pl.ds(value_start, BLOCK), pl.ds(head_size, head_size)
-            ]
-
-    exponent_scale = inverse_root * math.log2(math.e)
-    for g in range(group):
-        rows = pl.ds(g * BLOCK, BLOCK)
-        count = counts_ref[step * group + g]
-        raw_scores = lax.dot_general(
-            q_ref[rows, :],
-            kbuf[g],
-            (((1,), (1,)), ((), ())),
-            preferred_element_type=jnp.float32,
-        )
+            value_starts.append(pl.multiple_of(value_index * BLOCK, BLOCK))
+            parts.append(
+                lax.dot_general(
+                    queries,
+                    table[pl.ds(start, BLOCK), pl.ds(0, head_size)],
+                    (((1,), (1,)), ((), ())),
+                    preferred_element_type=jnp.float32,
+                )
+            )
+        raw_scores = jnp.concatenate(parts, axis=1)
         raw_max = jnp.max(raw_scores, axis=1, keepdims=True)
         weights = jnp.exp2((raw_scores - raw_max) * exponent_scale)
         padded = (slots - count).astype(jnp.float32)
         row_total = jnp.sum(weights, axis=1, keepdims=True) - padded * jnp.sum(
             weights[:, :BLOCK], axis=1, keepdims=True
         )
-        weighted_sum = jnp.dot(
-            weights.astype(jnp.bfloat16), vbuf[g], preferred_element_type=jnp.float32
-        )
+        rounded = weights.astype(jnp.bfloat16)
+        weighted_sum = jnp.zeros((BLOCK, head_size), jnp.float32)
+        for j in range(slots):
+            weighted_sum = weighted_sum + jnp.dot(
+                rounded[:, j * BLOCK : (j + 1) * BLOCK],
+                table[pl.ds(value_starts[j], BLOCK), pl.ds(head_size, head_size)],
+                preferred_element_type=jnp.float32,
+            )
         o_ref[rows, :] = (weighted_sum / row_total).astype(o_ref.dtype)
 
 
@@ -112,8 +113,6 @@
         out_specs=pl.BlockSpec((group * BLOCK, head_size), lambda b, *_: (b, 0)),
         scratch_shapes=[
             pltpu.VMEM((2 * other.shape[0] + BLOCK, 2 * head_size), own.dtype),
-            pltpu.VMEM((group, slots * BLOCK, head_size), own.dtype),
-            pltpu.VMEM((group, slots * BLOCK, head_size), own.dtype),
             pltpu.SemaphoreType.DMA((2,)),
         ],
     )

time: 82.3 us -> 84.9 us (1.032)
  Pallas kernels: 12.8 us -> 15.4 us
    pallas_call x1, Pallas kernels: 12.8 us -> 15.4 us  [attend(): pl.pallas_call(kernel, grid_spec=grid_spec, out_shape=jax.ShapeDtypeStruc...]
where the time goes in v10:
time: 84.9 us; the launch traced here: 84.5 us
  blocking collectives  62.6 us (74%)
  Pallas kernels  15.4 us (18%)
  local copies, waits for them, and re-layouts  3.43 us (4%)
  waiting for transfers between devices  2.77 us (3%)
    all_to_all x1, blocking collectives, per_device(): lax.all_to_all(stacked, 'wide', split_axis=1, concat_axis=0, tiled=True)  44.1 us
    all_to_all x1, blocking collectives, per_device(): lax.all_to_all(attended, 'wide', split_axis=0, concat_axis=1, tiled=True)  18.5 us
    pallas_call x1, Pallas kernels, attend(): pl.pallas_call(kernel, grid_spec=grid_spec, out_shape=jax.ShapeDtypeStruc...  15.4 us
    ppermute x1, waiting for transfers between devices, per_device(): other = lax.ppermute(own[:, head_size:], 'narrow', [(0, 1), (1, 0)])  2.77 us
    reshape x2, local copies, waits for them, and re-layouts, per_device(): a.reshape(rows, width, head_size)  2.48 us
  transfers between devices with their start and end apart: 1, of which 1 were waited for; matrix products, arithmetic and copies ran while one was open for 0% of the time, Pallas kernels for 0%

profile of v10, /device:TPU:0, one launch (start us, length us, event | category | flops | bytes accessed | tf_op | source)
XLA Modules:
  0.0 84.5 jit_solution(11163769803968305412)
XLA Ops:
  0.0 0.0 copy-start
  0.0 1.2 %copy_bitcast_fusion.3 = bf16[256,8,128]{2,0,1:T(8,128)(2,1)S(1)} fusion(bf16[256,1024]{1,0:T(8,128)(2,1)} %param.5), kind=kLoop, calls=%fused_computation.4 | loop fusion | bytes 1048576 | tf_op jit(solution)/shard_map/reshape | solution.py:132
  1.2 0.0 copy-done
  1.2 1.3 %copy_bitcast_fusion.1 = (bf16[256,8,128]{2,0,1:T(8,128)(2,1)S(1)}, bf16[256,8,128]{2,0,1:T(8,128)(2,1)S(1)}) fusion(bf16[256,1024]{1,0:T(8,128)(2,1)S(1)} %copy-done, bf16[256,1024]{1,0:T(8,128)(2,1)} %param.7), kind=kLoop, calls=%fused_computation.2 | loop fusion | bytes 2097152 | tf_op jit(solution)/shard_map/reshape | solution.py:132
  2.5 0.2 pad_maximum_fusion
  2.7 44.1 %all_to_all.34 = bf16[256,8,384]{2,0,1:T(8,128)(2,1)S(1)} all-to-all(bf16[256,8,384]{2,0,1:T(8,128)(2,1)S(1)} %pad_maximum_fusion), channel_id=1, replica_groups=mesh['groups'=2,'wide'=8,'narrow'=2] {'wide'}, dimensions={1} | all-to-all | bytes 3145728 | tf_op jit(solution)/shard_map/all_to_all | solution.py:134
  46.8 0.0 copy-start.1
  46.8 0.1 slice.4
  46.9 0.1 collective-permute-start
  47.0 2.8 %collective-permute-done.other_ref = bf16[2048,256]{1,0:T(8,128)(2,1)} collective-permute-done((bf16[2048,256]{1,0:T(8,128)(2,1)S(1)}, bf16[2048,256]{1,0:T(8,128)(2,1)}, u32[]{:S(2)}, u32[]{:S(2)}) %collective-permute-start) | collective-permute-done | bytes 1048608 | tf_op jit(solution)/shard_map/ppermute | solution.py:136
  49.8 0.0 copy-done.1
  49.8 15.4 %shard_map.55 = bf16[2048,128]{1,0:T(8,128)(2,1)} custom-call(s32[16,16]{1,0:T(8,128)} %bitcast.34, s32[16]{0:T(128)} %bitcast.35, s32[1]{0:T(128)} %bitcast.2.narrow_ref, bf16[2048,384]{1,0:T(8,128)(2,1)} %bitcast.31, bf16[2048,384]{1,0:T(8,128)(2,1)} %bitcast.32, bf16[2048,256]{1,0:T(8,128)(2,1)} %collective-permute-done.other_ref), custom_call_target="tpu_custom_call" | custom-call | tf_op jit(solution)/shard_map/pallas_call | solution.py:119
  65.2 18.5 %all_to_all.35 = bf16[8,256,128]{2,1,0:T(8,128)(2,1)S(1)} all-to-all(bf16[8,256,128]{2,1,0:T(8,128)(2,1)} %bitcast.33), channel_id=1, replica_groups=mesh['groups'=2,'wide'=8,'narrow'=2] {'wide'}, dimensions={0} | all-to-all | bytes 1048576 | tf_op jit(solution)/shard_map/all_to_all | solution.py:139
  83.7 0.9 %copy_bitcast_fusion = bf16[256,1024]{1,0:T(8,128)(2,1)} fusion(bf16[8,256,128]{2,1,0:T(8,128)(2,1)S(1)} %all_to_all.35), kind=kLoop, calls=%fused_computation.1 | loop fusion | bytes 1048576 | tf_op jit(solution)/shard_map/all_to_all | solution.py:139
Async XLA Ops:
  0.0 1.2 %copy-start = (bf16[256,1024]{1,0:T(8,128)(2,1)S(1)}, bf16[256,1024]{1,0:T(8,128)(2,1)}, u32[]{:S(2)}) copy-start(bf16[256,1024]{1,0:T(8,128)(2,1)} %param.6) | copy-start | bytes 1572868
  46.8 2.9 %copy-start.1 = (bf16[256,8,384]{2,0,1:T(8,128)(2,1)}, bf16[256,8,384]{2,0,1:T(8,128)(2,1)S(1)}, u32[]{:S(2)}) copy-start(bf16[256,8,384]{2,0,1:T(8,128)(2,1)S(1)} %all_to_all.34) | copy-start | bytes 4718596
  46.9 2.9 %collective-permute-start = (bf16[2048,256]{1,0:T(8,128)(2,1)S(1)}, bf16[2048,256]{1,0:T(8,128)(2,1)}, u32[]{:S(2)}, u32[]{:S(2)}) collective-permute-start(bf16[2048,256]{1,0:T(8,128)(2,1)S(1)} %slice.4), channel_id=1, source_target_pairs={{0,1},{1,0},{2,3},{3,2},{4,5},{5,4},{6,7},{7,6},{8,9},{9,8},{10,11... | collective-permute-start | bytes 3145736 | tf_op jit(solution)/shard_map/ppermute | solution.py:136

commit v11 on v8

--- a/solution.py
+++ b/solution.py
@@ -18,7 +18,8 @@
     narrow_ref,
     q_ref,
     own_ref,
-    other_ref,
+    other_lo_ref,
+    other_hi_ref,
     o_ref,
     table,
     kbuf,
@@ -29,7 +30,8 @@
     head_size,
 ):
     step = pl.program_id(0)
-    half_rows = other_ref.shape[0]
+    half_rows = 2 * other_lo_ref.shape[0]
+    piece = other_lo_ref.shape[0]
     n = narrow_ref[0]
 
     @pl.when(step == 0)
@@ -39,13 +41,18 @@
             table.at[pl.ds(n * half_rows, half_rows), :],
             sems.at[0],
         )
-        other_copy = pltpu.make_async_copy(
-            other_ref, table.at[pl.ds((1 - n) * half_rows, half_rows), :], sems.at[1]
+        lo_copy = pltpu.make_async_copy(
+            other_lo_ref, table.at[pl.ds((1 - n) * half_rows, piece), :], sems.at[1]
+        )
+        hi_copy = pltpu.make_async_copy(
+            other_hi_ref, table.at[pl.ds((1 - n) * half_rows + piece, piece), :], sems.at[2]
         )
         own_copy.start()
-        other_copy.start()
+        lo_copy.start()
+        hi_copy.start()
         own_copy.wait()
-        other_copy.wait()
+        lo_copy.wait()
+        hi_copy.wait()
 
     group = q_ref.shape[0] // BLOCK
     slots = lists_ref.shape[1]
@@ -93,7 +100,7 @@
         o_ref[rows, :] = (weighted_sum / row_total).astype(o_ref.dtype)
 
 
-def attend(own, other, lists, counts, narrow, head_size):
+def attend(own, other_lo, other_hi, lists, counts, narrow, head_size):
     rows = own.shape[0]
     query_blocks = rows // BLOCK
     group = max(g for g in range(1, GROUP + 1) if query_blocks % g == 0)
@@ -108,13 +115,14 @@
             pl.BlockSpec((group * BLOCK, head_size), lambda b, *_: (b, 0)),
             pl.BlockSpec(memory_space=pl.ANY),
             pl.BlockSpec(memory_space=pl.ANY),
+            pl.BlockSpec(memory_space=pl.ANY),
         ],
         out_specs=pl.BlockSpec((group * BLOCK, head_size), lambda b, *_: (b, 0)),
         scratch_shapes=[
-            pltpu.VMEM((2 * other.shape[0] + BLOCK, 2 * head_size), own.dtype),
+            pltpu.VMEM((own.shape[0] * 2 + BLOCK, 2 * head_size), own.dtype),
             pltpu.VMEM((group, slots * BLOCK, head_size), own.dtype),
             pltpu.VMEM((group, slots * BLOCK, head_size), own.dtype),
-            pltpu.SemaphoreType.DMA((2,)),
+            pltpu.SemaphoreType.DMA((3,)),
         ],
     )
     return pl.pallas_call(
@@ -122,7 +130,7 @@
         grid_spec=grid_spec,
         out_shape=jax.ShapeDtypeStruct((rows, head_size), jnp.bfloat16),
         compiler_params=pltpu.CompilerParams(dimension_semantics=("arbitrary",)),
-    )(lists, counts, narrow, own, own, other)
+    )(lists, counts, narrow, own, own, other_lo, other_hi)
 
 
 def per_device(queries, keys, values, block_lists, block_counts):
@@ -134,9 +142,13 @@
     )
     own = lax.all_to_all(stacked, "wide", split_axis=1, concat_axis=0, tiled=True)
     own = own.reshape(rows * width, 3 * head_size)
-    other = lax.ppermute(own[:, head_size:], "narrow", [(0, 1), (1, 0)])
+    piece = own.shape[0] // 2
+    other_lo, other_hi = (
+        lax.ppermute(own[rows_, head_size:], "narrow", [(0, 1), (1, 0)])
+        for rows_ in (slice(0, piece), slice(piece, None))
+    )
     narrow = lax.axis_index("narrow").astype(jnp.int32).reshape(1)
-    attended = attend(own, other, block_lists[0], block_counts[0], narrow, head_size)
+    attended = attend(own, other_lo, other_hi, block_lists[0], block_counts[0], narrow, head_size)
     return lax.all_to_all(attended, "wide", split_axis=0, concat_axis=1, tiled=True)
 
 

time: 82.3 us -> 82.3 us (level)
    ppermute x1 -> x2, waiting for transfers between devices: 2.77 us -> 2.28 us  [per_device(): lax.ppermute(own[rows_, head_size:], 'narrow', [(0, 1), (1, 0)])]
  transfers between devices with their start and end apart: 1 -> 2, of which waited for: 1 -> 2; matrix products, arithmetic and copies ran while one was open for 0% -> 0% of each run, Pallas kernels for 0% -> 0%
where the time goes in v11:
time: 82.3 us; the launch traced here: 81.9 us
  blocking collectives  62.6 us (76%)
  Pallas kernels  12.8 us (16%)
  local copies, waits for them, and re-layouts  3.43 us (4%)
  waiting for transfers between devices  2.28 us (3%)
    all_to_all x1, blocking collectives, per_device(): lax.all_to_all(stacked, 'wide', split_axis=1, concat_axis=0, tiled=True)  44.1 us
    all_to_all x1, blocking collectives, per_device(): lax.all_to_all(attended, 'wide', split_axis=0, concat_axis=1, tiled=True)  18.5 us
    pallas_call x1, Pallas kernels, attend(): pl.pallas_call(kernel, grid_spec=grid_spec, out_shape=jax.ShapeDtypeStruc...  12.8 us
    reshape x2, local copies, waits for them, and re-layouts, per_device(): a.reshape(rows, width, head_size)  2.48 us
    ppermute x2, waiting for transfers between devices, per_device(): lax.ppermute(own[rows_, head_size:], 'narrow', [(0, 1), (1, 0)])  2.28 us
  transfers between devices with their start and end apart: 2, of which 2 were waited for; matrix products, arithmetic and copies ran while one was open for 0% of the time, Pallas kernels for 0%

profile of v11, /device:TPU:0, one launch (start us, length us, event | category | flops | bytes accessed | tf_op | source)
XLA Modules:
  0.0 81.9 jit_solution(12380212231065372139)
XLA Ops:
  0.0 0.0 copy-start
  0.0 1.2 %copy_bitcast_fusion.3 = bf16[256,8,128]{2,0,1:T(8,128)(2,1)S(1)} fusion(bf16[256,1024]{1,0:T(8,128)(2,1)} %param.5), kind=kLoop, calls=%fused_computation.4 | loop fusion | bytes 1048576 | tf_op jit(solution)/shard_map/reshape | solution.py:141
  1.2 0.0 copy-done
  1.2 1.3 %copy_bitcast_fusion.1 = (bf16[256,8,128]{2,0,1:T(8,128)(2,1)S(1)}, bf16[256,8,128]{2,0,1:T(8,128)(2,1)S(1)}) fusion(bf16[256,1024]{1,0:T(8,128)(2,1)S(1)} %copy-done, bf16[256,1024]{1,0:T(8,128)(2,1)} %param.7), kind=kLoop, calls=%fused_computation.2 | loop fusion | bytes 2097152 | tf_op jit(solution)/shard_map/reshape | solution.py:141
  2.5 0.2 pad_maximum_fusion
  2.7 44.1 %all_to_all.34 = bf16[256,8,384]{2,0,1:T(8,128)(2,1)S(1)} all-to-all(bf16[256,8,384]{2,0,1:T(8,128)(2,1)S(1)} %pad_maximum_fusion), channel_id=1, replica_groups=mesh['groups'=2,'wide'=8,'narrow'=2] {'wide'}, dimensions={1} | all-to-all | bytes 3145728 | tf_op jit(solution)/shard_map/all_to_all | solution.py:143
  46.8 0.0 copy-start.1
  46.8 0.1 fusion
  46.9 0.1 collective-permute-start
  47.0 0.5 collective-permute-start.1
  47.5 1.5 %collective-permute-done.other_lo_ref = bf16[1024,256]{1,0:T(8,128)(2,1)} collective-permute-done((bf16[1024,256]{1,0:T(8,128)(2,1)S(1)}, bf16[1024,256]{1,0:T(8,128)(2,1)}, u32[]{:S(2)}, u32[]{:S(2)}) %collective-permute-start) | collective-permute-done | bytes 524320 | tf_op jit(solution)/shard_map/ppermute | solution.py:147
  49.0 0.7 collective-permute-done.1.other_hi_ref
  49.8 0.0 copy-done.1
  49.8 12.8 %shard_map.55 = bf16[2048,128]{1,0:T(8,128)(2,1)} custom-call(s32[16,16]{1,0:T(8,128)} %bitcast.34, s32[16]{0:T(128)} %bitcast.35, s32[1]{0:T(128)} %bitcast.2.narrow_ref, bf16[2048,384]{1,0:T(8,128)(2,1)} %bitcast.31, bf16[2048,384]{1,0:T(8,128)(2,1)} %bitcast.32, bf16[1024,256]{1,0:T(8,128)(2,1)} %collective-permute-done.other_lo_ref, ...), custom_call_target="tpu_custom_call" | custom-call | tf_op jit(solution)/shard_map/pallas_call | solution.py:128
  62.6 18.5 %all_to_all.35 = bf16[8,256,128]{2,1,0:T(8,128)(2,1)S(1)} all-to-all(bf16[8,256,128]{2,1,0:T(8,128)(2,1)} %bitcast.33), channel_id=1, replica_groups=mesh['groups'=2,'wide'=8,'narrow'=2] {'wide'}, dimensions={0} | all-to-all | bytes 1048576 | tf_op jit(solution)/shard_map/all_to_all | solution.py:152
  81.1 0.9 %copy_bitcast_fusion = bf16[256,1024]{1,0:T(8,128)(2,1)} fusion(bf16[8,256,128]{2,1,0:T(8,128)(2,1)S(1)} %all_to_all.35), kind=kLoop, calls=%fused_computation.1 | loop fusion | bytes 1048576 | tf_op jit(solution)/shard_map/all_to_all | solution.py:152
Async XLA Ops:
  0.0 1.2 %copy-start = (bf16[256,1024]{1,0:T(8,128)(2,1)S(1)}, bf16[256,1024]{1,0:T(8,128)(2,1)}, u32[]{:S(2)}) copy-start(bf16[256,1024]{1,0:T(8,128)(2,1)} %param.6) | copy-start | bytes 1572868
  46.8 2.9 %copy-start.1 = (bf16[256,8,384]{2,0,1:T(8,128)(2,1)}, bf16[256,8,384]{2,0,1:T(8,128)(2,1)S(1)}, u32[]{:S(2)}) copy-start(bf16[256,8,384]{2,0,1:T(8,128)(2,1)S(1)} %all_to_all.34) | copy-start | bytes 4718596
  46.9 2.1 %collective-permute-start = (bf16[1024,256]{1,0:T(8,128)(2,1)S(1)}, bf16[1024,256]{1,0:T(8,128)(2,1)}, u32[]{:S(2)}, u32[]{:S(2)}) collective-permute-start(bf16[1024,256]{1,0:T(8,128)(2,1)S(1)} %get-tuple-element.6), channel_id=1, source_target_pairs={{0,1},{1,0},{2,3},{3,2},{4,5},{5,4},{6,7},{7,6},{8,9},{9,8},{10,11... | collective-permute-start | bytes 1572872 | tf_op jit(solution)/shard_map/ppermute | solution.py:147
  47.0 2.8 %collective-permute-start.1 = (bf16[1024,256]{1,0:T(8,128)(2,1)S(1)}, bf16[1024,256]{1,0:T(8,128)(2,1)}, u32[]{:S(2)}, u32[]{:S(2)}) collective-permute-start(bf16[1024,256]{1,0:T(8,128)(2,1)S(1)} %get-tuple-element.5), channel_id=1, source_target_pairs={{0,1},{1,0},{2,3},{3,2},{4,5},{5,4},{6,7},{7,6},{8,9},{9,8},{10,11... | collective-permute-start | bytes 1572872 | tf_op jit(solution)/shard_map/ppermute | solution.py:147

commit v12 on v8

--- a/solution.py
+++ b/solution.py
@@ -32,21 +32,6 @@
     half_rows = other_ref.shape[0]
     n = narrow_ref[0]
 
-    @pl.when(step == 0)
-    def _():
-        own_copy = pltpu.make_async_copy(
-            own_ref.at[:, pl.ds(head_size, 2 * head_size)],
-            table.at[pl.ds(n * half_rows, half_rows), :],
-            sems.at[0],
-        )
-        other_copy = pltpu.make_async_copy(
-            other_ref, table.at[pl.ds((1 - n) * half_rows, half_rows), :], sems.at[1]
-        )
-        own_copy.start()
-        other_copy.start()
-        own_copy.wait()
-        other_copy.wait()
-
     group = q_ref.shape[0] // BLOCK
     slots = lists_ref.shape[1]
     key_blocks = 2 * half_rows // BLOCK
@@ -56,6 +41,27 @@
     def _():
         table[pl.ds(zero_block * BLOCK, BLOCK), :] = jnp.zeros((BLOCK, table.shape[1]), table.dtype)
 
+    def table_copies(part):
+        own_copy = pltpu.make_async_copy(
+            own_ref.at[:, pl.ds((1 + part) * head_size, head_size)],
+            table.at[pl.ds(n * half_rows, half_rows), pl.ds(part * head_size, head_size)],
+            sems.at[2 * part],
+        )
+        other_copy = pltpu.make_async_copy(
+            other_ref.at[:, pl.ds(part * head_size, head_size)],
+            table.at[pl.ds((1 - n) * half_rows, half_rows), pl.ds(part * head_size, head_size)],
+            sems.at[2 * part + 1],
+        )
+        return own_copy, other_copy
+
+    @pl.when(step == 0)
+    def _():
+        for copy in table_copies(0) + table_copies(1):
+            copy.start()
+        for copy in table_copies(0):
+            copy.wait()
+
+    starts = []
     for g in range(group):
         b = step * group + g
         count = counts_ref[b]
@@ -65,10 +71,18 @@
             index = jnp.minimum(jnp.maximum(index, 0), key_blocks - 1)
             value_index = jnp.where(j < count, index, zero_block)
             start = pl.multiple_of(index * BLOCK, BLOCK)
-            value_start = pl.multiple_of(value_index * BLOCK, BLOCK)
+            starts.append(pl.multiple_of(value_index * BLOCK, BLOCK))
             kbuf[g, pl.ds(j * BLOCK, BLOCK), :] = table[pl.ds(start, BLOCK), pl.ds(0, head_size)]
+
+    @pl.when(step == 0)
+    def _():
+        for copy in table_copies(1):
+            copy.wait()
+
+    for g in range(group):
+        for j in range(slots):
             vbuf[g, pl.ds(j * BLOCK, BLOCK), :] = table[
-                pl.ds(value_start, BLOCK), pl.ds(head_size, head_size)
+                pl.ds(starts[g * slots + j], BLOCK), pl.ds(head_size, head_size)
             ]
 
     exponent_scale = inverse_root * math.log2(math.e)
@@ -114,7 +128,7 @@
             pltpu.VMEM((2 * other.shape[0] + BLOCK, 2 * head_size), own.dtype),
             pltpu.VMEM((group, slots * BLOCK, head_size), own.dtype),
             pltpu.VMEM((group, slots * BLOCK, head_size), own.dtype),
-            pltpu.SemaphoreType.DMA((2,)),
+            pltpu.SemaphoreType.DMA((4,)),
         ],
     )
     return pl.pallas_call(
@@ -129,8 +143,11 @@
     rows = queries.shape[0]
     width = lax.axis_size("wide")
     head_size = queries.shape[1] // width
-    stacked = jnp.concatenate(
-        [a.reshape(rows, width, head_size) for a in (queries, keys, values)], axis=2
+    stacked = (
+        jnp.concatenate([queries, keys, values], axis=1)
+        .reshape(rows, 3, width, head_size)
+        .transpose(0, 2, 1, 3)
+        .reshape(rows, width, 3 * head_size)
     )
     own = lax.all_to_all(stacked, "wide", split_axis=1, concat_axis=0, tiled=True)
     own = own.reshape(rows * width, 3 * head_size)

time: 82.3 us -> 83 us (level)
  local copies, waits for them, and re-layouts: 3.43 us -> 1.46 us
  Pallas kernels: 12.8 us -> 14.3 us
  other arithmetic: 0.22 us -> 1.46 us
    reshape x2 -> x1, local copies, waits for them, and re-layouts: 2.48 us -> 0.2 us  [per_device(): stacked = jnp.concatenate([queries, keys, values], axis=1).reshape(rows,...]
    unnamed x0 -> x1, other arithmetic: none -> 1.46 us
    pallas_call x1, Pallas kernels: 12.8 us -> 14.3 us  [attend(): pl.pallas_call(kernel, grid_spec=grid_spec, out_shape=jax.ShapeDtypeStruc...]
where the time goes in v12:
time: 83 us; the launch traced here: 82.6 us
  blocking collectives  62.6 us (75%)
  Pallas kernels  14.3 us (17%)
  waiting for transfers between devices  2.77 us (3%)
  other arithmetic  1.46 us (2%)
  local copies, waits for them, and re-layouts  1.46 us (2%)
    all_to_all x1, blocking collectives, per_device(): lax.all_to_all(stacked, 'wide', split_axis=1, concat_axis=0, tiled=True)  44.1 us
    all_to_all x1, blocking collectives, per_device(): lax.all_to_all(attended, 'wide', split_axis=0, concat_axis=1, tiled=True)  18.5 us
    pallas_call x1, Pallas kernels, attend(): pl.pallas_call(kernel, grid_spec=grid_spec, out_shape=jax.ShapeDtypeStruc...  14.3 us
    ppermute x1, waiting for transfers between devices, per_device(): other = lax.ppermute(own[:, head_size:], 'narrow', [(0, 1), (1, 0)])  2.77 us
  transfers between devices with their start and end apart: 1, of which 1 were waited for; matrix products, arithmetic and copies ran while one was open for 0% of the time, Pallas kernels for 0%

profile of v12, /device:TPU:0, one launch (start us, length us, event | category | flops | bytes accessed | tf_op | source)
XLA Modules:
  0.0 82.6 jit_solution(12840929921757281887)
XLA Ops:
  0.0 1.5 %maximum_bitcast_fusion = bf16[32,8,24,128]{3,1,2,0:T(8,128)(2,1)S(1)} fusion(bf16[256,1024]{1,0:T(8,128)(2,1)} %param.7, bf16[256,1024]{1,0:T(8,128)(2,1)} %param.6, bf16[256,1024]{1,0:T(8,128)(2,1)} %param.5), kind=kLoop, calls=%fused_computation | loop fusion | flops 4718592 | bytes 3145728
  1.5 0.3 copy.13
  1.8 0.2 copy.10
  2.0 44.1 %all_to_all.34 = bf16[256,8,384]{2,0,1:T(8,128)(2,1)S(1)} all-to-all(bf16[256,8,384]{2,0,1:T(8,128)(2,1)S(1)} %copy.10), channel_id=1, replica_groups=mesh['groups'=2,'wide'=8,'narrow'=2] {'wide'}, dimensions={1} | all-to-all | bytes 3145728 | tf_op jit(solution)/shard_map/all_to_all | solution.py:152
  46.1 0.0 copy-start
  46.1 0.1 slice.4
  46.2 0.1 collective-permute-start
  46.2 2.8 %collective-permute-done.other_ref = bf16[2048,256]{1,0:T(8,128)(2,1)} collective-permute-done((bf16[2048,256]{1,0:T(8,128)(2,1)S(1)}, bf16[2048,256]{1,0:T(8,128)(2,1)}, u32[]{:S(2)}, u32[]{:S(2)}) %collective-permute-start) | collective-permute-done | bytes 1048608 | tf_op jit(solution)/shard_map/ppermute | solution.py:154
  49.0 0.0 copy-done
  49.0 14.3 %shard_map.55 = bf16[2048,128]{1,0:T(8,128)(2,1)} custom-call(s32[16,16]{1,0:T(8,128)} %bitcast.28, s32[16]{0:T(128)} %bitcast.29, s32[1]{0:T(128)} %bitcast.2.narrow_ref, bf16[2048,384]{1,0:T(8,128)(2,1)} %bitcast.24, bf16[2048,384]{1,0:T(8,128)(2,1)} %bitcast.25, bf16[2048,256]{1,0:T(8,128)(2,1)} %collective-permute-done.other_ref), custom_call_target="tpu_custom_call" | custom-call | tf_op jit(solution)/shard_map/pallas_call | solution.py:134
  63.3 18.5 %all_to_all.35 = bf16[8,256,128]{2,1,0:T(8,128)(2,1)S(1)} all-to-all(bf16[8,256,128]{2,1,0:T(8,128)(2,1)} %bitcast.27), channel_id=1, replica_groups=mesh['groups'=2,'wide'=8,'narrow'=2] {'wide'}, dimensions={0} | all-to-all | bytes 1048576 | tf_op jit(solution)/shard_map/all_to_all | solution.py:157
  81.8 0.9 %copy_bitcast_fusion = bf16[256,1024]{1,0:T(8,128)(2,1)} fusion(bf16[8,256,128]{2,1,0:T(8,128)(2,1)S(1)} %all_to_all.35), kind=kLoop, calls=%fused_computation.1 | loop fusion | bytes 1048576 | tf_op jit(solution)/shard_map/all_to_all | solution.py:157
Async XLA Ops:
  46.1 2.9 %copy-start = (bf16[256,8,384]{2,0,1:T(8,128)(2,1)}, bf16[256,8,384]{2,0,1:T(8,128)(2,1)S(1)}, u32[]{:S(2)}) copy-start(bf16[256,8,384]{2,0,1:T(8,128)(2,1)S(1)} %all_to_all.34) | copy-start | bytes 4718596
  46.2 2.9 %collective-permute-start = (bf16[2048,256]{1,0:T(8,128)(2,1)S(1)}, bf16[2048,256]{1,0:T(8,128)(2,1)}, u32[]{:S(2)}, u32[]{:S(2)}) collective-permute-start(bf16[2048,256]{1,0:T(8,128)(2,1)S(1)} %slice.4), channel_id=1, source_target_pairs={{0,1},{1,0},{2,3},{3,2},{4,5},{5,4},{6,7},{7,6},{8,9},{9,8},{10,11... | collective-permute-start | bytes 3145736 | tf_op jit(solution)/shard_map/ppermute | solution.py:154

commit v13 on v8

--- a/solution.py
+++ b/solution.py
@@ -129,8 +129,11 @@
     rows = queries.shape[0]
     width = lax.axis_size("wide")
     head_size = queries.shape[1] // width
-    stacked = jnp.concatenate(
-        [a.reshape(rows, width, head_size) for a in (queries, keys, values)], axis=2
+    stacked = (
+        jnp.concatenate([queries, keys, values], axis=1)
+        .reshape(rows, 3, width, head_size)
+        .transpose(0, 2, 1, 3)
+        .reshape(rows, width, 3 * head_size)
     )
     own = lax.all_to_all(stacked, "wide", split_axis=1, concat_axis=0, tiled=True)
     own = own.reshape(rows * width, 3 * head_size)

time: 82.3 us -> 81.6 us (level)
  local copies, waits for them, and re-layouts: 3.43 us -> 1.46 us
  other arithmetic: 0.22 us -> 1.46 us
    reshape x2 -> x1, local copies, waits for them, and re-layouts: 2.48 us -> 0.2 us  [per_device(): stacked = jnp.concatenate([queries, keys, values], axis=1).reshape(rows,...]
    unnamed x0 -> x1, other arithmetic: none -> 1.46 us
where the time goes in v13:
time: 81.6 us; the launch traced here: 81.2 us
  blocking collectives  62.6 us (77%)
  Pallas kernels  12.8 us (16%)
  waiting for transfers between devices  2.77 us (3%)
  other arithmetic  1.46 us (2%)
  local copies, waits for them, and re-layouts  1.46 us (2%)
    all_to_all x1, blocking collectives, per_device(): lax.all_to_all(stacked, 'wide', split_axis=1, concat_axis=0, tiled=True)  44.1 us
    all_to_all x1, blocking collectives, per_device(): lax.all_to_all(attended, 'wide', split_axis=0, concat_axis=1, tiled=True)  18.5 us
    pallas_call x1, Pallas kernels, attend(): pl.pallas_call(kernel, grid_spec=grid_spec, out_shape=jax.ShapeDtypeStruc...  12.8 us
    ppermute x1, waiting for transfers between devices, per_device(): other = lax.ppermute(own[:, head_size:], 'narrow', [(0, 1), (1, 0)])  2.77 us
  transfers between devices with their start and end apart: 1, of which 1 were waited for; matrix products, arithmetic and copies ran while one was open for 0% of the time, Pallas kernels for 0%

profile of v13, /device:TPU:0, one launch (start us, length us, event | category | flops | bytes accessed | tf_op | source)
XLA Modules:
  0.0 81.2 jit_solution(10289336988360467266)
XLA Ops:
  0.0 1.5 %maximum_bitcast_fusion = bf16[32,8,24,128]{3,1,2,0:T(8,128)(2,1)S(1)} fusion(bf16[256,1024]{1,0:T(8,128)(2,1)} %param.7, bf16[256,1024]{1,0:T(8,128)(2,1)} %param.6, bf16[256,1024]{1,0:T(8,128)(2,1)} %param.5), kind=kLoop, calls=%fused_computation | loop fusion | flops 4718592 | bytes 3145728
  1.5 0.3 copy.13
  1.8 0.2 copy.10
  2.0 44.1 %all_to_all.34 = bf16[256,8,384]{2,0,1:T(8,128)(2,1)S(1)} all-to-all(bf16[256,8,384]{2,0,1:T(8,128)(2,1)S(1)} %copy.10), channel_id=1, replica_groups=mesh['groups'=2,'wide'=8,'narrow'=2] {'wide'}, dimensions={1} | all-to-all | bytes 3145728 | tf_op jit(solution)/shard_map/all_to_all | solution.py:138
  46.1 0.0 copy-start
  46.1 0.1 slice.4
  46.2 0.1 collective-permute-start
  46.2 2.8 %collective-permute-done.other_ref = bf16[2048,256]{1,0:T(8,128)(2,1)} collective-permute-done((bf16[2048,256]{1,0:T(8,128)(2,1)S(1)}, bf16[2048,256]{1,0:T(8,128)(2,1)}, u32[]{:S(2)}, u32[]{:S(2)}) %collective-permute-start) | collective-permute-done | bytes 1048608 | tf_op jit(solution)/shard_map/ppermute | solution.py:140
  49.0 0.0 copy-done
  49.0 12.8 %shard_map.55 = bf16[2048,128]{1,0:T(8,128)(2,1)} custom-call(s32[16,16]{1,0:T(8,128)} %bitcast.28, s32[16]{0:T(128)} %bitcast.29, s32[1]{0:T(128)} %bitcast.2.narrow_ref, bf16[2048,384]{1,0:T(8,128)(2,1)} %bitcast.24, bf16[2048,384]{1,0:T(8,128)(2,1)} %bitcast.25, bf16[2048,256]{1,0:T(8,128)(2,1)} %collective-permute-done.other_ref), custom_call_target="tpu_custom_call" | custom-call | tf_op jit(solution)/shard_map/pallas_call | solution.py:120
  61.9 18.5 %all_to_all.35 = bf16[8,256,128]{2,1,0:T(8,128)(2,1)S(1)} all-to-all(bf16[8,256,128]{2,1,0:T(8,128)(2,1)} %bitcast.27), channel_id=1, replica_groups=mesh['groups'=2,'wide'=8,'narrow'=2] {'wide'}, dimensions={0} | all-to-all | bytes 1048576 | tf_op jit(solution)/shard_map/all_to_all | solution.py:143
  80.3 0.9 %copy_bitcast_fusion = bf16[256,1024]{1,0:T(8,128)(2,1)} fusion(bf16[8,256,128]{2,1,0:T(8,128)(2,1)S(1)} %all_to_all.35), kind=kLoop, calls=%fused_computation.1 | loop fusion | bytes 1048576 | tf_op jit(solution)/shard_map/all_to_all | solution.py:143
Async XLA Ops:
  46.1 2.9 %copy-start = (bf16[256,8,384]{2,0,1:T(8,128)(2,1)}, bf16[256,8,384]{2,0,1:T(8,128)(2,1)S(1)}, u32[]{:S(2)}) copy-start(bf16[256,8,384]{2,0,1:T(8,128)(2,1)S(1)} %all_to_all.34) | copy-start | bytes 4718596
  46.2 2.9 %collective-permute-start = (bf16[2048,256]{1,0:T(8,128)(2,1)S(1)}, bf16[2048,256]{1,0:T(8,128)(2,1)}, u32[]{:S(2)}, u32[]{:S(2)}) collective-permute-start(bf16[2048,256]{1,0:T(8,128)(2,1)S(1)} %slice.4), channel_id=1, source_target_pairs={{0,1},{1,0},{2,3},{3,2},{4,5},{5,4},{6,7},{7,6},{8,9},{9,8},{10,11... | collective-permute-start | bytes 3145736 | tf_op jit(solution)/shard_map/ppermute | solution.py:140

commit v14 on v13

--- a/solution.py
+++ b/solution.py
@@ -9,7 +9,7 @@
 from jax.sharding import PartitionSpec as P
 
 BLOCK = 128
-GROUP = 8
+GROUP = 16
 
 
 def attend_kernel(

time: 81.6 us -> 81.5 us (level)
  no operation moved by 1% of the time
where the time goes in v14:
time: 81.5 us; the launch traced here: 81.1 us
  blocking collectives  62.6 us (77%)
  Pallas kernels  12.7 us (16%)
  waiting for transfers between devices  2.77 us (3%)
  other arithmetic  1.46 us (2%)
  local copies, waits for them, and re-layouts  1.46 us (2%)
    all_to_all x1, blocking collectives, per_device(): lax.all_to_all(stacked, 'wide', split_axis=1, concat_axis=0, tiled=True)  44.1 us
    all_to_all x1, blocking collectives, per_device(): lax.all_to_all(attended, 'wide', split_axis=0, concat_axis=1, tiled=True)  18.5 us
    pallas_call x1, Pallas kernels, attend(): pl.pallas_call(kernel, grid_spec=grid_spec, out_shape=jax.ShapeDtypeStruc...  12.7 us
    ppermute x1, waiting for transfers between devices, per_device(): other = lax.ppermute(own[:, head_size:], 'narrow', [(0, 1), (1, 0)])  2.77 us
  transfers between devices with their start and end apart: 1, of which 1 were waited for; matrix products, arithmetic and copies ran while one was open for 0% of the time, Pallas kernels for 0%

profile of v14, /device:TPU:0, one launch (start us, length us, event | category | flops | bytes accessed | tf_op | source)
XLA Modules:
  0.0 81.1 jit_solution(1441400807710131600)
XLA Ops:
  0.0 1.5 %maximum_bitcast_fusion = bf16[32,8,24,128]{3,1,2,0:T(8,128)(2,1)S(1)} fusion(bf16[256,1024]{1,0:T(8,128)(2,1)} %param.7, bf16[256,1024]{1,0:T(8,128)(2,1)} %param.6, bf16[256,1024]{1,0:T(8,128)(2,1)} %param.5), kind=kLoop, calls=%fused_computation | loop fusion | flops 4718592 | bytes 3145728
  1.5 0.3 copy.13
  1.8 0.2 copy.10
  2.0 44.1 %all_to_all.34 = bf16[256,8,384]{2,0,1:T(8,128)(2,1)S(1)} all-to-all(bf16[256,8,384]{2,0,1:T(8,128)(2,1)S(1)} %copy.10), channel_id=1, replica_groups=mesh['groups'=2,'wide'=8,'narrow'=2] {'wide'}, dimensions={1} | all-to-all | bytes 3145728 | tf_op jit(solution)/shard_map/all_to_all | solution.py:138
  46.1 0.0 copy-start
  46.1 0.1 slice.4
  46.2 0.1 collective-permute-start
  46.2 2.8 %collective-permute-done.other_ref = bf16[2048,256]{1,0:T(8,128)(2,1)} collective-permute-done((bf16[2048,256]{1,0:T(8,128)(2,1)S(1)}, bf16[2048,256]{1,0:T(8,128)(2,1)}, u32[]{:S(2)}, u32[]{:S(2)}) %collective-permute-start) | collective-permute-done | bytes 1048608 | tf_op jit(solution)/shard_map/ppermute | solution.py:140
  49.0 0.0 copy-done
  49.0 12.7 %shard_map.55 = bf16[2048,128]{1,0:T(8,128)(2,1)} custom-call(s32[16,16]{1,0:T(8,128)} %bitcast.28, s32[16]{0:T(128)} %bitcast.29, s32[1]{0:T(128)} %bitcast.2.narrow_ref, bf16[2048,384]{1,0:T(8,128)(2,1)} %bitcast.24, bf16[2048,384]{1,0:T(8,128)(2,1)} %bitcast.25, bf16[2048,256]{1,0:T(8,128)(2,1)} %collective-permute-done.other_ref), custom_call_target="tpu_custom_call" | custom-call | tf_op jit(solution)/shard_map/pallas_call | solution.py:120
  61.7 18.5 %all_to_all.35 = bf16[8,256,128]{2,1,0:T(8,128)(2,1)S(1)} all-to-all(bf16[8,256,128]{2,1,0:T(8,128)(2,1)} %bitcast.27), channel_id=1, replica_groups=mesh['groups'=2,'wide'=8,'narrow'=2] {'wide'}, dimensions={0} | all-to-all | bytes 1048576 | tf_op jit(solution)/shard_map/all_to_all | solution.py:143
  80.2 0.9 %copy_bitcast_fusion = bf16[256,1024]{1,0:T(8,128)(2,1)} fusion(bf16[8,256,128]{2,1,0:T(8,128)(2,1)S(1)} %all_to_all.35), kind=kLoop, calls=%fused_computation.1 | loop fusion | bytes 1048576 | tf_op jit(solution)/shard_map/all_to_all | solution.py:143
Async XLA Ops:
  46.1 2.9 %copy-start = (bf16[256,8,384]{2,0,1:T(8,128)(2,1)}, bf16[256,8,384]{2,0,1:T(8,128)(2,1)S(1)}, u32[]{:S(2)}) copy-start(bf16[256,8,384]{2,0,1:T(8,128)(2,1)S(1)} %all_to_all.34) | copy-start | bytes 4718596
  46.2 2.9 %collective-permute-start = (bf16[2048,256]{1,0:T(8,128)(2,1)S(1)}, bf16[2048,256]{1,0:T(8,128)(2,1)}, u32[]{:S(2)}, u32[]{:S(2)}) collective-permute-start(bf16[2048,256]{1,0:T(8,128)(2,1)S(1)} %slice.4), channel_id=1, source_target_pairs={{0,1},{1,0},{2,3},{3,2},{4,5},{5,4},{6,7},{7,6},{8,9},{9,8},{10,11... | collective-permute-start | bytes 3145736 | tf_op jit(solution)/shard_map/ppermute | solution.py:140

commit v15 on v14

--- a/solution.py
+++ b/solution.py
@@ -21,6 +21,7 @@
     other_ref,
     o_ref,
     table,
+    qbuf,
     kbuf,
     vbuf,
     sems,
@@ -31,6 +32,13 @@
     step = pl.program_id(0)
     half_rows = other_ref.shape[0]
     n = narrow_ref[0]
+    query_rows = qbuf.shape[0]
+    query_copy = pltpu.make_async_copy(
+        q_ref.at[pl.ds(pl.multiple_of(step * query_rows, BLOCK), query_rows), pl.ds(0, head_size)],
+        qbuf,
+        sems.at[2],
+    )
+    query_copy.start()
 
     @pl.when(step == 0)
     def _():
@@ -47,7 +55,9 @@
         own_copy.wait()
         other_copy.wait()
 
-    group = q_ref.shape[0] // BLOCK
+    query_copy.wait()
+
+    group = qbuf.shape[0] // BLOCK
     slots = lists_ref.shape[1]
     key_blocks = 2 * half_rows // BLOCK
     zero_block = key_blocks
@@ -76,7 +86,7 @@
         rows = pl.ds(g * BLOCK, BLOCK)
         count = counts_ref[step * group + g]
         raw_scores = lax.dot_general(
-            q_ref[rows, :],
+            qbuf[rows, :],
             kbuf[g],
             (((1,), (1,)), ((), ())),
             preferred_element_type=jnp.float32,
@@ -105,16 +115,17 @@
         num_scalar_prefetch=3,
         grid=(query_blocks // group,),
         in_specs=[
-            pl.BlockSpec((group * BLOCK, head_size), lambda b, *_: (b, 0)),
+            pl.BlockSpec(memory_space=pl.ANY),
             pl.BlockSpec(memory_space=pl.ANY),
             pl.BlockSpec(memory_space=pl.ANY),
         ],
         out_specs=pl.BlockSpec((group * BLOCK, head_size), lambda b, *_: (b, 0)),
         scratch_shapes=[
             pltpu.VMEM((2 * other.shape[0] + BLOCK, 2 * head_size), own.dtype),
+            pltpu.VMEM((group * BLOCK, head_size), own.dtype),
             pltpu.VMEM((group, slots * BLOCK, head_size), own.dtype),
             pltpu.VMEM((group, slots * BLOCK, head_size), own.dtype),
-            pltpu.SemaphoreType.DMA((2,)),
+            pltpu.SemaphoreType.DMA((3,)),
         ],
     )
     return pl.pallas_call(

time: 81.5 us -> 80.6 us (0.989)
  no operation moved by 1% of the time
where the time goes in v15:
time: 80.6 us; the launch traced here: 80.3 us
  blocking collectives  62.6 us (78%)
  Pallas kernels  11.9 us (15%)
  waiting for transfers between devices  2.77 us (3%)
  other arithmetic  1.46 us (2%)
  local copies, waits for them, and re-layouts  1.46 us (2%)
    all_to_all x1, blocking collectives, per_device(): lax.all_to_all(stacked, 'wide', split_axis=1, concat_axis=0, tiled=True)  44.1 us
    all_to_all x1, blocking collectives, per_device(): lax.all_to_all(attended, 'wide', split_axis=0, concat_axis=1, tiled=True)  18.5 us
    pallas_call x1, Pallas kernels, attend(): pl.pallas_call(kernel, grid_spec=grid_spec, out_shape=jax.ShapeDtypeStruc...  11.9 us
    ppermute x1, waiting for transfers between devices, per_device(): other = lax.ppermute(own[:, head_size:], 'narrow', [(0, 1), (1, 0)])  2.77 us
  transfers between devices with their start and end apart: 1, of which 1 were waited for; matrix products, arithmetic and copies ran while one was open for 0% of the time, Pallas kernels for 0%

profile of v15, /device:TPU:0, one launch (start us, length us, event | category | flops | bytes accessed | tf_op | source)
XLA Modules:
  0.0 80.3 jit_solution(15874085042931377809)
XLA Ops:
  0.0 1.5 %maximum_bitcast_fusion = bf16[32,8,24,128]{3,1,2,0:T(8,128)(2,1)S(1)} fusion(bf16[256,1024]{1,0:T(8,128)(2,1)} %param.7, bf16[256,1024]{1,0:T(8,128)(2,1)} %param.6, bf16[256,1024]{1,0:T(8,128)(2,1)} %param.5), kind=kLoop, calls=%fused_computation | loop fusion | flops 4718592 | bytes 3145728
  1.5 0.3 copy.13
  1.8 0.2 copy.10
  2.0 44.1 %all_to_all.34 = bf16[256,8,384]{2,0,1:T(8,128)(2,1)S(1)} all-to-all(bf16[256,8,384]{2,0,1:T(8,128)(2,1)S(1)} %copy.10), channel_id=1, replica_groups=mesh['groups'=2,'wide'=8,'narrow'=2] {'wide'}, dimensions={1} | all-to-all | bytes 3145728 | tf_op jit(solution)/shard_map/all_to_all | solution.py:149
  46.1 0.0 copy-start
  46.1 0.1 slice.4
  46.2 0.1 collective-permute-start
  46.2 2.8 %collective-permute-done.other_ref = bf16[2048,256]{1,0:T(8,128)(2,1)} collective-permute-done((bf16[2048,256]{1,0:T(8,128)(2,1)S(1)}, bf16[2048,256]{1,0:T(8,128)(2,1)}, u32[]{:S(2)}, u32[]{:S(2)}) %collective-permute-start) | collective-permute-done | bytes 1048608 | tf_op jit(solution)/shard_map/ppermute | solution.py:151
  49.0 0.0 copy-done
  49.0 11.9 %shard_map.55 = bf16[2048,128]{1,0:T(8,128)(2,1)} custom-call(s32[16,16]{1,0:T(8,128)} %bitcast.28, s32[16]{0:T(128)} %bitcast.29, s32[1]{0:T(128)} %bitcast.2.narrow_ref, bf16[2048,384]{1,0:T(8,128)(2,1)} %bitcast.24, bf16[2048,384]{1,0:T(8,128)(2,1)} %bitcast.25, bf16[2048,256]{1,0:T(8,128)(2,1)} %collective-permute-done.other_ref), custom_call_target="tpu_custom_call" | custom-call | tf_op jit(solution)/shard_map/pallas_call | solution.py:131
  60.9 18.5 %all_to_all.35 = bf16[8,256,128]{2,1,0:T(8,128)(2,1)S(1)} all-to-all(bf16[8,256,128]{2,1,0:T(8,128)(2,1)} %bitcast.27), channel_id=1, replica_groups=mesh['groups'=2,'wide'=8,'narrow'=2] {'wide'}, dimensions={0} | all-to-all | bytes 1048576 | tf_op jit(solution)/shard_map/all_to_all | solution.py:154
  79.4 0.9 %copy_bitcast_fusion = bf16[256,1024]{1,0:T(8,128)(2,1)} fusion(bf16[8,256,128]{2,1,0:T(8,128)(2,1)S(1)} %all_to_all.35), kind=kLoop, calls=%fused_computation.1 | loop fusion | bytes 1048576 | tf_op jit(solution)/shard_map/all_to_all | solution.py:154
Async XLA Ops:
  46.1 2.9 %copy-start = (bf16[256,8,384]{2,0,1:T(8,128)(2,1)}, bf16[256,8,384]{2,0,1:T(8,128)(2,1)S(1)}, u32[]{:S(2)}) copy-start(bf16[256,8,384]{2,0,1:T(8,128)(2,1)S(1)} %all_to_all.34) | copy-start | bytes 4718596
  46.2 2.9 %collective-permute-start = (bf16[2048,256]{1,0:T(8,128)(2,1)S(1)}, bf16[2048,256]{1,0:T(8,128)(2,1)}, u32[]{:S(2)}, u32[]{:S(2)}) collective-permute-start(bf16[2048,256]{1,0:T(8,128)(2,1)S(1)} %slice.4), channel_id=1, source_target_pairs={{0,1},{1,0},{2,3},{3,2},{4,5},{5,4},{6,7},{7,6},{8,9},{9,8},{10,11... | collective-permute-start | bytes 3145736 | tf_op jit(solution)/shard_map/ppermute | solution.py:151

commit v16 on v15

--- a/solution.py
+++ b/solution.py
@@ -22,6 +22,7 @@
     o_ref,
     table,
     qbuf,
+    obuf,
     kbuf,
     vbuf,
     sems,
@@ -82,6 +83,7 @@
             ]
 
     exponent_scale = inverse_root * math.log2(math.e)
+    out_copies = []
     for g in range(group):
         rows = pl.ds(g * BLOCK, BLOCK)
         count = counts_ref[step * group + g]
@@ -100,7 +102,16 @@
         weighted_sum = jnp.dot(
             weights.astype(jnp.bfloat16), vbuf[g], preferred_element_type=jnp.float32
         )
-        o_ref[rows, :] = (weighted_sum / row_total).astype(o_ref.dtype)
+        obuf[rows, :] = (weighted_sum / row_total).astype(obuf.dtype)
+        out_copy = pltpu.make_async_copy(
+            obuf.at[rows, :],
+            o_ref.at[pl.ds(pl.multiple_of(step * query_rows + g * BLOCK, BLOCK), BLOCK), :],
+            sems.at[3 + g],
+        )
+        out_copy.start()
+        out_copies.append(out_copy)
+    for out_copy in out_copies:
+        out_copy.wait()
 
 
 def attend(own, other, lists, counts, narrow, head_size):
@@ -119,13 +130,14 @@
             pl.BlockSpec(memory_space=pl.ANY),
             pl.BlockSpec(memory_space=pl.ANY),
         ],
-        out_specs=pl.BlockSpec((group * BLOCK, head_size), lambda b, *_: (b, 0)),
+        out_specs=pl.BlockSpec(memory_space=pl.ANY),
         scratch_shapes=[
             pltpu.VMEM((2 * other.shape[0] + BLOCK, 2 * head_size), own.dtype),
             pltpu.VMEM((group * BLOCK, head_size), own.dtype),
+            pltpu.VMEM((group * BLOCK, head_size), jnp.bfloat16),
             pltpu.VMEM((group, slots * BLOCK, head_size), own.dtype),
             pltpu.VMEM((group, slots * BLOCK, head_size), own.dtype),
-            pltpu.SemaphoreType.DMA((3,)),
+            pltpu.SemaphoreType.DMA((3 + group,)),
         ],
     )
     return pl.pallas_call(

time: 80.6 us -> 80.6 us (level)
  no operation moved by 1% of the time
where the time goes in v16:
time: 80.6 us; the launch traced here: 80.2 us
  blocking collectives  62.6 us (78%)
  Pallas kernels  11.9 us (15%)
  waiting for transfers between devices  2.77 us (3%)
  other arithmetic  1.46 us (2%)
  local copies, waits for them, and re-layouts  1.46 us (2%)
    all_to_all x1, blocking collectives, per_device(): lax.all_to_all(stacked, 'wide', split_axis=1, concat_axis=0, tiled=True)  44.1 us
    all_to_all x1, blocking collectives, per_device(): lax.all_to_all(attended, 'wide', split_axis=0, concat_axis=1, tiled=True)  18.5 us
    pallas_call x1, Pallas kernels, attend(): pl.pallas_call(kernel, grid_spec=grid_spec, out_shape=jax.ShapeDtypeStruc...  11.9 us
    ppermute x1, waiting for transfers between devices, per_device(): other = lax.ppermute(own[:, head_size:], 'narrow', [(0, 1), (1, 0)])  2.77 us
  transfers between devices with their start and end apart: 1, of which 1 were waited for; matrix products, arithmetic and copies ran while one was open for 0% of the time, Pallas kernels for 0%

profile of v16, /device:TPU:0, one launch (start us, length us, event | category | flops | bytes accessed | tf_op | source)
XLA Modules:
  0.0 80.2 jit_solution(10913752528356489702)
XLA Ops:
  0.0 1.5 %maximum_bitcast_fusion = bf16[32,8,24,128]{3,1,2,0:T(8,128)(2,1)S(1)} fusion(bf16[256,1024]{1,0:T(8,128)(2,1)} %param.7, bf16[256,1024]{1,0:T(8,128)(2,1)} %param.6, bf16[256,1024]{1,0:T(8,128)(2,1)} %param.5), kind=kLoop, calls=%fused_computation | loop fusion | flops 4718592 | bytes 3145728
  1.5 0.3 copy.13
  1.8 0.2 copy.10
  2.0 44.1 %all_to_all.34 = bf16[256,8,384]{2,0,1:T(8,128)(2,1)S(1)} all-to-all(bf16[256,8,384]{2,0,1:T(8,128)(2,1)S(1)} %copy.10), channel_id=1, replica_groups=mesh['groups'=2,'wide'=8,'narrow'=2] {'wide'}, dimensions={1} | all-to-all | bytes 3145728 | tf_op jit(solution)/shard_map/all_to_all | solution.py:161
  46.1 0.0 copy-start
  46.1 0.1 slice.4
  46.2 0.1 collective-permute-start
  46.2 2.8 %collective-permute-done.other_ref = bf16[2048,256]{1,0:T(8,128)(2,1)} collective-permute-done((bf16[2048,256]{1,0:T(8,128)(2,1)S(1)}, bf16[2048,256]{1,0:T(8,128)(2,1)}, u32[]{:S(2)}, u32[]{:S(2)}) %collective-permute-start) | collective-permute-done | bytes 1048608 | tf_op jit(solution)/shard_map/ppermute | solution.py:163
  49.0 0.0 copy-done
  49.0 11.9 %shard_map.55 = bf16[2048,128]{1,0:T(8,128)(2,1)} custom-call(s32[16,16]{1,0:T(8,128)} %bitcast.28, s32[16]{0:T(128)} %bitcast.29, s32[1]{0:T(128)} %bitcast.2.narrow_ref, bf16[2048,384]{1,0:T(8,128)(2,1)} %bitcast.24, bf16[2048,384]{1,0:T(8,128)(2,1)} %bitcast.25, bf16[2048,256]{1,0:T(8,128)(2,1)} %collective-permute-done.other_ref), custom_call_target="tpu_custom_call" | custom-call | tf_op jit(solution)/shard_map/pallas_call | solution.py:143
  60.9 18.5 %all_to_all.35 = bf16[8,256,128]{2,1,0:T(8,128)(2,1)S(1)} all-to-all(bf16[8,256,128]{2,1,0:T(8,128)(2,1)} %bitcast.27), channel_id=1, replica_groups=mesh['groups'=2,'wide'=8,'narrow'=2] {'wide'}, dimensions={0} | all-to-all | bytes 1048576 | tf_op jit(solution)/shard_map/all_to_all | solution.py:166
  79.4 0.9 %copy_bitcast_fusion = bf16[256,1024]{1,0:T(8,128)(2,1)} fusion(bf16[8,256,128]{2,1,0:T(8,128)(2,1)S(1)} %all_to_all.35), kind=kLoop, calls=%fused_computation.1 | loop fusion | bytes 1048576 | tf_op jit(solution)/shard_map/all_to_all | solution.py:166
Async XLA Ops:
  46.1 2.9 %copy-start = (bf16[256,8,384]{2,0,1:T(8,128)(2,1)}, bf16[256,8,384]{2,0,1:T(8,128)(2,1)S(1)}, u32[]{:S(2)}) copy-start(bf16[256,8,384]{2,0,1:T(8,128)(2,1)S(1)} %all_to_all.34) | copy-start | bytes 4718596
  46.2 2.9 %collective-permute-start = (bf16[2048,256]{1,0:T(8,128)(2,1)S(1)}, bf16[2048,256]{1,0:T(8,128)(2,1)}, u32[]{:S(2)}, u32[]{:S(2)}) collective-permute-start(bf16[2048,256]{1,0:T(8,128)(2,1)S(1)} %slice.4), channel_id=1, source_target_pairs={{0,1},{1,0},{2,3},{3,2},{4,5},{5,4},{6,7},{7,6},{8,9},{9,8},{10,11... | collective-permute-start | bytes 3145736 | tf_op jit(solution)/shard_map/ppermute | solution.py:163

commit v17 on v15

--- a/solution.py
+++ b/solution.py
@@ -94,9 +94,10 @@
         raw_max = jnp.max(raw_scores, axis=1, keepdims=True)
         weights = jnp.exp2((raw_scores - raw_max) * exponent_scale)
         padded = (slots - count).astype(jnp.float32)
-        row_total = jnp.sum(weights, axis=1, keepdims=True) - padded * jnp.sum(
-            weights[:, :BLOCK], axis=1, keepdims=True
-        )
+        slot_sums = weights[:, :BLOCK]
+        for j in range(1, slots):
+            slot_sums = slot_sums + weights[:, j * BLOCK : (j + 1) * BLOCK]
+        row_total = jnp.sum(slot_sums - padded * weights[:, :BLOCK], axis=1, keepdims=True)
         weighted_sum = jnp.dot(
             weights.astype(jnp.bfloat16), vbuf[g], preferred_element_type=jnp.float32
         )

time: 80.6 us -> 80.6 us (level)
  no operation moved by 1% of the time
where the time goes in v17:
time: 80.6 us; the launch traced here: 80.3 us
  blocking collectives  62.6 us (78%)
  Pallas kernels  11.9 us (15%)
  waiting for transfers between devices  2.77 us (3%)
  other arithmetic  1.46 us (2%)
  local copies, waits for them, and re-layouts  1.46 us (2%)
    all_to_all x1, blocking collectives, per_device(): lax.all_to_all(stacked, 'wide', split_axis=1, concat_axis=0, tiled=True)  44.1 us
    all_to_all x1, blocking collectives, per_device(): lax.all_to_all(attended, 'wide', split_axis=0, concat_axis=1, tiled=True)  18.5 us
    pallas_call x1, Pallas kernels, attend(): pl.pallas_call(kernel, grid_spec=grid_spec, out_shape=jax.ShapeDtypeStruc...  11.9 us
    ppermute x1, waiting for transfers between devices, per_device(): other = lax.ppermute(own[:, head_size:], 'narrow', [(0, 1), (1, 0)])  2.77 us
  transfers between devices with their start and end apart: 1, of which 1 were waited for; matrix products, arithmetic and copies ran while one was open for 0% of the time, Pallas kernels for 0%

profile of v17, /device:TPU:0, one launch (start us, length us, event | category | flops | bytes accessed | tf_op | source)
XLA Modules:
  0.0 80.3 jit_solution(14458124113578724060)
XLA Ops:
  0.0 1.5 %maximum_bitcast_fusion = bf16[32,8,24,128]{3,1,2,0:T(8,128)(2,1)S(1)} fusion(bf16[256,1024]{1,0:T(8,128)(2,1)} %param.7, bf16[256,1024]{1,0:T(8,128)(2,1)} %param.6, bf16[256,1024]{1,0:T(8,128)(2,1)} %param.5), kind=kLoop, calls=%fused_computation | loop fusion | flops 4718592 | bytes 3145728
  1.5 0.3 copy.13
  1.8 0.2 copy.10
  2.0 44.1 %all_to_all.34 = bf16[256,8,384]{2,0,1:T(8,128)(2,1)S(1)} all-to-all(bf16[256,8,384]{2,0,1:T(8,128)(2,1)S(1)} %copy.10), channel_id=1, replica_groups=mesh['groups'=2,'wide'=8,'narrow'=2] {'wide'}, dimensions={1} | all-to-all | bytes 3145728 | tf_op jit(solution)/shard_map/all_to_all | solution.py:150
  46.1 0.0 copy-start
  46.1 0.1 slice.4
  46.2 0.1 collective-permute-start
  46.2 2.8 %collective-permute-done.other_ref = bf16[2048,256]{1,0:T(8,128)(2,1)} collective-permute-done((bf16[2048,256]{1,0:T(8,128)(2,1)S(1)}, bf16[2048,256]{1,0:T(8,128)(2,1)}, u32[]{:S(2)}, u32[]{:S(2)}) %collective-permute-start) | collective-permute-done | bytes 1048608 | tf_op jit(solution)/shard_map/ppermute | solution.py:152
  49.0 0.0 copy-done
  49.0 11.9 %shard_map.55 = bf16[2048,128]{1,0:T(8,128)(2,1)} custom-call(s32[16,16]{1,0:T(8,128)} %bitcast.28, s32[16]{0:T(128)} %bitcast.29, s32[1]{0:T(128)} %bitcast.2.narrow_ref, bf16[2048,384]{1,0:T(8,128)(2,1)} %bitcast.24, bf16[2048,384]{1,0:T(8,128)(2,1)} %bitcast.25, bf16[2048,256]{1,0:T(8,128)(2,1)} %collective-permute-done.other_ref), custom_call_target="tpu_custom_call" | custom-call | tf_op jit(solution)/shard_map/pallas_call | solution.py:132
  60.9 18.5 %all_to_all.35 = bf16[8,256,128]{2,1,0:T(8,128)(2,1)S(1)} all-to-all(bf16[8,256,128]{2,1,0:T(8,128)(2,1)} %bitcast.27), channel_id=1, replica_groups=mesh['groups'=2,'wide'=8,'narrow'=2] {'wide'}, dimensions={0} | all-to-all | bytes 1048576 | tf_op jit(solution)/shard_map/all_to_all | solution.py:155
  79.4 0.9 %copy_bitcast_fusion = bf16[256,1024]{1,0:T(8,128)(2,1)} fusion(bf16[8,256,128]{2,1,0:T(8,128)(2,1)S(1)} %all_to_all.35), kind=kLoop, calls=%fused_computation.1 | loop fusion | bytes 1048576 | tf_op jit(solution)/shard_map/all_to_all | solution.py:155
Async XLA Ops:
  46.1 2.9 %copy-start = (bf16[256,8,384]{2,0,1:T(8,128)(2,1)}, bf16[256,8,384]{2,0,1:T(8,128)(2,1)S(1)}, u32[]{:S(2)}) copy-start(bf16[256,8,384]{2,0,1:T(8,128)(2,1)S(1)} %all_to_all.34) | copy-start | bytes 4718596
  46.2 2.9 %collective-permute-start = (bf16[2048,256]{1,0:T(8,128)(2,1)S(1)}, bf16[2048,256]{1,0:T(8,128)(2,1)}, u32[]{:S(2)}, u32[]{:S(2)}) collective-permute-start(bf16[2048,256]{1,0:T(8,128)(2,1)S(1)} %slice.4), channel_id=1, source_target_pairs={{0,1},{1,0},{2,3},{3,2},{4,5},{5,4},{6,7},{7,6},{8,9},{9,8},{10,11... | collective-permute-start | bytes 3145736 | tf_op jit(solution)/shard_map/ppermute | solution.py:152
